TPU v7x, 512 devices: a whole 4x4x16 slice. The times are simulated.
512 devices in a mesh: grp: 16 (over z), ep: 32 (over x, y, core).
Axes of the slice: x: 4, y: 4, z: 16, core: 2. Of those that a mesh axis runs over, the one named last changes fastest.
Arguments:
- q_nope: bfloat16 [3072, 2048], P(('grp', 'ep')), may hold values from -15 to 15
- q_rope: bfloat16 [3072, 1024], P(('grp', 'ep')), may hold values from -8 to 8
- tree_latent: bfloat16 [3072, 576], P(('grp', 'ep')), may hold values from -12 to 12
- cache_pool: bfloat16 [4096, 64, 576], P(('grp', 'ep')), may hold values from -7 to 7
- page_table: int32 [4096], P(('grp', 'ep')), may hold values from 0 to 7, as said below
- cache_len: int32 [64], P('grp'), may hold values from 512 to 4096
- parents: int32 [64, 48], P('grp'), may hold values from 0 to 46, as said below
- w_key: bfloat16 [16, 512, 128], replicated, may hold values from -0.5 to 0.5
- w_value: bfloat16 [16, 512, 128], P('grp'), may hold values from -0.25 to 0.25
- out_weight: bfloat16 [2048, 2048], P('grp'), may hold values from -0.125 to 0.125
Outputs:
- attn_out: bfloat16 [3072, 2048], P(('grp', 'ep'))
Inputs may be any that keep to these rules, and one draw needn't show every extreme that they name: `page_table`: each device's block of 8 entries is an arrangement of 0 to 7; entry k of the block names the page of that device's own block of the pool that holds the device's k-th page of positions. parents[r, 0] = 0, and for i >= 1, max(0, i - 4) <= parents[r, i] <= i - 1.
All inputs are finite; a program needn't handle non-finite values.
Results may differ from a plain program's by a relative error of at most 0.039.
Values may be sent and summed in bfloat16 or wider, within the bound.
No kernel may reach another device: no remote copies, remote signals or barrier semaphores. Data moves between devices by JAX's collectives and lax.ppermute only.
A program may use at most 64 MiB of HBM per device.

v0:
```python
import math

import jax
import jax.numpy as jnp
from jax import lax
from jax.sharding import PartitionSpec as P

TREE = 48
REQ_GRP = 4


def from_partner(block, axis, bit):
    count = lax.axis_size(axis)
    route = []
    for low in range(count):
        high = low | 1 << bit
        if high != low and high < count:
            route += [(low, high), (high, low)]
    return lax.ppermute(block, axis, route)


def for_sending(value):
    return jax.tree.map(lambda a: a.astype(jnp.bfloat16) if a.dtype == jnp.float32 else a, value)


def ancestors(parent_row):
    count = parent_row.shape[0]
    order = jnp.arange(count, dtype=jnp.int32)
    links = ((order[None, :] == parent_row[:, None]) & (order[:, None] > 0)).astype(jnp.float32)
    reach = jnp.eye(count, dtype=jnp.float32) + links
    for repeat in range(int(count).bit_length()):
        reach = jnp.minimum(jnp.dot(reach, reach, precision=lax.Precision.HIGHEST), 1.0)
    return reach > 0.5


def absorb(nope_rows, w_key):
    return jnp.einsum("thn,hrn->thr", nope_rows, w_key, preferred_element_type=jnp.float32).astype(
        jnp.bfloat16
    )


def append_partner(mine, partner, position, bit_level):
    upper_side = jnp.right_shift(position, bit_level) & 1 == 1
    former = jnp.where(upper_side, partner, mine)
    latter = jnp.where(upper_side, mine, partner)
    return jnp.concatenate([former, latter], axis=0)


def combine_parts(kept_part, received):
    kept_sum, kept_high, kept_total = kept_part
    got_sum, got_high, got_total = received
    joint_high = jnp.maximum(kept_high, got_high)
    factor_kept = jnp.exp(kept_high - joint_high)
    factor_got = jnp.exp(got_high - joint_high)
    merged_sum = kept_sum * factor_kept[..., None] + got_sum * factor_got[..., None]
    merged_total = kept_total * factor_kept + got_total * factor_got
    return (merged_sum, joint_high, merged_total)


def per_device(
    q_nope,
    q_rope,
    tree_latent,
    cache_pool,
    page_table,
    cache_len,
    parents,
    w_key,
    w_value,
    out_weight,
):
    head_count = w_key.shape[0]
    latent_width = w_key.shape[1]
    nope_width = w_key.shape[2]
    token_count = q_nope.shape[0]
    rope_width = q_rope.shape[1] // head_count
    per_request = lax.axis_size("ep") // REQ_GRP
    doublings = per_request.bit_length() - 1
    position = lax.axis_index("ep")
    local_rank = position % per_request
    local_request = position // per_request
    score_scale = 1.0 / math.sqrt(nope_width + rope_width)
    nope_rows = q_nope.reshape(token_count, head_count, nope_width)
    rope_rows = q_rope.reshape(token_count, head_count, rope_width)
    queries = jnp.concatenate([absorb(nope_rows, w_key), rope_rows], axis=2)
    for bit_level in range(doublings):
        partner = from_partner(queries, "ep", bit_level)
        queries = append_partner(queries, partner, position, bit_level)
    pages_read = jnp.take(cache_pool, page_table, axis=0)
    cached = pages_read.reshape(-1, pages_read.shape[2])
    pos_count = cached.shape[0]
    all_keys = jnp.concatenate([cached, tree_latent], axis=0)
    my_length = lax.dynamic_index_in_dim(cache_len, local_request, 0, keepdims=False)
    cache_ok = local_rank * pos_count + jnp.arange(pos_count, dtype=jnp.int32) < my_length
    parent_row = lax.dynamic_index_in_dim(parents, local_request, 0, keepdims=False)
    family = ancestors(parent_row)
    tree_ok = lax.dynamic_slice_in_dim(family, local_rank * token_count, token_count, 1)
    allowed = jnp.concatenate(
        [jnp.broadcast_to(cache_ok[None, :], (TREE, pos_count)), tree_ok], axis=1
    )
    scores = (
        jnp.einsum("ihl,kl->ihk", queries, all_keys, preferred_element_type=jnp.float32)
        * score_scale
    )
    masked = jnp.where(allowed[:, None, :], scores, -1e30)
    highest = jnp.max(masked, axis=2)
    powers = jnp.where(allowed[:, None, :], jnp.exp(masked - highest[..., None]), 0.0)
    total = jnp.sum(powers, axis=2)
    partial_value = jnp.einsum(
        "ihk,kr->ihr",
        powers.astype(jnp.bfloat16),
        all_keys[:, :latent_width],
        preferred_element_type=jnp.float32,
    )
    state = (partial_value, highest, total)
    for bit_level in reversed(range(doublings)):
        half_rows = state[0].shape[0] // 2
        upper_side = jnp.right_shift(position, bit_level) & 1 == 1
        lower_part = tuple((member[:half_rows] for member in state))
        upper_part = tuple((member[half_rows:] for member in state))
        kept_part = tuple(
            (jnp.where(upper_side, upper, lower) for lower, upper in zip(lower_part, upper_part))
        )
        sent_part = tuple(
            (jnp.where(upper_side, lower, upper) for lower, upper in zip(lower_part, upper_part))
        )
        received = from_partner(
            (for_sending(sent_part[0]), for_sending(sent_part[1]), for_sending(sent_part[2])),
            "ep",
            bit_level,
        )
        state = combine_parts(kept_part, received)
    merged_sum, merged_high, merged_total = state
    merged = merged_sum / merged_total[..., None]
    spread = lax.all_to_all(
        for_sending(merged), "grp", split_axis=1, concat_axis=0, tiled=True
    ).astype(merged.dtype)
    head_rows = jnp.einsum(
        "thr,hrn->thn", spread, w_value.astype(jnp.float32), precision=lax.Precision.HIGHEST
    ).astype(jnp.bfloat16)
    head_rows = head_rows.reshape(head_rows.shape[0], -1)
    return lax.psum_scatter(
        jnp.dot(head_rows, out_weight, preferred_element_type=jnp.float32).astype(jnp.bfloat16),
        "grp",
        scatter_dimension=0,
        tiled=True,
    )


def solution(mesh):
    return jax.shard_map(
        per_device,
        mesh=mesh,
        in_specs=(
            P(("grp", "ep"), None),
            P(("grp", "ep"), None),
            P(("grp", "ep"), None),
            P(("grp", "ep"), None, None),
            P(("grp", "ep")),
            P("grp"),
            P("grp", None),
            P(),
            P("grp", None, None),
            P("grp", None),
        ),
        out_specs=P(("grp", "ep"), None),
        check_vma=False,
    )
```

profile of v0, /device:TPU:6, one launch (start us, length us, event | category | flops | bytes accessed | tf_op | source)
XLA Modules:
  0.0 161.3 jit_solution(9365920657968930823)
XLA Ops:
  3.1 1.9 %collective-permute-start = (bf16[6,16,576]{2,0,1:T(8,128)(2,1)S(1)}, bf16[6,16,576]{2,0,1:T(8,128)(2,1)S(1)}, u32[]{:S(2)}, u32[]{:S(2)}) collective-permute-start(bf16[6,16,576]{2,0,1:T(8,128)(2,1)S(1)} %pad_maximum_fusion.4), channel_id=1, source_target_pairs={{0,1},{1,0},{2,3},{3,2},{4,5},{5,4},{6,7},{7,6},{8,9},{9,8},{10,11... | collective-permute-start | bytes 331784 | tf_op jit(solution)/shard_map/ppermute | solution.py:19
  8.5 3.5 %collective-permute-start.1 = (bf16[12,16,576]{2,0,1:T(8,128)(2,1)S(1)}, bf16[12,16,576]{2,0,1:T(8,128)(2,1)}, u32[]{:S(2)}, u32[]{:S(2)}) collective-permute-start(bf16[12,16,576]{2,0,1:T(8,128)(2,1)S(1)} %pad_maximum_fusion.3), channel_id=1, source_target_pairs={{0,2},{2,0},{1,3},{3,1},{4,6},{6,4},{5,7},{7,5},{8,10},{10,8},{9,1... | collective-permute-start | bytes 663560 | tf_op jit(solution)/shard_map/ppermute | solution.py:19
  12.0 1.8 %gather_fusion = bf16[8,64,576]{2,1,0:T(8,128)(2,1)S(1)} fusion(bf16[8,64,576]{2,1,0:T(8,128)(2,1)} %param.13, s32[1024]{0:T(1024)S(1)} %pad_clamp_fusion), kind=kCustom, calls=%fused_computation | custom fusion | bytes 1179680 | tf_op jit(solution)/shard_map/jit(_take)/gather | solution.py:89
  13.8 6.8 %collective-permute-done.1 = bf16[12,16,576]{2,0,1:T(8,128)(2,1)} collective-permute-done((bf16[12,16,576]{2,0,1:T(8,128)(2,1)S(1)}, bf16[12,16,576]{2,0,1:T(8,128)(2,1)}, u32[]{:S(2)}, u32[]{:S(2)}) %collective-permute-start.1) | collective-permute-done | bytes 221216 | tf_op jit(solution)/shard_map/ppermute | solution.py:19
  21.9 5.1 %collective-permute-start.2 = (bf16[24,16,576]{2,0,1:T(8,128)(2,1)S(1)}, bf16[24,16,576]{2,0,1:T(8,128)(2,1)S(1)}, u32[]{:S(2)}, u32[]{:S(2)}) collective-permute-start(bf16[24,16,576]{2,0,1:T(8,128)(2,1)S(1)} %pad_maximum_fusion.2), channel_id=1, source_target_pairs={{0,4},{4,0},{1,5},{5,1},{2,6},{6,2},{3,7},{7,3},{8,12},{12,8},{9,1... | collective-permute-start | bytes 1327112 | tf_op jit(solution)/shard_map/ppermute | solution.py:19
  27.2 10.9 %collective-permute-done.2 = bf16[24,16,576]{2,0,1:T(8,128)(2,1)S(1)} collective-permute-done((bf16[24,16,576]{2,0,1:T(8,128)(2,1)S(1)}, bf16[24,16,576]{2,0,1:T(8,128)(2,1)S(1)}, u32[]{:S(2)}, u32[]{:S(2)}) %collective-permute-start.2) | collective-permute-done | bytes 442400 | tf_op jit(solution)/shard_map/ppermute | solution.py:19
  39.6 5.1 %collective-permute-start.3 = (bf16[24,16]{1,0:T(8,128)(2,1)S(1)}, bf16[24,16]{1,0:T(8,128)(2,1)S(1)}, u32[]{:S(2)}, u32[]{:S(2)}) collective-permute-start(bf16[24,16]{1,0:T(8,128)(2,1)S(1)} %select_convert_fusion.4), channel_id=1, source_target_pairs={{0,4},{4,0},{1,5},{5,1},{2,6},{6,2},{3,7},{7,3},{8,12},{12,8},{9,1... | collective-permute-start | bytes 2312 | tf_op jit(solution)/shard_map/ppermute | solution.py:19
  45.6 2.2 %collective-permute-start.9 = (bf16[24,16]{1,0:T(8,128)(2,1)S(1)}, bf16[24,16]{1,0:T(8,128)(2,1)S(1)}, u32[]{:S(2)}, u32[]{:S(2)}) collective-permute-start(bf16[24,16]{1,0:T(8,128)(2,1)S(1)} %select_convert_fusion.3), channel_id=1, source_target_pairs={{0,4},{4,0},{1,5},{5,1},{2,6},{6,2},{3,7},{7,3},{8,12},{12,8},{9,1... | collective-permute-start | bytes 2312 | tf_op jit(solution)/shard_map/ppermute | solution.py:19
  48.8 3.9 %collective-permute-done.9 = bf16[24,16]{1,0:T(8,128)(2,1)S(1)} collective-permute-done((bf16[24,16]{1,0:T(8,128)(2,1)S(1)}, bf16[24,16]{1,0:T(8,128)(2,1)S(1)}, u32[]{:S(2)}, u32[]{:S(2)}) %collective-permute-start.9) | collective-permute-done | bytes 800 | tf_op jit(solution)/shard_map/ppermute | solution.py:19
  52.7 2.6 %collective-permute-start.5 = (bf16[12,16]{1,0:T(8,128)(2,1)S(1)}, bf16[12,16]{1,0:T(8,128)(2,1)S(1)}, u32[]{:S(2)}, u32[]{:S(2)}) collective-permute-start(bf16[12,16]{1,0:T(8,128)(2,1)S(1)} %select_convert_fusion.6), channel_id=1, source_target_pairs={{0,2},{2,0},{1,3},{3,1},{4,6},{6,4},{5,7},{7,5},{8,10},{10,8},{9,1... | collective-permute-start | bytes 1160 | tf_op jit(solution)/shard_map/ppermute | solution.py:19
  55.3 3.3 %collective-permute-start.10 = (bf16[12,16]{1,0:T(8,128)(2,1)S(1)}, bf16[12,16]{1,0:T(8,128)(2,1)S(1)}, u32[]{:S(2)}, u32[]{:S(2)}) collective-permute-start(bf16[12,16]{1,0:T(8,128)(2,1)S(1)} %select_convert_fusion.5), channel_id=1, source_target_pairs={{0,2},{2,0},{1,3},{3,1},{4,6},{6,4},{5,7},{7,5},{8,10},{10,8},{9,1... | collective-permute-start | bytes 1160 | tf_op jit(solution)/shard_map/ppermute | solution.py:19
  58.6 2.4 %collective-permute-start.4 = (bf16[24,16,512]{2,1,0:T(8,128)(2,1)S(1)}, bf16[24,16,512]{2,1,0:T(8,128)(2,1)S(1)}, u32[]{:S(2)}, u32[]{:S(2)}) collective-permute-start(bf16[24,16,512]{2,1,0:T(8,128)(2,1)S(1)} %select_convert_fusion), channel_id=1, source_target_pairs={{0,4},{4,0},{1,5},{5,1},{2,6},{6,2},{3,7},{7,3},{8,12},{12,8},{9,1... | collective-permute-start | bytes 1179656 | tf_op jit(solution)/shard_map/ppermute | solution.py:19
  61.1 1.9 %collective-permute-start.7 = (bf16[6,16]{1,0:T(8,128)(2,1)S(1)}, bf16[6,16]{1,0:T(8,128)(2,1)S(1)}, u32[]{:S(2)}, u32[]{:S(2)}) collective-permute-start(bf16[6,16]{1,0:T(8,128)(2,1)S(1)} %select_convert_fusion.8), channel_id=1, source_target_pairs={{0,1},{1,0},{2,3},{3,2},{4,5},{5,4},{6,7},{7,6},{8,9},{9,8},{10,11... | collective-permute-start | bytes 584 | tf_op jit(solution)/shard_map/ppermute | solution.py:19
  63.0 6.8 %collective-permute-done.4 = bf16[24,16,512]{2,1,0:T(8,128)(2,1)S(1)} collective-permute-done((bf16[24,16,512]{2,1,0:T(8,128)(2,1)S(1)}, bf16[24,16,512]{2,1,0:T(8,128)(2,1)S(1)}, u32[]{:S(2)}, u32[]{:S(2)}) %collective-permute-start.4) | collective-permute-done | bytes 393248 | tf_op jit(solution)/shard_map/ppermute | solution.py:19
  70.1 2.7 %collective-permute-start.6 = (bf16[12,16,512]{2,1,0:T(8,128)(2,1)S(1)}, bf16[12,16,512]{2,1,0:T(8,128)(2,1)S(1)}, u32[]{:S(2)}, u32[]{:S(2)}) collective-permute-start(bf16[12,16,512]{2,1,0:T(8,128)(2,1)S(1)} %select_convert_fusion.1), channel_id=1, source_target_pairs={{0,2},{2,0},{1,3},{3,1},{4,6},{6,4},{5,7},{7,5},{8,10},{10,8},{9,1... | collective-permute-start | bytes 589832 | tf_op jit(solution)/shard_map/ppermute | solution.py:19
  72.9 1.9 %collective-permute-start.11 = (bf16[6,16]{1,0:T(8,128)(2,1)S(1)}, bf16[6,16]{1,0:T(8,128)(2,1)S(1)}, u32[]{:S(2)}, u32[]{:S(2)}) collective-permute-start(bf16[6,16]{1,0:T(8,128)(2,1)S(1)} %select_convert_fusion.7), channel_id=1, source_target_pairs={{0,1},{1,0},{2,3},{3,2},{4,5},{5,4},{6,7},{7,6},{8,9},{9,8},{10,11... | collective-permute-start | bytes 584 | tf_op jit(solution)/shard_map/ppermute | solution.py:19
  74.8 3.0 %collective-permute-done.6 = bf16[12,16,512]{2,1,0:T(8,128)(2,1)S(1)} collective-permute-done((bf16[12,16,512]{2,1,0:T(8,128)(2,1)S(1)}, bf16[12,16,512]{2,1,0:T(8,128)(2,1)S(1)}, u32[]{:S(2)}, u32[]{:S(2)}) %collective-permute-start.6) | collective-permute-done | bytes 196640 | tf_op jit(solution)/shard_map/ppermute | solution.py:19
  78.0 1.9 %collective-permute-start.8 = (bf16[6,16,512]{2,1,0:T(8,128)(2,1)S(1)}, bf16[6,16,512]{2,1,0:T(8,128)(2,1)S(1)}, u32[]{:S(2)}, u32[]{:S(2)}) collective-permute-start(bf16[6,16,512]{2,1,0:T(8,128)(2,1)S(1)} %select_convert_fusion.2), channel_id=1, source_target_pairs={{0,1},{1,0},{2,3},{3,2},{4,5},{5,4},{6,7},{7,6},{8,9},{9,8},{10,11... | collective-permute-start | bytes 294920 | tf_op jit(solution)/shard_map/ppermute | solution.py:19
  81.4 29.7 %all_to_all.15 = bf16[6,16,512]{2,0,1:T(8,128)(2,1)S(1)} all-to-all(bf16[6,16,512]{2,0,1:T(8,128)(2,1)S(1)} %copy.23), channel_id=1, replica_groups=mesh['grp'=16,'ep'=32] {'grp'}, dimensions={1} | all-to-all | bytes 196608 | tf_op jit(solution)/shard_map/all_to_all | solution.py:135
  111.6 33.7 %fusion = bf16[8,2048]{1,0:T(8,128)(2,1)S(1)} fusion(bf16[96,2048]{1,0:T(8,128)(2,1)S(1)} %convolution_convert_fusion), kind=kCustom, calls=%all-reduce-scatter | all-reduce-scatter fusion | flops 262145 | bytes 428032
  145.3 2.6 %collective-permute-start.14 = (bf16[8,2048]{1,0:T(8,128)(2,1)S(1)}, bf16[8,2048]{1,0:T(8,128)(2,1)S(1)}, u32[]{:S(2)}, u32[]{:S(2)}) collective-permute-start(bf16[8,2048]{1,0:T(8,128)(2,1)S(1)} %fusion), channel_id=1, source_target_pairs={{0,96},{32,128},{64,160},{96,192},{128,224},{160,256},{192,288},{2... | collective-permute-start | bytes 98312
  148.0 4.0 %collective-permute-start.13 = (bf16[8,2048]{1,0:T(8,128)(2,1)S(1)}, bf16[8,2048]{1,0:T(8,128)(2,1)S(1)}, u32[]{:S(2)}, u32[]{:S(2)}) collective-permute-start(bf16[8,2048]{1,0:T(8,128)(2,1)S(1)} %fusion), channel_id=1, source_target_pairs={{0,64},{32,96},{64,128},{96,160},{128,192},{160,224},{192,256},{22... | collective-permute-start | bytes 98312
  151.9 3.1 %collective-permute-start.12 = (bf16[8,2048]{1,0:T(8,128)(2,1)S(1)}, bf16[8,2048]{1,0:T(8,128)(2,1)S(1)}, u32[]{:S(2)}, u32[]{:S(2)}) collective-permute-start(bf16[8,2048]{1,0:T(8,128)(2,1)S(1)} %fusion), channel_id=1, source_target_pairs={{0,32},{32,64},{64,96},{96,128},{128,160},{160,192},{192,224},{224... | collective-permute-start | bytes 98312
  155.1 3.1 %collective-permute-start.15 = (bf16[6,2048]{1,0:T(8,128)(2,1)S(1)}, bf16[6,2048]{1,0:T(8,128)(2,1)S(1)}, u32[]{:S(2)}, u32[]{:S(2)}) collective-permute-start(bf16[6,2048]{1,0:T(8,128)(2,1)S(1)} %slice.98), channel_id=1, source_target_pairs={{0,128},{32,160},{64,192},{96,224},{128,256},{160,288},{192,320},{... | collective-permute-start | bytes 73736
  (78 shorter events, 16.2 us)
Async XLA Ops:
  0.0 1.6 copy-start
  0.0 5.0 %copy-start.4 = (s32[8]{0:T(128)S(1)}, s32[8]{0:T(128)}, u32[]{:S(2)}) copy-start(s32[8]{0:T(128)} %param.14) | copy-start | bytes 100
  0.0 5.1 %copy-start.5 = (s32[4]{0:T(128)S(1)}, s32[4]{0:T(128)}, u32[]{:S(2)}) copy-start(s32[4]{0:T(128)} %param.15) | copy-start | bytes 52
  3.1 5.2 %collective-permute-start = (bf16[6,16,576]{2,0,1:T(8,128)(2,1)S(1)}, bf16[6,16,576]{2,0,1:T(8,128)(2,1)S(1)}, u32[]{:S(2)}, u32[]{:S(2)}) collective-permute-start(bf16[6,16,576]{2,0,1:T(8,128)(2,1)S(1)} %pad_maximum_fusion.4), channel_id=1, source_target_pairs={{0,1},{1,0},{2,3},{3,2},{4,5},{5,4},{6,7},{7,6},{8,9},{9,8},{10,11... | collective-permute-start | bytes 331784 | tf_op jit(solution)/shard_map/ppermute | solution.py:19
  8.5 12.1 %collective-permute-start.1 = (bf16[12,16,576]{2,0,1:T(8,128)(2,1)S(1)}, bf16[12,16,576]{2,0,1:T(8,128)(2,1)}, u32[]{:S(2)}, u32[]{:S(2)}) collective-permute-start(bf16[12,16,576]{2,0,1:T(8,128)(2,1)S(1)} %pad_maximum_fusion.3), channel_id=1, source_target_pairs={{0,2},{2,0},{1,3},{3,1},{4,6},{6,4},{5,7},{7,5},{8,10},{10,8},{9,1... | collective-permute-start | bytes 663560 | tf_op jit(solution)/shard_map/ppermute | solution.py:19
  21.9 16.2 %collective-permute-start.2 = (bf16[24,16,576]{2,0,1:T(8,128)(2,1)S(1)}, bf16[24,16,576]{2,0,1:T(8,128)(2,1)S(1)}, u32[]{:S(2)}, u32[]{:S(2)}) collective-permute-start(bf16[24,16,576]{2,0,1:T(8,128)(2,1)S(1)} %pad_maximum_fusion.2), channel_id=1, source_target_pairs={{0,4},{4,0},{1,5},{5,1},{2,6},{6,2},{3,7},{7,3},{8,12},{12,8},{9,1... | collective-permute-start | bytes 1327112 | tf_op jit(solution)/shard_map/ppermute | solution.py:19
  27.2 11.3 %copy-start.3 = (bf16[6,576]{1,0:T(8,128)(2,1)S(1)}, bf16[6,576]{1,0:T(8,128)(2,1)}, u32[]{:S(2)}) copy-start(bf16[6,576]{1,0:T(8,128)(2,1)} %param.12) | copy-start | bytes 20740
  39.6 9.1 %collective-permute-start.3 = (bf16[24,16]{1,0:T(8,128)(2,1)S(1)}, bf16[24,16]{1,0:T(8,128)(2,1)S(1)}, u32[]{:S(2)}, u32[]{:S(2)}) collective-permute-start(bf16[24,16]{1,0:T(8,128)(2,1)S(1)} %select_convert_fusion.4), channel_id=1, source_target_pairs={{0,4},{4,0},{1,5},{5,1},{2,6},{6,2},{3,7},{7,3},{8,12},{12,8},{9,1... | collective-permute-start | bytes 2312 | tf_op jit(solution)/shard_map/ppermute | solution.py:19
  45.6 7.0 %collective-permute-start.9 = (bf16[24,16]{1,0:T(8,128)(2,1)S(1)}, bf16[24,16]{1,0:T(8,128)(2,1)S(1)}, u32[]{:S(2)}, u32[]{:S(2)}) collective-permute-start(bf16[24,16]{1,0:T(8,128)(2,1)S(1)} %select_convert_fusion.3), channel_id=1, source_target_pairs={{0,4},{4,0},{1,5},{5,1},{2,6},{6,2},{3,7},{7,3},{8,12},{12,8},{9,1... | collective-permute-start | bytes 2312 | tf_op jit(solution)/shard_map/ppermute | solution.py:19
  52.7 8.4 %collective-permute-start.5 = (bf16[12,16]{1,0:T(8,128)(2,1)S(1)}, bf16[12,16]{1,0:T(8,128)(2,1)S(1)}, u32[]{:S(2)}, u32[]{:S(2)}) collective-permute-start(bf16[12,16]{1,0:T(8,128)(2,1)S(1)} %select_convert_fusion.6), channel_id=1, source_target_pairs={{0,2},{2,0},{1,3},{3,1},{4,6},{6,4},{5,7},{7,5},{8,10},{10,8},{9,1... | collective-permute-start | bytes 1160 | tf_op jit(solution)/shard_map/ppermute | solution.py:19
  55.3 5.8 %collective-permute-start.10 = (bf16[12,16]{1,0:T(8,128)(2,1)S(1)}, bf16[12,16]{1,0:T(8,128)(2,1)S(1)}, u32[]{:S(2)}, u32[]{:S(2)}) collective-permute-start(bf16[12,16]{1,0:T(8,128)(2,1)S(1)} %select_convert_fusion.5), channel_id=1, source_target_pairs={{0,2},{2,0},{1,3},{3,1},{4,6},{6,4},{5,7},{7,5},{8,10},{10,8},{9,1... | collective-permute-start | bytes 1160 | tf_op jit(solution)/shard_map/ppermute | solution.py:19
  58.6 11.2 %collective-permute-start.4 = (bf16[24,16,512]{2,1,0:T(8,128)(2,1)S(1)}, bf16[24,16,512]{2,1,0:T(8,128)(2,1)S(1)}, u32[]{:S(2)}, u32[]{:S(2)}) collective-permute-start(bf16[24,16,512]{2,1,0:T(8,128)(2,1)S(1)} %select_convert_fusion), channel_id=1, source_target_pairs={{0,4},{4,0},{1,5},{5,1},{2,6},{6,2},{3,7},{7,3},{8,12},{12,8},{9,1... | collective-permute-start | bytes 1179656 | tf_op jit(solution)/shard_map/ppermute | solution.py:19
  61.1 18.8 %collective-permute-start.7 = (bf16[6,16]{1,0:T(8,128)(2,1)S(1)}, bf16[6,16]{1,0:T(8,128)(2,1)S(1)}, u32[]{:S(2)}, u32[]{:S(2)}) collective-permute-start(bf16[6,16]{1,0:T(8,128)(2,1)S(1)} %select_convert_fusion.8), channel_id=1, source_target_pairs={{0,1},{1,0},{2,3},{3,2},{4,5},{5,4},{6,7},{7,6},{8,9},{9,8},{10,11... | collective-permute-start | bytes 584 | tf_op jit(solution)/shard_map/ppermute | solution.py:19
  70.1 41.1 %copy-start.2 = (bf16[1,512,128]{2,1,0:T(8,128)(2,1)S(1)}, bf16[1,512,128]{2,1,0:T(8,128)(2,1)}, u32[]{:S(2)}) copy-start(bf16[1,512,128]{2,1,0:T(8,128)(2,1)} %param.18) | copy-start | bytes 393220
  70.1 41.3 %copy-start.1 = (bf16[128,2048]{1,0:T(8,128)(2,1)S(1)}, bf16[128,2048]{1,0:T(8,128)(2,1)}, u32[]{:S(2)}) copy-start(bf16[128,2048]{1,0:T(8,128)(2,1)} %param.19) | copy-start | bytes 1572868
  70.1 7.7 %collective-permute-start.6 = (bf16[12,16,512]{2,1,0:T(8,128)(2,1)S(1)}, bf16[12,16,512]{2,1,0:T(8,128)(2,1)S(1)}, u32[]{:S(2)}, u32[]{:S(2)}) collective-permute-start(bf16[12,16,512]{2,1,0:T(8,128)(2,1)S(1)} %select_convert_fusion.1), channel_id=1, source_target_pairs={{0,2},{2,0},{1,3},{3,1},{4,6},{6,4},{5,7},{7,5},{8,10},{10,8},{9,1... | collective-permute-start | bytes 589832 | tf_op jit(solution)/shard_map/ppermute | solution.py:19
  72.9 7.1 %collective-permute-start.11 = (bf16[6,16]{1,0:T(8,128)(2,1)S(1)}, bf16[6,16]{1,0:T(8,128)(2,1)S(1)}, u32[]{:S(2)}, u32[]{:S(2)}) collective-permute-start(bf16[6,16]{1,0:T(8,128)(2,1)S(1)} %select_convert_fusion.7), channel_id=1, source_target_pairs={{0,1},{1,0},{2,3},{3,2},{4,5},{5,4},{6,7},{7,6},{8,9},{9,8},{10,11... | collective-permute-start | bytes 584 | tf_op jit(solution)/shard_map/ppermute | solution.py:19
  78.0 3.2 %collective-permute-start.8 = (bf16[6,16,512]{2,1,0:T(8,128)(2,1)S(1)}, bf16[6,16,512]{2,1,0:T(8,128)(2,1)S(1)}, u32[]{:S(2)}, u32[]{:S(2)}) collective-permute-start(bf16[6,16,512]{2,1,0:T(8,128)(2,1)S(1)} %select_convert_fusion.2), channel_id=1, source_target_pairs={{0,1},{1,0},{2,3},{3,2},{4,5},{5,4},{6,7},{7,6},{8,9},{9,8},{10,11... | collective-permute-start | bytes 294920 | tf_op jit(solution)/shard_map/ppermute | solution.py:19
  145.3 14.8 %collective-permute-start.14 = (bf16[8,2048]{1,0:T(8,128)(2,1)S(1)}, bf16[8,2048]{1,0:T(8,128)(2,1)S(1)}, u32[]{:S(2)}, u32[]{:S(2)}) collective-permute-start(bf16[8,2048]{1,0:T(8,128)(2,1)S(1)} %fusion), channel_id=1, source_target_pairs={{0,96},{32,128},{64,160},{96,192},{128,224},{160,256},{192,288},{2... | collective-permute-start | bytes 98312
  148.0 12.1 %collective-permute-start.13 = (bf16[8,2048]{1,0:T(8,128)(2,1)S(1)}, bf16[8,2048]{1,0:T(8,128)(2,1)S(1)}, u32[]{:S(2)}, u32[]{:S(2)}) collective-permute-start(bf16[8,2048]{1,0:T(8,128)(2,1)S(1)} %fusion), channel_id=1, source_target_pairs={{0,64},{32,96},{64,128},{96,160},{128,192},{160,224},{192,256},{22... | collective-permute-start | bytes 98312
  151.9 8.2 %collective-permute-start.12 = (bf16[8,2048]{1,0:T(8,128)(2,1)S(1)}, bf16[8,2048]{1,0:T(8,128)(2,1)S(1)}, u32[]{:S(2)}, u32[]{:S(2)}) collective-permute-start(bf16[8,2048]{1,0:T(8,128)(2,1)S(1)} %fusion), channel_id=1, source_target_pairs={{0,32},{32,64},{64,96},{96,128},{128,160},{160,192},{192,224},{224... | collective-permute-start | bytes 98312
  155.1 5.0 %collective-permute-start.15 = (bf16[6,2048]{1,0:T(8,128)(2,1)S(1)}, bf16[6,2048]{1,0:T(8,128)(2,1)S(1)}, u32[]{:S(2)}, u32[]{:S(2)}) collective-permute-start(bf16[6,2048]{1,0:T(8,128)(2,1)S(1)} %slice.98), channel_id=1, source_target_pairs={{0,128},{32,160},{64,192},{96,224},{128,256},{160,288},{192,320},{... | collective-permute-start | bytes 73736
where the time goes:
time: 163 us; the launch traced here: 161 us
  blocking collectives  63.5 us (39%)
  starting transfers between devices  47.4 us (29%)
  waiting for transfers between devices  32.6 us (20%)
  local copies, waits for them, and re-layouts  7.42 us (5%)
  matrix products  4.85 us (3%)
  other arithmetic  4.39 us (3%)
    ppermute x12, starting transfers between devices, from_partner(): return lax.ppermute(block, axis, route)  34.6 us
    unnamed x1, blocking collectives  33.7 us
    ppermute x12, waiting for transfers between devices, from_partner(): return lax.ppermute(block, axis, route)  32.5 us
    all_to_all x1, blocking collectives, per_device(): lax.all_to_all(for_sending(merged), 'grp', split_axis=1, concat_axis=0, t...  29.7 us
    unnamed x4, starting transfers between devices  12.8 us
  transfers between devices with their start and end apart: 16, of which 6 were waited for; matrix products, arithmetic and copies ran while one was open for 5% of the time, Pallas kernels for 0%

commit v1 on v0

--- a/solution.py
+++ b/solution.py
@@ -19,8 +19,9 @@
     return lax.ppermute(block, axis, route)
 
 
-def for_sending(value):
-    return jax.tree.map(lambda a: a.astype(jnp.bfloat16) if a.dtype == jnp.float32 else a, value)
+def bit_reversed(count):
+    width = count.bit_length() - 1
+    return [int(format(index, f"0{width}b")[::-1], 2) if width else 0 for index in range(count)]
 
 
 def ancestors(parent_row):
@@ -44,6 +45,26 @@
     former = jnp.where(upper_side, partner, mine)
     latter = jnp.where(upper_side, mine, partner)
     return jnp.concatenate([former, latter], axis=0)
+
+
+def split_high(high):
+    high_hi = high.astype(jnp.bfloat16)
+    high_lo = (high - high_hi.astype(jnp.float32)).astype(jnp.bfloat16)
+    return high_hi, high_lo
+
+
+def pack_part(part_sum, part_high, part_total, width):
+    high_hi, high_lo = split_high(part_high)
+    stats = jnp.concatenate([high_hi, high_lo, part_total.astype(jnp.bfloat16)], axis=1)
+    stats = jnp.pad(stats, ((0, 0), (0, width - stats.shape[1])))
+    return jnp.concatenate([part_sum.astype(jnp.bfloat16), stats[:, None, :]], axis=1)
+
+
+def unpack_part(packed, heads):
+    stats = packed[:, heads].astype(jnp.float32)
+    high = stats[:, :heads] + stats[:, heads : 2 * heads]
+    total = stats[:, 2 * heads : 3 * heads]
+    return packed[:, :heads].astype(jnp.float32), high, total
 
 
 def combine_parts(kept_part, received):
@@ -75,6 +96,7 @@
     token_count = q_nope.shape[0]
     rope_width = q_rope.shape[1] // head_count
     per_request = lax.axis_size("ep") // REQ_GRP
+    grp_size = lax.axis_size("grp")
     doublings = per_request.bit_length() - 1
     position = lax.axis_index("ep")
     local_rank = position % per_request
@@ -83,18 +105,30 @@
     nope_rows = q_nope.reshape(token_count, head_count, nope_width)
     rope_rows = q_rope.reshape(token_count, head_count, rope_width)
     queries = jnp.concatenate([absorb(nope_rows, w_key), rope_rows], axis=2)
-    for bit_level in range(doublings):
+    for bit_level in reversed(range(doublings)):
         partner = from_partner(queries, "ep", bit_level)
         queries = append_partner(queries, partner, position, bit_level)
-    pages_read = jnp.take(cache_pool, page_table, axis=0)
-    cached = pages_read.reshape(-1, pages_read.shape[2])
+    cached = cache_pool.reshape(-1, cache_pool.shape[2])
+    page_count, page_rows = cache_pool.shape[0], cache_pool.shape[1]
     pos_count = cached.shape[0]
     all_keys = jnp.concatenate([cached, tree_latent], axis=0)
+    slots = jnp.arange(page_count, dtype=jnp.int32)
+    logical_of_slot = jnp.sum(
+        jnp.where(page_table[:, None] == slots[None, :], slots[:, None], 0), axis=0
+    )
+    place = (
+        local_rank * pos_count
+        + jnp.repeat(logical_of_slot, page_rows) * page_rows
+        + jnp.tile(jnp.arange(page_rows, dtype=jnp.int32), page_count)
+    )
     my_length = lax.dynamic_index_in_dim(cache_len, local_request, 0, keepdims=False)
-    cache_ok = local_rank * pos_count + jnp.arange(pos_count, dtype=jnp.int32) < my_length
+    cache_ok = place < my_length
     parent_row = lax.dynamic_index_in_dim(parents, local_request, 0, keepdims=False)
     family = ancestors(parent_row)
-    tree_ok = lax.dynamic_slice_in_dim(family, local_rank * token_count, token_count, 1)
+    tree_cols = lax.dynamic_slice_in_dim(family, local_rank * token_count, token_count, 1)
+    tree_ok = tree_cols.reshape(per_request, token_count, token_count)[
+        jnp.array(bit_reversed(per_request))
+    ].reshape(TREE, token_count)
     allowed = jnp.concatenate(
         [jnp.broadcast_to(cache_ok[None, :], (TREE, pos_count)), tree_ok], axis=1
     )
@@ -113,7 +147,7 @@
         preferred_element_type=jnp.float32,
     )
     state = (partial_value, highest, total)
-    for bit_level in reversed(range(doublings)):
+    for bit_level in range(doublings):
         half_rows = state[0].shape[0] // 2
         upper_side = jnp.right_shift(position, bit_level) & 1 == 1
         lower_part = tuple((member[:half_rows] for member in state))
@@ -124,27 +158,31 @@
         sent_part = tuple(
             (jnp.where(upper_side, lower, upper) for lower, upper in zip(lower_part, upper_part))
         )
-        received = from_partner(
-            (for_sending(sent_part[0]), for_sending(sent_part[1]), for_sending(sent_part[2])),
-            "ep",
-            bit_level,
-        )
-        state = combine_parts(kept_part, received)
+        received = from_partner(pack_part(*sent_part, latent_width), "ep", bit_level)
+        state = combine_parts(kept_part, unpack_part(received, head_count))
     merged_sum, merged_high, merged_total = state
     merged = merged_sum / merged_total[..., None]
     spread = lax.all_to_all(
-        for_sending(merged), "grp", split_axis=1, concat_axis=0, tiled=True
-    ).astype(merged.dtype)
-    head_rows = jnp.einsum(
-        "thr,hrn->thn", spread, w_value.astype(jnp.float32), precision=lax.Precision.HIGHEST
+        merged.astype(jnp.bfloat16), "grp", split_axis=1, concat_axis=0, tiled=True
+    )
+    spread = spread.reshape(grp_size, token_count, latent_width)[jnp.array(bit_reversed(grp_size))]
+    head_rows = jnp.dot(
+        spread.reshape(grp_size * token_count, latent_width),
+        w_value[0],
+        preferred_element_type=jnp.float32,
     ).astype(jnp.bfloat16)
-    head_rows = head_rows.reshape(head_rows.shape[0], -1)
-    return lax.psum_scatter(
-        jnp.dot(head_rows, out_weight, preferred_element_type=jnp.float32).astype(jnp.bfloat16),
-        "grp",
-        scatter_dimension=0,
-        tiled=True,
-    )
+    rows_out = jnp.dot(head_rows, out_weight, preferred_element_type=jnp.float32)
+    group = lax.axis_index("grp")
+    for bit_level in range(grp_size.bit_length() - 1):
+        half_rows = rows_out.shape[0] // 2
+        upper_side = jnp.right_shift(group, bit_level) & 1 == 1
+        lower, upper = rows_out[:half_rows], rows_out[half_rows:]
+        kept = jnp.where(upper_side, upper, lower)
+        sent = jnp.where(upper_side, lower, upper)
+        rows_out = kept + from_partner(sent.astype(jnp.bfloat16), "grp", bit_level).astype(
+            jnp.float32
+        )
+    return rows_out.astype(jnp.bfloat16)
 
 
 def solution(mesh):

time: 163 us -> 132 us (0.81)
  blocking collectives: 63.5 us -> 0 us
  waiting for transfers between devices: 32.6 us -> 64.4 us
  starting transfers between devices: 47.4 us -> 49.7 us
  local copies, waits for them, and re-layouts: 7.42 us -> 5.16 us
    unnamed x1 -> x0, blocking collectives: 33.7 us -> none
    all_to_all x1 -> x0, blocking collectives: 29.7 us -> none  [per_device(): lax.all_to_all(for_sending(merged), 'grp', split_axis=1, concat_axis=0, t...]
    ppermute x12 -> x10, waiting for transfers between devices: 32.5 us -> 51 us  [from_partner(): return lax.ppermute(block, axis, route)]
    all_to_all x0 -> x1, starting transfers between devices: none -> 15.2 us  [per_device(): lax.all_to_all(merged.astype(jnp.bfloat16), 'grp', split_axis=1, concat_a...]
    all_to_all x0 -> x1, waiting for transfers between devices: none -> 13.4 us  [per_device(): lax.all_to_all(merged.astype(jnp.bfloat16), 'grp', split_axis=1, concat_a...]
    unnamed x4 -> x0, starting transfers between devices: 12.8 us -> none
    unnamed x16 -> x17, local copies, waits for them, and re-layouts: 3.15 us -> 0.66 us
    ppermute x12 -> x10, starting transfers between devices: 34.6 us -> 34.5 us  [from_partner(): return lax.ppermute(block, axis, route)]
  transfers between devices with their start and end apart: 16 -> 11, of which waited for: 6 -> 11; matrix products, arithmetic and copies ran while one was open for 5% -> 3% of each run, Pallas kernels for 0% -> 0%
where the time goes in v1:
time: 132 us; the launch traced here: 131 us
  waiting for transfers between devices  64.4 us (49%)
  starting transfers between devices  49.7 us (38%)
  matrix products  5.72 us (4%)
  other arithmetic  5.69 us (4%)
  local copies, waits for them, and re-layouts  5.16 us (4%)
    ppermute x10, waiting for transfers between devices, from_partner(): return lax.ppermute(block, axis, route)  51 us
    ppermute x10, starting transfers between devices, from_partner(): return lax.ppermute(block, axis, route)  34.5 us
    all_to_all x1, starting transfers between devices, per_device(): lax.all_to_all(merged.astype(jnp.bfloat16), 'grp', split_axis=1, concat_a...  15.2 us
    all_to_all x1, waiting for transfers between devices, per_device(): lax.all_to_all(merged.astype(jnp.bfloat16), 'grp', split_axis=1, concat_a...  13.4 us
  transfers between devices with their start and end apart: 11, of which 11 were waited for; matrix products, arithmetic and copies ran while one was open for 3% of the time, Pallas kernels for 0%

profile of v1, /device:TPU:6, one launch (start us, length us, event | category | flops | bytes accessed | tf_op | source)
XLA Modules:
  0.0 131.3 jit_solution(8417598578340801870)
XLA Ops:
  1.6 1.4 %fusion.3 = bf16[6,16,512]{2,0,1:T(8,128)(2,1)S(1)} fusion(bf16[16,512,128]{2,1,0:T(8,128)(2,1)S(1)} %copy-done, bf16[6,2048]{1,0:T(8,128)(2,1)} %param.12), kind=kOutput, calls=%fused_computation.8 | convolution fusion | flops 12632064 | bytes 2220032 | tf_op jit(solution)/shard_map/thn,hrn->thr/dot_general | solution.py:38
  3.1 5.1 %collective-permute-start = (bf16[6,16,576]{2,0,1:T(8,128)(2,1)S(1)}, bf16[6,16,576]{2,0,1:T(8,128)(2,1)S(1)}, u32[]{:S(2)}, u32[]{:S(2)}) collective-permute-start(bf16[6,16,576]{2,0,1:T(8,128)(2,1)S(1)} %pad_maximum_fusion.6), channel_id=1, source_target_pairs={{0,4},{4,0},{1,5},{5,1},{2,6},{6,2},{3,7},{7,3},{8,12},{12,8},{9,1... | collective-permute-start | bytes 331784 | tf_op jit(solution)/shard_map/ppermute | solution.py:19
  12.6 3.5 %collective-permute-start.1 = (bf16[12,16,576]{2,0,1:T(8,128)(2,1)S(1)}, bf16[12,16,576]{2,0,1:T(8,128)(2,1)S(1)}, u32[]{:S(2)}, u32[]{:S(2)}) collective-permute-start(bf16[12,16,576]{2,0,1:T(8,128)(2,1)S(1)} %pad_maximum_fusion.4), channel_id=1, source_target_pairs={{0,2},{2,0},{1,3},{3,1},{4,6},{6,4},{5,7},{7,5},{8,10},{10,8},{9,1... | collective-permute-start | bytes 663560 | tf_op jit(solution)/shard_map/ppermute | solution.py:19
  16.1 7.0 %collective-permute-done.1 = bf16[12,16,576]{2,0,1:T(8,128)(2,1)S(1)} collective-permute-done((bf16[12,16,576]{2,0,1:T(8,128)(2,1)S(1)}, bf16[12,16,576]{2,0,1:T(8,128)(2,1)S(1)}, u32[]{:S(2)}, u32[]{:S(2)}) %collective-permute-start.1) | collective-permute-done | bytes 221216 | tf_op jit(solution)/shard_map/ppermute | solution.py:19
  24.2 1.9 %collective-permute-start.2 = (bf16[24,16,576]{2,0,1:T(8,128)(2,1)}, bf16[24,16,576]{2,0,1:T(8,128)(2,1)S(1)}, u32[]{:S(2)}, u32[]{:S(2)}) collective-permute-start(bf16[24,16,576]{2,0,1:T(8,128)(2,1)} %pad_maximum_fusion.3), channel_id=1, source_target_pairs={{0,1},{1,0},{2,3},{3,2},{4,5},{5,4},{6,7},{7,6},{8,9},{9,8},{10,11... | collective-permute-start | bytes 1327112 | tf_op jit(solution)/shard_map/ppermute | solution.py:19
  27.0 1.2 collective-permute-done.2
  28.6 1.2 fusion
  31.9 2.0 %collective-permute-start.3 = (bf16[24,17,512]{2,0,1:T(8,128)(2,1)S(1)}, bf16[24,17,512]{2,0,1:T(8,128)(2,1)S(1)}, u32[]{:S(2)}, u32[]{:S(2)}) collective-permute-start(bf16[24,17,512]{2,0,1:T(8,128)(2,1)S(1)} %copy.89), channel_id=1, source_target_pairs={{0,1},{1,0},{2,3},{3,2},{4,5},{5,4},{6,7},{7,6},{8,9},{9,8},{10,11... | collective-permute-start | bytes 1253384 | tf_op jit(solution)/shard_map/ppermute | solution.py:19
  34.0 1.6 %collective-permute-done.3 = bf16[24,17,512]{2,0,1:T(8,128)(2,1)S(1)} collective-permute-done((bf16[24,17,512]{2,0,1:T(8,128)(2,1)S(1)}, bf16[24,17,512]{2,0,1:T(8,128)(2,1)S(1)}, u32[]{:S(2)}, u32[]{:S(2)}) %collective-permute-start.3) | collective-permute-done | bytes 417824 | tf_op jit(solution)/shard_map/ppermute | solution.py:19
  36.3 3.6 %collective-permute-start.4 = (bf16[12,17,512]{2,1,0:T(8,128)(2,1)S(1)}, bf16[12,17,512]{2,1,0:T(8,128)(2,1)S(1)}, u32[]{:S(2)}, u32[]{:S(2)}) collective-permute-start(bf16[12,17,512]{2,1,0:T(8,128)(2,1)S(1)} %pad_maximum_fusion.5), channel_id=1, source_target_pairs={{0,2},{2,0},{1,3},{3,1},{4,6},{6,4},{5,7},{7,5},{8,10},{10,8},{9,1... | collective-permute-start | bytes 626696 | tf_op jit(solution)/shard_map/ppermute | solution.py:19
  39.9 7.5 %collective-permute-done.4 = bf16[12,17,512]{2,1,0:T(8,128)(2,1)S(1)} collective-permute-done((bf16[12,17,512]{2,1,0:T(8,128)(2,1)S(1)}, bf16[12,17,512]{2,1,0:T(8,128)(2,1)S(1)}, u32[]{:S(2)}, u32[]{:S(2)}) %collective-permute-start.4) | collective-permute-done | bytes 208928 | tf_op jit(solution)/shard_map/ppermute | solution.py:19
  47.8 5.1 %collective-permute-start.5 = (bf16[6,17,512]{2,1,0:T(8,128)(2,1)S(1)}, bf16[6,17,512]{2,1,0:T(8,128)(2,1)S(1)}, u32[]{:S(2)}, u32[]{:S(2)}) collective-permute-start(bf16[6,17,512]{2,1,0:T(8,128)(2,1)S(1)} %pad_maximum_fusion.7), channel_id=1, source_target_pairs={{0,4},{4,0},{1,5},{5,1},{2,6},{6,2},{3,7},{7,3},{8,12},{12,8},{9,1... | collective-permute-start | bytes 313352 | tf_op jit(solution)/shard_map/ppermute | solution.py:19
  52.9 3.4 %collective-permute-done.5 = bf16[6,17,512]{2,1,0:T(8,128)(2,1)S(1)} collective-permute-done((bf16[6,17,512]{2,1,0:T(8,128)(2,1)S(1)}, bf16[6,17,512]{2,1,0:T(8,128)(2,1)S(1)}, u32[]{:S(2)}, u32[]{:S(2)}) %collective-permute-start.5) | collective-permute-done | bytes 104480 | tf_op jit(solution)/shard_map/ppermute | solution.py:19
  57.3 15.2 %all-to-all-start = ((bf16[6,16,512]{2,0,1:T(8,128)(2,1)}), bf16[6,16,512]{2,0,1:T(8,128)(2,1)S(1)}, u32[]{:S(2)}, u32[]{:S(2)}) async-start(bf16[6,16,512]{2,0,1:T(8,128)(2,1)} %copy.94), calls=%async_computation | async-start | bytes 262144 | tf_op jit(solution)/shard_map/all_to_all | solution.py:165
  72.5 13.4 %all-to-all-done = bf16[6,16,512]{2,0,1:T(8,128)(2,1)S(1)} async-done(((bf16[6,16,512]{2,0,1:T(8,128)(2,1)}), bf16[6,16,512]{2,0,1:T(8,128)(2,1)S(1)}, u32[]{:S(2)}, u32[]{:S(2)}) %all-to-all-start) | async-done | bytes 98336 | tf_op jit(solution)/shard_map/all_to_all | solution.py:165
  86.5 1.3 fusion.4
  87.8 2.9 %collective-permute-start.6 = (bf16[48,2048]{1,0:T(8,128)(2,1)S(1)}, bf16[48,2048]{1,0:T(8,128)(2,1)S(1)}, u32[]{:S(2)}, u32[]{:S(2)}) collective-permute-start(bf16[48,2048]{1,0:T(8,128)(2,1)S(1)} %select_convert_fusion.1), channel_id=1, source_target_pairs={{0,32},{32,0},{64,96},{96,64},{128,160},{160,128},{192,224},{224,1... | collective-permute-start | bytes 589832 | tf_op jit(solution)/shard_map/ppermute | solution.py:19
  90.8 4.6 %collective-permute-done.6 = bf16[48,2048]{1,0:T(8,128)(2,1)S(1)} collective-permute-done((bf16[48,2048]{1,0:T(8,128)(2,1)S(1)}, bf16[48,2048]{1,0:T(8,128)(2,1)S(1)}, u32[]{:S(2)}, u32[]{:S(2)}) %collective-permute-start.6) | collective-permute-done | bytes 196640 | tf_op jit(solution)/shard_map/ppermute | solution.py:19
  95.5 3.2 %collective-permute-start.7 = (bf16[24,2048]{1,0:T(8,128)(2,1)S(1)}, bf16[24,2048]{1,0:T(8,128)(2,1)S(1)}, u32[]{:S(2)}, u32[]{:S(2)}) collective-permute-start(bf16[24,2048]{1,0:T(8,128)(2,1)S(1)} %select_convert_fusion.3), channel_id=1, source_target_pairs={{0,64},{64,0},{32,96},{96,32},{128,192},{192,128},{160,224},{224,1... | collective-permute-start | bytes 294920 | tf_op jit(solution)/shard_map/ppermute | solution.py:19
  98.7 5.2 %collective-permute-done.7 = bf16[24,2048]{1,0:T(8,128)(2,1)S(1)} collective-permute-done((bf16[24,2048]{1,0:T(8,128)(2,1)S(1)}, bf16[24,2048]{1,0:T(8,128)(2,1)S(1)}, u32[]{:S(2)}, u32[]{:S(2)}) %collective-permute-start.7) | collective-permute-done | bytes 98336 | tf_op jit(solution)/shard_map/ppermute | solution.py:19
  104.0 3.5 %collective-permute-start.8 = (bf16[12,2048]{1,0:T(8,128)(2,1)S(1)}, bf16[12,2048]{1,0:T(8,128)(2,1)S(1)}, u32[]{:S(2)}, u32[]{:S(2)}) collective-permute-start(bf16[12,2048]{1,0:T(8,128)(2,1)S(1)} %select_convert_fusion.5), channel_id=1, source_target_pairs={{0,128},{128,0},{32,160},{160,32},{64,192},{192,64},{96,224},{224,... | collective-permute-start | bytes 147464 | tf_op jit(solution)/shard_map/ppermute | solution.py:19
  107.5 8.2 %collective-permute-done.8 = bf16[12,2048]{1,0:T(8,128)(2,1)S(1)} collective-permute-done((bf16[12,2048]{1,0:T(8,128)(2,1)S(1)}, bf16[12,2048]{1,0:T(8,128)(2,1)S(1)}, u32[]{:S(2)}, u32[]{:S(2)}) %collective-permute-start.8) | collective-permute-done | bytes 49184 | tf_op jit(solution)/shard_map/ppermute | solution.py:19
  115.8 3.6 %collective-permute-start.9 = (bf16[6,2048]{1,0:T(8,128)(2,1)S(1)}, bf16[6,2048]{1,0:T(8,128)(2,1)S(1)}, u32[]{:S(2)}, u32[]{:S(2)}) collective-permute-start(bf16[6,2048]{1,0:T(8,128)(2,1)S(1)} %select_convert_fusion.6), channel_id=1, source_target_pairs={{0,256},{256,0},{32,288},{288,32},{64,320},{320,64},{96,352},{352,... | collective-permute-start | bytes 73736 | tf_op jit(solution)/shard_map/ppermute | solution.py:19
  119.4 11.2 %collective-permute-done.9 = bf16[6,2048]{1,0:T(8,128)(2,1)S(1)} collective-permute-done((bf16[6,2048]{1,0:T(8,128)(2,1)S(1)}, bf16[6,2048]{1,0:T(8,128)(2,1)S(1)}, u32[]{:S(2)}, u32[]{:S(2)}) %collective-permute-start.9) | collective-permute-done | bytes 24608 | tf_op jit(solution)/shard_map/ppermute | solution.py:19
  (91 shorter events, 13.8 us)
Async XLA Ops:
  0.0 1.6 %copy-start = (bf16[16,512,128]{2,1,0:T(8,128)(2,1)S(1)}, bf16[16,512,128]{2,1,0:T(8,128)(2,1)}, u32[]{:S(2)}) copy-start(bf16[16,512,128]{2,1,0:T(8,128)(2,1)} %param.19) | copy-start | bytes 6291460
  0.0 10.1 %copy-start.3 = (s32[8]{0:T(128)S(1)}, s32[8]{0:T(128)}, u32[]{:S(2)}) copy-start(s32[8]{0:T(128)} %constant.105) | copy-start | bytes 100
  0.0 10.7 %copy-start.6 = (s32[4]{0:T(128)S(1)}, s32[4]{0:T(128)}, u32[]{:S(2)}) copy-start(s32[4]{0:T(128)} %param.17) | copy-start | bytes 52
  0.0 11.3 %copy-start.7 = (s32[8]{0:T(128)S(1)}, s32[8]{0:T(128)}, u32[]{:S(2)}) copy-start(s32[8]{0:T(128)} %param.16) | copy-start | bytes 100
  3.1 9.3 %collective-permute-start = (bf16[6,16,576]{2,0,1:T(8,128)(2,1)S(1)}, bf16[6,16,576]{2,0,1:T(8,128)(2,1)S(1)}, u32[]{:S(2)}, u32[]{:S(2)}) collective-permute-start(bf16[6,16,576]{2,0,1:T(8,128)(2,1)S(1)} %pad_maximum_fusion.6), channel_id=1, source_target_pairs={{0,4},{4,0},{1,5},{5,1},{2,6},{6,2},{3,7},{7,3},{8,12},{12,8},{9,1... | collective-permute-start | bytes 331784 | tf_op jit(solution)/shard_map/ppermute | solution.py:19
  12.6 10.5 %collective-permute-start.1 = (bf16[12,16,576]{2,0,1:T(8,128)(2,1)S(1)}, bf16[12,16,576]{2,0,1:T(8,128)(2,1)S(1)}, u32[]{:S(2)}, u32[]{:S(2)}) collective-permute-start(bf16[12,16,576]{2,0,1:T(8,128)(2,1)S(1)} %pad_maximum_fusion.4), channel_id=1, source_target_pairs={{0,2},{2,0},{1,3},{3,1},{4,6},{6,4},{5,7},{7,5},{8,10},{10,8},{9,1... | collective-permute-start | bytes 663560 | tf_op jit(solution)/shard_map/ppermute | solution.py:19
  24.2 4.0 %collective-permute-start.2 = (bf16[24,16,576]{2,0,1:T(8,128)(2,1)}, bf16[24,16,576]{2,0,1:T(8,128)(2,1)S(1)}, u32[]{:S(2)}, u32[]{:S(2)}) collective-permute-start(bf16[24,16,576]{2,0,1:T(8,128)(2,1)} %pad_maximum_fusion.3), channel_id=1, source_target_pairs={{0,1},{1,0},{2,3},{3,2},{4,5},{5,4},{6,7},{7,6},{8,9},{9,8},{10,11... | collective-permute-start | bytes 1327112 | tf_op jit(solution)/shard_map/ppermute | solution.py:19
  27.0 1.6 %copy-start.4 = (bf16[8,64,576]{2,1,0:T(8,128)(2,1)S(1)}, bf16[8,64,576]{2,1,0:T(8,128)(2,1)}, u32[]{:S(2)}) copy-start(bf16[8,64,576]{2,1,0:T(8,128)(2,1)} %param.15) | copy-start | bytes 1769476
  27.0 1.6 %copy-start.5 = (bf16[6,576]{1,0:T(8,128)(2,1)S(1)}, bf16[6,576]{1,0:T(8,128)(2,1)}, u32[]{:S(2)}) copy-start(bf16[6,576]{1,0:T(8,128)(2,1)} %param.14) | copy-start | bytes 20740
  31.9 3.7 %collective-permute-start.3 = (bf16[24,17,512]{2,0,1:T(8,128)(2,1)S(1)}, bf16[24,17,512]{2,0,1:T(8,128)(2,1)S(1)}, u32[]{:S(2)}, u32[]{:S(2)}) collective-permute-start(bf16[24,17,512]{2,0,1:T(8,128)(2,1)S(1)} %copy.89), channel_id=1, source_target_pairs={{0,1},{1,0},{2,3},{3,2},{4,5},{5,4},{6,7},{7,6},{8,9},{9,8},{10,11... | collective-permute-start | bytes 1253384 | tf_op jit(solution)/shard_map/ppermute | solution.py:19
  36.2 36.3 %copy-start.2 = (s32[16]{0:T(128)S(1)}, s32[16]{0:T(128)}, u32[]{:S(2)}) copy-start(s32[16]{0:T(128)} %constant.106) | copy-start | bytes 196
  36.2 50.2 %copy-start.1 = (bf16[128,2048]{1,0:T(8,128)(2,1)S(1)}, bf16[128,2048]{1,0:T(8,128)(2,1)}, u32[]{:S(2)}) copy-start(bf16[128,2048]{1,0:T(8,128)(2,1)} %param.21) | copy-start | bytes 1572868
  36.3 11.1 %collective-permute-start.4 = (bf16[12,17,512]{2,1,0:T(8,128)(2,1)S(1)}, bf16[12,17,512]{2,1,0:T(8,128)(2,1)S(1)}, u32[]{:S(2)}, u32[]{:S(2)}) collective-permute-start(bf16[12,17,512]{2,1,0:T(8,128)(2,1)S(1)} %pad_maximum_fusion.5), channel_id=1, source_target_pairs={{0,2},{2,0},{1,3},{3,1},{4,6},{6,4},{5,7},{7,5},{8,10},{10,8},{9,1... | collective-permute-start | bytes 626696 | tf_op jit(solution)/shard_map/ppermute | solution.py:19
  47.8 8.5 %collective-permute-start.5 = (bf16[6,17,512]{2,1,0:T(8,128)(2,1)S(1)}, bf16[6,17,512]{2,1,0:T(8,128)(2,1)S(1)}, u32[]{:S(2)}, u32[]{:S(2)}) collective-permute-start(bf16[6,17,512]{2,1,0:T(8,128)(2,1)S(1)} %pad_maximum_fusion.7), channel_id=1, source_target_pairs={{0,4},{4,0},{1,5},{5,1},{2,6},{6,2},{3,7},{7,3},{8,12},{12,8},{9,1... | collective-permute-start | bytes 313352 | tf_op jit(solution)/shard_map/ppermute | solution.py:19
  57.3 28.6 %all-to-all-start = ((bf16[6,16,512]{2,0,1:T(8,128)(2,1)}), bf16[6,16,512]{2,0,1:T(8,128)(2,1)S(1)}, u32[]{:S(2)}, u32[]{:S(2)}) async-start(bf16[6,16,512]{2,0,1:T(8,128)(2,1)} %copy.94), calls=%async_computation | async-start | bytes 262144 | tf_op jit(solution)/shard_map/all_to_all | solution.py:165
  87.8 7.6 %collective-permute-start.6 = (bf16[48,2048]{1,0:T(8,128)(2,1)S(1)}, bf16[48,2048]{1,0:T(8,128)(2,1)S(1)}, u32[]{:S(2)}, u32[]{:S(2)}) collective-permute-start(bf16[48,2048]{1,0:T(8,128)(2,1)S(1)} %select_convert_fusion.1), channel_id=1, source_target_pairs={{0,32},{32,0},{64,96},{96,64},{128,160},{160,128},{192,224},{224,1... | collective-permute-start | bytes 589832 | tf_op jit(solution)/shard_map/ppermute | solution.py:19
  95.5 8.5 %collective-permute-start.7 = (bf16[24,2048]{1,0:T(8,128)(2,1)S(1)}, bf16[24,2048]{1,0:T(8,128)(2,1)S(1)}, u32[]{:S(2)}, u32[]{:S(2)}) collective-permute-start(bf16[24,2048]{1,0:T(8,128)(2,1)S(1)} %select_convert_fusion.3), channel_id=1, source_target_pairs={{0,64},{64,0},{32,96},{96,32},{128,192},{192,128},{160,224},{224,1... | collective-permute-start | bytes 294920 | tf_op jit(solution)/shard_map/ppermute | solution.py:19
  104.0 11.7 %collective-permute-start.8 = (bf16[12,2048]{1,0:T(8,128)(2,1)S(1)}, bf16[12,2048]{1,0:T(8,128)(2,1)S(1)}, u32[]{:S(2)}, u32[]{:S(2)}) collective-permute-start(bf16[12,2048]{1,0:T(8,128)(2,1)S(1)} %select_convert_fusion.5), channel_id=1, source_target_pairs={{0,128},{128,0},{32,160},{160,32},{64,192},{192,64},{96,224},{224,... | collective-permute-start | bytes 147464 | tf_op jit(solution)/shard_map/ppermute | solution.py:19
  115.8 14.9 %collective-permute-start.9 = (bf16[6,2048]{1,0:T(8,128)(2,1)S(1)}, bf16[6,2048]{1,0:T(8,128)(2,1)S(1)}, u32[]{:S(2)}, u32[]{:S(2)}) collective-permute-start(bf16[6,2048]{1,0:T(8,128)(2,1)S(1)} %select_convert_fusion.6), channel_id=1, source_target_pairs={{0,256},{256,0},{32,288},{288,32},{64,320},{320,64},{96,352},{352,... | collective-permute-start | bytes 73736 | tf_op jit(solution)/shard_map/ppermute | solution.py:19

commit v2 on v1

--- a/solution.py
+++ b/solution.py
@@ -102,6 +102,10 @@
     local_rank = position % per_request
     local_request = position // per_request
     score_scale = 1.0 / math.sqrt(nope_width + rope_width)
+    column_count = out_weight.shape[1] // 2
+    own_columns = lax.dynamic_slice_in_dim(out_weight, (position & 1) * column_count, column_count, 1)
+    out_columns = lax.all_gather(own_columns, "grp", axis=0, tiled=True)
+    all_values = lax.all_gather(w_value, "grp", axis=0, tiled=True)
     nope_rows = q_nope.reshape(token_count, head_count, nope_width)
     rope_rows = q_rope.reshape(token_count, head_count, rope_width)
     queries = jnp.concatenate([absorb(nope_rows, w_key), rope_rows], axis=2)
@@ -161,28 +165,24 @@
         received = from_partner(pack_part(*sent_part, latent_width), "ep", bit_level)
         state = combine_parts(kept_part, unpack_part(received, head_count))
     merged_sum, merged_high, merged_total = state
-    merged = merged_sum / merged_total[..., None]
-    spread = lax.all_to_all(
-        merged.astype(jnp.bfloat16), "grp", split_axis=1, concat_axis=0, tiled=True
-    )
-    spread = spread.reshape(grp_size, token_count, latent_width)[jnp.array(bit_reversed(grp_size))]
-    head_rows = jnp.dot(
-        spread.reshape(grp_size * token_count, latent_width),
-        w_value[0],
-        preferred_element_type=jnp.float32,
+    merged = (merged_sum / merged_total[..., None]).astype(jnp.bfloat16)
+    head_rows = jnp.einsum(
+        "thr,hrn->thn", merged, all_values, preferred_element_type=jnp.float32
     ).astype(jnp.bfloat16)
-    rows_out = jnp.dot(head_rows, out_weight, preferred_element_type=jnp.float32)
-    group = lax.axis_index("grp")
-    for bit_level in range(grp_size.bit_length() - 1):
-        half_rows = rows_out.shape[0] // 2
-        upper_side = jnp.right_shift(group, bit_level) & 1 == 1
-        lower, upper = rows_out[:half_rows], rows_out[half_rows:]
-        kept = jnp.where(upper_side, upper, lower)
-        sent = jnp.where(upper_side, lower, upper)
-        rows_out = kept + from_partner(sent.astype(jnp.bfloat16), "grp", bit_level).astype(
-            jnp.float32
-        )
-    return rows_out.astype(jnp.bfloat16)
+    head_rows = head_rows.reshape(token_count, head_count * nope_width)
+    both_rows = append_partner(head_rows, from_partner(head_rows, "ep", 0), position, 0)
+    out_half = jnp.dot(both_rows, out_columns, preferred_element_type=jnp.float32).astype(
+        jnp.bfloat16
+    )
+    core_upper = position & 1 == 1
+    mine = jnp.where(core_upper, out_half[token_count:], out_half[:token_count])
+    theirs = jnp.where(core_upper, out_half[:token_count], out_half[token_count:])
+    other_half = from_partner(theirs, "ep", 0)
+    return jnp.where(
+        core_upper,
+        jnp.concatenate([other_half, mine], axis=1),
+        jnp.concatenate([mine, other_half], axis=1),
+    )
 
 
 def solution(mesh):

time: 132 us -> 178 us (1.35)
  waiting for transfers between devices: 64.4 us -> 119 us
  starting transfers between devices: 49.7 us -> 25 us
  between operations: 0.62 us -> 13.9 us
  matrix products: 5.72 us -> 9.24 us
    all_gather x0 -> x2, waiting for transfers between devices: none -> 95.2 us  [the longest x1 71.7 us: per_device(): out_columns = lax.all_gather(own_columns, 'grp', axis=0, tiled=True)]
    ppermute x10 -> x8, waiting for transfers between devices: 51 us -> 23.2 us  [from_partner(): return lax.ppermute(block, axis, route)]
    all_to_all x1 -> x0, starting transfers between devices: 15.2 us -> none  [per_device(): lax.all_to_all(merged.astype(jnp.bfloat16), 'grp', split_axis=1, concat_a...]
    all_to_all x1 -> x0, waiting for transfers between devices: 13.4 us -> none  [per_device(): lax.all_to_all(merged.astype(jnp.bfloat16), 'grp', split_axis=1, concat_a...]
    ppermute x10 -> x8, starting transfers between devices: 34.5 us -> 25 us  [from_partner(): return lax.ppermute(block, axis, route)]
    dot_general x1 -> x2, matrix products: 1.28 us -> 4.81 us  [the longest x1 2.84 us: per_device(): jnp.dot(both_rows, out_columns, preferred_element_type=jnp.float32)]
  transfers between devices with their start and end apart: 11 -> 10, of which waited for: 11 -> 10; matrix products, arithmetic and copies ran while one was open for 3% -> 9% of each run, Pallas kernels for 0% -> 0%
where the time goes in v2:
time: 178 us; the launch traced here: 177 us
  waiting for transfers between devices  119 us (67%)
  starting transfers between devices  25 us (14%)
  between operations  13.9 us (8%)
  matrix products  9.24 us (5%)
  other arithmetic  5.51 us (3%)
  local copies, waits for them, and re-layouts  3.87 us (2%)
    all_gather x1, waiting for transfers between devices, per_device(): out_columns = lax.all_gather(own_columns, 'grp', axis=0, tiled=True)  71.7 us
    ppermute x8, starting transfers between devices, from_partner(): return lax.ppermute(block, axis, route)  25 us
    all_gather x1, waiting for transfers between devices, per_device(): all_values = lax.all_gather(w_value, 'grp', axis=0, tiled=True)  23.6 us
    ppermute x8, waiting for transfers between devices, from_partner(): return lax.ppermute(block, axis, route)  23.2 us
  transfers between devices with their start and end apart: 10, of which 10 were waited for; matrix products, arithmetic and copies ran while one was open for 9% of the time, Pallas kernels for 0%

profile of v2, /device:TPU:6, one launch (start us, length us, event | category | flops | bytes accessed | tf_op | source)
XLA Modules:
  0.0 176.7 jit_solution(14294641664372504808)
XLA Ops:
  8.2 1.4 fusion.3
  9.7 5.1 %collective-permute-start = (bf16[6,16,576]{2,0,1:T(8,128)(2,1)S(1)}, bf16[6,16,576]{2,0,1:T(8,128)(2,1)S(1)}, u32[]{:S(2)}, u32[]{:S(2)}) collective-permute-start(bf16[6,16,576]{2,0,1:T(8,128)(2,1)S(1)} %pad_maximum_fusion.6), channel_id=1, source_target_pairs={{0,4},{4,0},{1,5},{5,1},{2,6},{6,2},{3,7},{7,3},{8,12},{12,8},{9,1... | collective-permute-start | bytes 331784 | tf_op jit(solution)/shard_map/ppermute | solution.py:19
  18.0 1.0 collective-permute-done
  19.2 3.5 %collective-permute-start.1 = (bf16[12,16,576]{2,0,1:T(8,128)(2,1)S(1)}, bf16[12,16,576]{2,0,1:T(8,128)(2,1)S(1)}, u32[]{:S(2)}, u32[]{:S(2)}) collective-permute-start(bf16[12,16,576]{2,0,1:T(8,128)(2,1)S(1)} %pad_maximum_fusion.4), channel_id=1, source_target_pairs={{0,2},{2,0},{1,3},{3,1},{4,6},{6,4},{5,7},{7,5},{8,10},{10,8},{9,1... | collective-permute-start | bytes 663560 | tf_op jit(solution)/shard_map/ppermute | solution.py:19
  23.4 6.3 %collective-permute-done.1 = bf16[12,16,576]{2,0,1:T(8,128)(2,1)S(1)} collective-permute-done((bf16[12,16,576]{2,0,1:T(8,128)(2,1)S(1)}, bf16[12,16,576]{2,0,1:T(8,128)(2,1)S(1)}, u32[]{:S(2)}, u32[]{:S(2)}) %collective-permute-start.1) | collective-permute-done | bytes 221216 | tf_op jit(solution)/shard_map/ppermute | solution.py:19
  29.9 0.9 pad_maximum_fusion.3
  30.8 1.9 %collective-permute-start.2 = (bf16[24,16,576]{2,0,1:T(8,128)(2,1)}, bf16[24,16,576]{2,0,1:T(8,128)(2,1)S(1)}, u32[]{:S(2)}, u32[]{:S(2)}) collective-permute-start(bf16[24,16,576]{2,0,1:T(8,128)(2,1)} %pad_maximum_fusion.3), channel_id=1, source_target_pairs={{0,1},{1,0},{2,3},{3,2},{4,5},{5,4},{6,7},{7,6},{8,9},{9,8},{10,11... | collective-permute-start | bytes 1327112 | tf_op jit(solution)/shard_map/ppermute | solution.py:19
  33.6 1.2 collective-permute-done.2
  35.2 1.2 fusion
  37.3 0.9 fusion.5
  38.5 2.0 %collective-permute-start.3 = (bf16[24,17,512]{2,0,1:T(8,128)(2,1)S(1)}, bf16[24,17,512]{2,0,1:T(8,128)(2,1)S(1)}, u32[]{:S(2)}, u32[]{:S(2)}) collective-permute-start(bf16[24,17,512]{2,0,1:T(8,128)(2,1)S(1)} %copy.89), channel_id=1, source_target_pairs={{0,1},{1,0},{2,3},{3,2},{4,5},{5,4},{6,7},{7,6},{8,9},{9,8},{10,11... | collective-permute-start | bytes 1253384 | tf_op jit(solution)/shard_map/ppermute | solution.py:19
  40.6 1.6 collective-permute-done.3
  42.8 3.5 %collective-permute-start.4 = (bf16[12,17,512]{2,1,0:T(8,128)(2,1)S(1)}, bf16[12,17,512]{2,1,0:T(8,128)(2,1)S(1)}, u32[]{:S(2)}, u32[]{:S(2)}) collective-permute-start(bf16[12,17,512]{2,1,0:T(8,128)(2,1)S(1)} %pad_maximum_fusion.5), channel_id=1, source_target_pairs={{0,2},{2,0},{1,3},{3,1},{4,6},{6,4},{5,7},{7,5},{8,10},{10,8},{9,1... | collective-permute-start | bytes 626696 | tf_op jit(solution)/shard_map/ppermute | solution.py:19
  46.3 7.5 %collective-permute-done.4 = bf16[12,17,512]{2,1,0:T(8,128)(2,1)S(1)} collective-permute-done((bf16[12,17,512]{2,1,0:T(8,128)(2,1)S(1)}, bf16[12,17,512]{2,1,0:T(8,128)(2,1)S(1)}, u32[]{:S(2)}, u32[]{:S(2)}) %collective-permute-start.4) | collective-permute-done | bytes 208928 | tf_op jit(solution)/shard_map/ppermute | solution.py:19
  54.2 5.1 %collective-permute-start.5 = (bf16[6,17,512]{2,1,0:T(8,128)(2,1)S(1)}, bf16[6,17,512]{2,1,0:T(8,128)(2,1)S(1)}, u32[]{:S(2)}, u32[]{:S(2)}) collective-permute-start(bf16[6,17,512]{2,1,0:T(8,128)(2,1)S(1)} %pad_maximum_fusion.7), channel_id=1, source_target_pairs={{0,4},{4,0},{1,5},{5,1},{2,6},{6,2},{3,7},{7,3},{8,12},{12,8},{9,1... | collective-permute-start | bytes 313352 | tf_op jit(solution)/shard_map/ppermute | solution.py:19
  59.3 3.4 %collective-permute-done.5 = bf16[6,17,512]{2,1,0:T(8,128)(2,1)S(1)} collective-permute-done((bf16[6,17,512]{2,1,0:T(8,128)(2,1)S(1)}, bf16[6,17,512]{2,1,0:T(8,128)(2,1)S(1)}, u32[]{:S(2)}, u32[]{:S(2)}) %collective-permute-start.5) | collective-permute-done | bytes 104480 | tf_op jit(solution)/shard_map/ppermute | solution.py:19
  63.0 23.6 %all-gather.3.cloned.1.call-done = bf16[16,512,128]{2,1,0:T(8,128)(2,1)} async-done(((bf16[1,512,128]{2,1,0:T(8,128)(2,1)}), bf16[16,512,128]{2,1,0:T(8,128)(2,1)}) %all-gather.3.cloned.1.call-update) | async-done | bytes 2097168 | tf_op jit(solution)/shard_map/all_gather | solution.py:108
  86.6 2.0 %fusion.4 = bf16[6,2048]{1,0:T(8,128)(2,1)S(1)} fusion(bf16[16,512,128]{2,1,0:T(8,128)(2,1)} %all-gather.3.cloned.1.call-done, bf16[6,16,512]{2,1,0:T(8,128)(2,1)S(1)} %divide_convert_fusion), kind=kOutput, calls=%fused_computation.10 | convolution fusion | flops 12595200 | bytes 2220032 | tf_op jit(solution)/shard_map/thr,hrn->thn/dot_general | solution.py:169
  88.5 1.9 %collective-permute-start.6 = (bf16[6,2048]{1,0:T(8,128)(2,1)S(1)}, bf16[6,2048]{1,0:T(8,128)(2,1)S(1)}, u32[]{:S(2)}, u32[]{:S(2)}) collective-permute-start(bf16[6,2048]{1,0:T(8,128)(2,1)S(1)} %fusion.4), channel_id=1, source_target_pairs={{0,1},{1,0},{2,3},{3,2},{4,5},{5,4},{6,7},{7,6},{8,9},{9,8},{10,11... | collective-permute-start | bytes 73736 | tf_op jit(solution)/shard_map/ppermute | solution.py:19
  90.5 1.2 collective-permute-done.6
  91.6 71.7 %all-gather.5.cloned.1.call-done = bf16[2048,1024]{1,0:T(8,128)(2,1)} async-done(((bf16[128,1024]{1,0:T(8,128)(2,1)}), bf16[2048,1024]{1,0:T(8,128)(2,1)}) %all-gather.5.cloned.1.call-update) | async-done | bytes 4194320 | tf_op jit(solution)/shard_map/all_gather | solution.py:107
  163.3 2.8 %convolution_convert_fusion.1 = bf16[12,1024]{1,0:T(8,128)(2,1)S(1)} fusion(bf16[2048,1024]{1,0:T(8,128)(2,1)} %all-gather.5.cloned.1.call-done, bf16[6,2048]{1,0:T(8,128)(2,1)S(1)} %get-tuple-element.29, bf16[6,2048]{1,0:T(8,128)(2,1)S(1)} %get-tuple-element.28), kind=kOutput, calls=%fused_computation.8 | convolution fusion | flops 50442240 | bytes 4268032 | tf_op jit(solution)/shard_map/dot_general | solution.py:174
  166.2 1.9 %collective-permute-start.7 = (bf16[6,1024]{1,0:T(8,128)(2,1)S(1)}, bf16[6,1024]{1,0:T(8,128)(2,1)S(1)}, u32[]{:S(2)}, u32[]{:S(2)}) collective-permute-start(bf16[6,1024]{1,0:T(8,128)(2,1)S(1)} %get-tuple-element.30), channel_id=1, source_target_pairs={{0,1},{1,0},{2,3},{3,2},{4,5},{5,4},{6,7},{7,6},{8,9},{9,8},{10,11... | collective-permute-start | bytes 36872 | tf_op jit(solution)/shard_map/ppermute | solution.py:19
  168.1 1.1 collective-permute-done.7
  (82 shorter events, 10.2 us)
Async XLA Ops:
  6.5 1.6 copy-start
  6.5 8.2 %copy-start.1 = (bf16[128,2048]{1,0:T(8,128)(2,1)S(1)}, bf16[128,2048]{1,0:T(8,128)(2,1)}, u32[]{:S(2)}) copy-start(bf16[128,2048]{1,0:T(8,128)(2,1)} %param.20) | copy-start | bytes 1572868
  6.5 80.0 %all-gather.3.cloned.1.call-start = ((), (), s32[]{:S(2)}) async-start(), calls=%async_computation | async-start | bytes 2228224 | tf_op jit(solution)/shard_map/all_gather | solution.py:108
  7.3 156.1 %all-gather.5.cloned.1.call-start = ((), (), s32[]{:S(2)}) async-start(), calls=%async_computation.1 | async-start | bytes 4456448 | tf_op jit(solution)/shard_map/all_gather | solution.py:107
  8.2 9.2 %copy-start.5 = (s32[8]{0:T(128)S(1)}, s32[8]{0:T(128)}, u32[]{:S(2)}) copy-start(s32[8]{0:T(128)} %param.15) | copy-start | bytes 100
  8.2 9.3 %copy-start.6 = (s32[4]{0:T(128)S(1)}, s32[4]{0:T(128)}, u32[]{:S(2)}) copy-start(s32[4]{0:T(128)} %param.16) | copy-start | bytes 52
  9.7 9.3 %collective-permute-start = (bf16[6,16,576]{2,0,1:T(8,128)(2,1)S(1)}, bf16[6,16,576]{2,0,1:T(8,128)(2,1)S(1)}, u32[]{:S(2)}, u32[]{:S(2)}) collective-permute-start(bf16[6,16,576]{2,0,1:T(8,128)(2,1)S(1)} %pad_maximum_fusion.6), channel_id=1, source_target_pairs={{0,4},{4,0},{1,5},{5,1},{2,6},{6,2},{3,7},{7,3},{8,12},{12,8},{9,1... | collective-permute-start | bytes 331784 | tf_op jit(solution)/shard_map/ppermute | solution.py:19
  17.2 15.6 %copy-start.2 = (s32[8]{0:T(128)S(1)}, s32[8]{0:T(128)}, u32[]{:S(2)}) copy-start(s32[8]{0:T(128)} %constant.93) | copy-start | bytes 100
  19.2 10.5 %collective-permute-start.1 = (bf16[12,16,576]{2,0,1:T(8,128)(2,1)S(1)}, bf16[12,16,576]{2,0,1:T(8,128)(2,1)S(1)}, u32[]{:S(2)}, u32[]{:S(2)}) collective-permute-start(bf16[12,16,576]{2,0,1:T(8,128)(2,1)S(1)} %pad_maximum_fusion.4), channel_id=1, source_target_pairs={{0,2},{2,0},{1,3},{3,1},{4,6},{6,4},{5,7},{7,5},{8,10},{10,8},{9,1... | collective-permute-start | bytes 663560 | tf_op jit(solution)/shard_map/ppermute | solution.py:19
  30.8 4.0 %collective-permute-start.2 = (bf16[24,16,576]{2,0,1:T(8,128)(2,1)}, bf16[24,16,576]{2,0,1:T(8,128)(2,1)S(1)}, u32[]{:S(2)}, u32[]{:S(2)}) collective-permute-start(bf16[24,16,576]{2,0,1:T(8,128)(2,1)} %pad_maximum_fusion.3), channel_id=1, source_target_pairs={{0,1},{1,0},{2,3},{3,2},{4,5},{5,4},{6,7},{7,6},{8,9},{9,8},{10,11... | collective-permute-start | bytes 1327112 | tf_op jit(solution)/shard_map/ppermute | solution.py:19
  33.5 1.6 copy-start.3
  33.6 1.6 copy-start.4
  38.5 3.7 %collective-permute-start.3 = (bf16[24,17,512]{2,0,1:T(8,128)(2,1)S(1)}, bf16[24,17,512]{2,0,1:T(8,128)(2,1)S(1)}, u32[]{:S(2)}, u32[]{:S(2)}) collective-permute-start(bf16[24,17,512]{2,0,1:T(8,128)(2,1)S(1)} %copy.89), channel_id=1, source_target_pairs={{0,1},{1,0},{2,3},{3,2},{4,5},{5,4},{6,7},{7,6},{8,9},{9,8},{10,11... | collective-permute-start | bytes 1253384 | tf_op jit(solution)/shard_map/ppermute | solution.py:19
  42.8 10.9 %collective-permute-start.4 = (bf16[12,17,512]{2,1,0:T(8,128)(2,1)S(1)}, bf16[12,17,512]{2,1,0:T(8,128)(2,1)S(1)}, u32[]{:S(2)}, u32[]{:S(2)}) collective-permute-start(bf16[12,17,512]{2,1,0:T(8,128)(2,1)S(1)} %pad_maximum_fusion.5), channel_id=1, source_target_pairs={{0,2},{2,0},{1,3},{3,1},{4,6},{6,4},{5,7},{7,5},{8,10},{10,8},{9,1... | collective-permute-start | bytes 626696 | tf_op jit(solution)/shard_map/ppermute | solution.py:19
  54.2 8.5 %collective-permute-start.5 = (bf16[6,17,512]{2,1,0:T(8,128)(2,1)S(1)}, bf16[6,17,512]{2,1,0:T(8,128)(2,1)S(1)}, u32[]{:S(2)}, u32[]{:S(2)}) collective-permute-start(bf16[6,17,512]{2,1,0:T(8,128)(2,1)S(1)} %pad_maximum_fusion.7), channel_id=1, source_target_pairs={{0,4},{4,0},{1,5},{5,1},{2,6},{6,2},{3,7},{7,3},{8,12},{12,8},{9,1... | collective-permute-start | bytes 313352 | tf_op jit(solution)/shard_map/ppermute | solution.py:19
  88.5 3.1 %collective-permute-start.6 = (bf16[6,2048]{1,0:T(8,128)(2,1)S(1)}, bf16[6,2048]{1,0:T(8,128)(2,1)S(1)}, u32[]{:S(2)}, u32[]{:S(2)}) collective-permute-start(bf16[6,2048]{1,0:T(8,128)(2,1)S(1)} %fusion.4), channel_id=1, source_target_pairs={{0,1},{1,0},{2,3},{3,2},{4,5},{5,4},{6,7},{7,6},{8,9},{9,8},{10,11... | collective-permute-start | bytes 73736 | tf_op jit(solution)/shard_map/ppermute | solution.py:19
  166.2 3.1 %collective-permute-start.7 = (bf16[6,1024]{1,0:T(8,128)(2,1)S(1)}, bf16[6,1024]{1,0:T(8,128)(2,1)S(1)}, u32[]{:S(2)}, u32[]{:S(2)}) collective-permute-start(bf16[6,1024]{1,0:T(8,128)(2,1)S(1)} %get-tuple-element.30), channel_id=1, source_target_pairs={{0,1},{1,0},{2,3},{3,2},{4,5},{5,4},{6,7},{7,6},{8,9},{9,8},{10,11... | collective-permute-start | bytes 36872 | tf_op jit(solution)/shard_map/ppermute | solution.py:19
Sparse Core Ops, SparseCore 0:
  9.4 77.0 all-gather.2
  88.6 74.6 all-gather.4

commit v3 on v1

--- a/solution.py
+++ b/solution.py
@@ -102,12 +102,13 @@
     local_rank = position % per_request
     local_request = position // per_request
     score_scale = 1.0 / math.sqrt(nope_width + rope_width)
-    nope_rows = q_nope.reshape(token_count, head_count, nope_width)
-    rope_rows = q_rope.reshape(token_count, head_count, rope_width)
+    raw_rows = jnp.concatenate([q_nope, q_rope], axis=1)
+    for bit_level in reversed(range(doublings)):
+        partner = from_partner(raw_rows, "ep", bit_level)
+        raw_rows = append_partner(raw_rows, partner, position, bit_level)
+    nope_rows = raw_rows[:, : q_nope.shape[1]].reshape(TREE, head_count, nope_width)
+    rope_rows = raw_rows[:, q_nope.shape[1] :].reshape(TREE, head_count, rope_width)
     queries = jnp.concatenate([absorb(nope_rows, w_key), rope_rows], axis=2)
-    for bit_level in reversed(range(doublings)):
-        partner = from_partner(queries, "ep", bit_level)
-        queries = append_partner(queries, partner, position, bit_level)
     cached = cache_pool.reshape(-1, cache_pool.shape[2])
     page_count, page_rows = cache_pool.shape[0], cache_pool.shape[1]
     pos_count = cached.shape[0]
@@ -163,7 +164,7 @@
     merged_sum, merged_high, merged_total = state
     merged = merged_sum / merged_total[..., None]
     spread = lax.all_to_all(
-        merged.astype(jnp.bfloat16), "grp", split_axis=1, concat_axis=0, tiled=True
+        jnp.swapaxes(merged.astype(jnp.bfloat16), 0, 1), "grp", split_axis=0, concat_axis=0, tiled=True
     )
     spread = spread.reshape(grp_size, token_count, latent_width)[jnp.array(bit_reversed(grp_size))]
     head_rows = jnp.dot(

time: 132 us -> 126 us (0.955)
  starting transfers between devices: 49.7 us -> 45.6 us
  waiting for transfers between devices: 64.4 us -> 62.4 us
    ppermute x10, starting transfers between devices: 34.5 us -> 30.4 us  [from_partner(): return lax.ppermute(block, axis, route)]
    ppermute x10, waiting for transfers between devices: 51 us -> 48.9 us  [from_partner(): return lax.ppermute(block, axis, route)]
  transfers between devices with their start and end apart: 11 -> 11, of which waited for: 11 -> 10; matrix products, arithmetic and copies ran while one was open for 3% -> 5% of each run, Pallas kernels for 0% -> 0%
where the time goes in v3:
time: 126 us
  waiting for transfers between devices  62.4 us (50%)
  starting transfers between devices  45.6 us (36%)
  local copies, waits for them, and re-layouts  6.22 us (5%)
  other arithmetic  5.58 us (4%)
  matrix products  5.14 us (4%)
    ppermute x10, waiting for transfers between devices, from_partner(): return lax.ppermute(block, axis, route)  48.9 us
    ppermute x10, starting transfers between devices, from_partner(): return lax.ppermute(block, axis, route)  30.4 us
    all_to_all x1, starting transfers between devices, per_device(): lax.all_to_all(jnp.swapaxes(merged.astype(jnp.bfloat16), 0, 1), 'grp', sp...  15.2 us
    all_to_all x1, waiting for transfers between devices, per_device(): lax.all_to_all(jnp.swapaxes(merged.astype(jnp.bfloat16), 0, 1), 'grp', sp...  13.4 us
  transfers between devices with their start and end apart: 11, of which 10 were waited for; matrix products, arithmetic and copies ran while one was open for 5% of the time, Pallas kernels for 0%

profile of v3, /device:TPU:6, one launch (start us, length us, event | category | flops | bytes accessed | tf_op | source)
XLA Modules:
  0.0 125.5 jit_solution(3766914270828643726)
XLA Ops:
  1.6 5.1 %collective-permute-start = (bf16[6,3072]{1,0:T(8,128)(2,1)S(1)}, bf16[6,3072]{1,0:T(8,128)(2,1)S(1)}, u32[]{:S(2)}, u32[]{:S(2)}) collective-permute-start(bf16[6,3072]{1,0:T(8,128)(2,1)S(1)} %constant_dynamic-update-slice_fusion), channel_id=1, source_target_pairs={{0,4},{4,0},{1,5},{5,1},{2,6},{6,2},{3,7},{7,3},{8,12},{12,8},{9,1... | collective-permute-start | bytes 110600 | tf_op jit(solution)/shard_map/ppermute | solution.py:19
  6.8 1.2 dynamic_slice.11
  11.5 2.6 %collective-permute-start.1 = (bf16[12,3072]{1,0:T(8,128)(2,1)S(1)}, bf16[12,3072]{1,0:T(8,128)(2,1)S(1)}, u32[]{:S(2)}, u32[]{:S(2)}) collective-permute-start(bf16[12,3072]{1,0:T(8,128)(2,1)S(1)} %pad_maximum_fusion.7), channel_id=1, source_target_pairs={{0,2},{2,0},{1,3},{3,1},{4,6},{6,4},{5,7},{7,5},{8,10},{10,8},{9,1... | collective-permute-start | bytes 221192 | tf_op jit(solution)/shard_map/ppermute | solution.py:19
  15.4 2.7 %collective-permute-done.1 = bf16[12,3072]{1,0:T(8,128)(2,1)S(1)} collective-permute-done((bf16[12,3072]{1,0:T(8,128)(2,1)S(1)}, bf16[12,3072]{1,0:T(8,128)(2,1)S(1)}, u32[]{:S(2)}, u32[]{:S(2)}) %collective-permute-start.1) | collective-permute-done | bytes 73760 | tf_op jit(solution)/shard_map/ppermute | solution.py:19
  18.1 1.9 %collective-permute-start.2 = (bf16[24,3072]{1,0:T(8,128)(2,1)S(1)}, bf16[24,3072]{1,0:T(8,128)(2,1)S(1)}, u32[]{:S(2)}, u32[]{:S(2)}) collective-permute-start(bf16[24,3072]{1,0:T(8,128)(2,1)S(1)} %pad_maximum_fusion.4), channel_id=1, source_target_pairs={{0,1},{1,0},{2,3},{3,2},{4,5},{5,4},{6,7},{7,6},{8,9},{9,8},{10,11... | collective-permute-start | bytes 442376 | tf_op jit(solution)/shard_map/ppermute | solution.py:19
  20.1 1.3 %collective-permute-done.2 = bf16[24,3072]{1,0:T(8,128)(2,1)S(1)} collective-permute-done((bf16[24,3072]{1,0:T(8,128)(2,1)S(1)}, bf16[24,3072]{1,0:T(8,128)(2,1)S(1)}, u32[]{:S(2)}, u32[]{:S(2)}) %collective-permute-start.2) | collective-permute-done | bytes 147488 | tf_op jit(solution)/shard_map/ppermute | solution.py:19
  22.8 1.1 fusion
  26.2 2.0 %collective-permute-start.3 = (bf16[24,17,512]{2,0,1:T(8,128)(2,1)S(1)}, bf16[24,17,512]{2,0,1:T(8,128)(2,1)S(1)}, u32[]{:S(2)}, u32[]{:S(2)}) collective-permute-start(bf16[24,17,512]{2,0,1:T(8,128)(2,1)S(1)} %copy.96), channel_id=1, source_target_pairs={{0,1},{1,0},{2,3},{3,2},{4,5},{5,4},{6,7},{7,6},{8,9},{9,8},{10,11... | collective-permute-start | bytes 1253384 | tf_op jit(solution)/shard_map/ppermute | solution.py:19
  28.2 1.6 %collective-permute-done.3 = bf16[24,17,512]{2,0,1:T(8,128)(2,1)S(1)} collective-permute-done((bf16[24,17,512]{2,0,1:T(8,128)(2,1)S(1)}, bf16[24,17,512]{2,0,1:T(8,128)(2,1)S(1)}, u32[]{:S(2)}, u32[]{:S(2)}) %collective-permute-start.3) | collective-permute-done | bytes 417824 | tf_op jit(solution)/shard_map/ppermute | solution.py:19
  30.5 2.7 %collective-permute-start.4 = (bf16[12,17,512]{2,1,0:T(8,128)(2,1)S(1)}, bf16[12,17,512]{2,1,0:T(8,128)(2,1)S(1)}, u32[]{:S(2)}, u32[]{:S(2)}) collective-permute-start(bf16[12,17,512]{2,1,0:T(8,128)(2,1)S(1)} %pad_maximum_fusion.3), channel_id=1, source_target_pairs={{0,2},{2,0},{1,3},{3,1},{4,6},{6,4},{5,7},{7,5},{8,10},{10,8},{9,1... | collective-permute-start | bytes 626696 | tf_op jit(solution)/shard_map/ppermute | solution.py:19
  33.2 8.4 %collective-permute-done.4 = bf16[12,17,512]{2,1,0:T(8,128)(2,1)S(1)} collective-permute-done((bf16[12,17,512]{2,1,0:T(8,128)(2,1)S(1)}, bf16[12,17,512]{2,1,0:T(8,128)(2,1)S(1)}, u32[]{:S(2)}, u32[]{:S(2)}) %collective-permute-start.4) | collective-permute-done | bytes 208928 | tf_op jit(solution)/shard_map/ppermute | solution.py:19
  42.0 2.8 %collective-permute-start.5 = (bf16[6,17,512]{2,1,0:T(8,128)(2,1)S(1)}, bf16[6,17,512]{2,1,0:T(8,128)(2,1)S(1)}, u32[]{:S(2)}, u32[]{:S(2)}) collective-permute-start(bf16[6,17,512]{2,1,0:T(8,128)(2,1)S(1)} %pad_maximum_fusion.5), channel_id=1, source_target_pairs={{0,4},{4,0},{1,5},{5,1},{2,6},{6,2},{3,7},{7,3},{8,12},{12,8},{9,1... | collective-permute-start | bytes 313352 | tf_op jit(solution)/shard_map/ppermute | solution.py:19
  44.8 5.8 %collective-permute-done.5 = bf16[6,17,512]{2,1,0:T(8,128)(2,1)S(1)} collective-permute-done((bf16[6,17,512]{2,1,0:T(8,128)(2,1)S(1)}, bf16[6,17,512]{2,1,0:T(8,128)(2,1)S(1)}, u32[]{:S(2)}, u32[]{:S(2)}) %collective-permute-start.5) | collective-permute-done | bytes 104480 | tf_op jit(solution)/shard_map/ppermute | solution.py:19
  51.5 15.2 %all-to-all-start = ((bf16[16,6,512]{2,1,0:T(8,128)(2,1)}), bf16[16,6,512]{2,1,0:T(8,128)(2,1)S(1)}, u32[]{:S(2)}, u32[]{:S(2)}) async-start(bf16[16,6,512]{2,1,0:T(8,128)(2,1)} %copy.101), calls=%async_computation | async-start | bytes 262144 | tf_op jit(solution)/shard_map/all_to_all | solution.py:166
  66.7 13.4 %all-to-all-done = bf16[16,6,512]{2,1,0:T(8,128)(2,1)S(1)} async-done(((bf16[16,6,512]{2,1,0:T(8,128)(2,1)}), bf16[16,6,512]{2,1,0:T(8,128)(2,1)S(1)}, u32[]{:S(2)}, u32[]{:S(2)}) %all-to-all-start) | async-done | bytes 98336 | tf_op jit(solution)/shard_map/all_to_all | solution.py:166
  80.8 1.3 %fusion.4 = f32[96,2048]{1,0:T(8,128)S(1)} fusion(bf16[128,2048]{1,0:T(8,128)(2,1)S(1)} %copy-done.1, bf16[96,512]{1,0:T(8,128)(2,1)S(1)} %reshape.66, bf16[1,512,128]{2,1,0:T(8,128)(2,1)} %param.20), kind=kOutput, calls=%fused_computation.15 | convolution fusion | flops 62926848 | bytes 1540096 | tf_op jit(solution)/shard_map/dot_general | solution.py:175
  82.1 2.9 %collective-permute-start.6 = (bf16[48,2048]{1,0:T(8,128)(2,1)S(1)}, bf16[48,2048]{1,0:T(8,128)(2,1)S(1)}, u32[]{:S(2)}, u32[]{:S(2)}) collective-permute-start(bf16[48,2048]{1,0:T(8,128)(2,1)S(1)} %select_convert_fusion.1), channel_id=1, source_target_pairs={{0,32},{32,0},{64,96},{96,64},{128,160},{160,128},{192,224},{224,1... | collective-permute-start | bytes 589832 | tf_op jit(solution)/shard_map/ppermute | solution.py:19
  85.0 4.6 %collective-permute-done.6 = bf16[48,2048]{1,0:T(8,128)(2,1)S(1)} collective-permute-done((bf16[48,2048]{1,0:T(8,128)(2,1)S(1)}, bf16[48,2048]{1,0:T(8,128)(2,1)S(1)}, u32[]{:S(2)}, u32[]{:S(2)}) %collective-permute-start.6) | collective-permute-done | bytes 196640 | tf_op jit(solution)/shard_map/ppermute | solution.py:19
  89.8 3.2 %collective-permute-start.7 = (bf16[24,2048]{1,0:T(8,128)(2,1)S(1)}, bf16[24,2048]{1,0:T(8,128)(2,1)S(1)}, u32[]{:S(2)}, u32[]{:S(2)}) collective-permute-start(bf16[24,2048]{1,0:T(8,128)(2,1)S(1)} %select_convert_fusion.3), channel_id=1, source_target_pairs={{0,64},{64,0},{32,96},{96,32},{128,192},{192,128},{160,224},{224,1... | collective-permute-start | bytes 294920 | tf_op jit(solution)/shard_map/ppermute | solution.py:19
  93.0 5.2 %collective-permute-done.7 = bf16[24,2048]{1,0:T(8,128)(2,1)S(1)} collective-permute-done((bf16[24,2048]{1,0:T(8,128)(2,1)S(1)}, bf16[24,2048]{1,0:T(8,128)(2,1)S(1)}, u32[]{:S(2)}, u32[]{:S(2)}) %collective-permute-start.7) | collective-permute-done | bytes 98336 | tf_op jit(solution)/shard_map/ppermute | solution.py:19
  98.3 3.5 %collective-permute-start.8 = (bf16[12,2048]{1,0:T(8,128)(2,1)S(1)}, bf16[12,2048]{1,0:T(8,128)(2,1)S(1)}, u32[]{:S(2)}, u32[]{:S(2)}) collective-permute-start(bf16[12,2048]{1,0:T(8,128)(2,1)S(1)} %select_convert_fusion.5), channel_id=1, source_target_pairs={{0,128},{128,0},{32,160},{160,32},{64,192},{192,64},{96,224},{224,... | collective-permute-start | bytes 147464 | tf_op jit(solution)/shard_map/ppermute | solution.py:19
  101.8 8.2 %collective-permute-done.8 = bf16[12,2048]{1,0:T(8,128)(2,1)S(1)} collective-permute-done((bf16[12,2048]{1,0:T(8,128)(2,1)S(1)}, bf16[12,2048]{1,0:T(8,128)(2,1)S(1)}, u32[]{:S(2)}, u32[]{:S(2)}) %collective-permute-start.8) | collective-permute-done | bytes 49184 | tf_op jit(solution)/shard_map/ppermute | solution.py:19
  110.0 3.6 %collective-permute-start.9 = (bf16[6,2048]{1,0:T(8,128)(2,1)S(1)}, bf16[6,2048]{1,0:T(8,128)(2,1)S(1)}, u32[]{:S(2)}, u32[]{:S(2)}) collective-permute-start(bf16[6,2048]{1,0:T(8,128)(2,1)S(1)} %select_convert_fusion.6), channel_id=1, source_target_pairs={{0,256},{256,0},{32,288},{288,32},{64,320},{320,64},{96,352},{352,... | collective-permute-start | bytes 73736 | tf_op jit(solution)/shard_map/ppermute | solution.py:19
  113.7 11.2 %collective-permute-done.9 = bf16[6,2048]{1,0:T(8,128)(2,1)S(1)} collective-permute-done((bf16[6,2048]{1,0:T(8,128)(2,1)S(1)}, bf16[6,2048]{1,0:T(8,128)(2,1)S(1)}, u32[]{:S(2)}, u32[]{:S(2)}) %collective-permute-start.9) | collective-permute-done | bytes 24608 | tf_op jit(solution)/shard_map/ppermute | solution.py:19
  (87 shorter events, 13.3 us)
Async XLA Ops:
  0.0 21.7 %copy-start = (bf16[16,512,128]{2,1,0:T(8,128)(2,1)S(1)}, bf16[16,512,128]{2,1,0:T(8,128)(2,1)}, u32[]{:S(2)}) copy-start(bf16[16,512,128]{2,1,0:T(8,128)(2,1)} %param.19) | copy-start | bytes 6291460
  1.6 9.8 %collective-permute-start = (bf16[6,3072]{1,0:T(8,128)(2,1)S(1)}, bf16[6,3072]{1,0:T(8,128)(2,1)S(1)}, u32[]{:S(2)}, u32[]{:S(2)}) collective-permute-start(bf16[6,3072]{1,0:T(8,128)(2,1)S(1)} %constant_dynamic-update-slice_fusion), channel_id=1, source_target_pairs={{0,4},{4,0},{1,5},{5,1},{2,6},{6,2},{3,7},{7,3},{8,12},{12,8},{9,1... | collective-permute-start | bytes 110600 | tf_op jit(solution)/shard_map/ppermute | solution.py:19
  11.5 6.5 %collective-permute-start.1 = (bf16[12,3072]{1,0:T(8,128)(2,1)S(1)}, bf16[12,3072]{1,0:T(8,128)(2,1)S(1)}, u32[]{:S(2)}, u32[]{:S(2)}) collective-permute-start(bf16[12,3072]{1,0:T(8,128)(2,1)S(1)} %pad_maximum_fusion.7), channel_id=1, source_target_pairs={{0,2},{2,0},{1,3},{3,1},{4,6},{6,4},{5,7},{7,5},{8,10},{10,8},{9,1... | collective-permute-start | bytes 221192 | tf_op jit(solution)/shard_map/ppermute | solution.py:19
  18.1 3.3 %collective-permute-start.2 = (bf16[24,3072]{1,0:T(8,128)(2,1)S(1)}, bf16[24,3072]{1,0:T(8,128)(2,1)S(1)}, u32[]{:S(2)}, u32[]{:S(2)}) collective-permute-start(bf16[24,3072]{1,0:T(8,128)(2,1)S(1)} %pad_maximum_fusion.4), channel_id=1, source_target_pairs={{0,1},{1,0},{2,3},{3,2},{4,5},{5,4},{6,7},{7,6},{8,9},{9,8},{10,11... | collective-permute-start | bytes 442376 | tf_op jit(solution)/shard_map/ppermute | solution.py:19
  21.7 1.1 copy-start.3
  21.7 1.1 copy-start.4
  26.2 3.7 %collective-permute-start.3 = (bf16[24,17,512]{2,0,1:T(8,128)(2,1)S(1)}, bf16[24,17,512]{2,0,1:T(8,128)(2,1)S(1)}, u32[]{:S(2)}, u32[]{:S(2)}) collective-permute-start(bf16[24,17,512]{2,0,1:T(8,128)(2,1)S(1)} %copy.96), channel_id=1, source_target_pairs={{0,1},{1,0},{2,3},{3,2},{4,5},{5,4},{6,7},{7,6},{8,9},{9,8},{10,11... | collective-permute-start | bytes 1253384 | tf_op jit(solution)/shard_map/ppermute | solution.py:19
  30.4 36.3 %copy-start.2 = (s32[16]{0:T(128)S(1)}, s32[16]{0:T(128)}, u32[]{:S(2)}) copy-start(s32[16]{0:T(128)} %constant.106) | copy-start | bytes 196
  30.5 50.3 %copy-start.1 = (bf16[128,2048]{1,0:T(8,128)(2,1)S(1)}, bf16[128,2048]{1,0:T(8,128)(2,1)}, u32[]{:S(2)}) copy-start(bf16[128,2048]{1,0:T(8,128)(2,1)} %param.21) | copy-start | bytes 1572868
  30.5 11.1 %collective-permute-start.4 = (bf16[12,17,512]{2,1,0:T(8,128)(2,1)S(1)}, bf16[12,17,512]{2,1,0:T(8,128)(2,1)S(1)}, u32[]{:S(2)}, u32[]{:S(2)}) collective-permute-start(bf16[12,17,512]{2,1,0:T(8,128)(2,1)S(1)} %pad_maximum_fusion.3), channel_id=1, source_target_pairs={{0,2},{2,0},{1,3},{3,1},{4,6},{6,4},{5,7},{7,5},{8,10},{10,8},{9,1... | collective-permute-start | bytes 626696 | tf_op jit(solution)/shard_map/ppermute | solution.py:19
  42.0 8.5 %collective-permute-start.5 = (bf16[6,17,512]{2,1,0:T(8,128)(2,1)S(1)}, bf16[6,17,512]{2,1,0:T(8,128)(2,1)S(1)}, u32[]{:S(2)}, u32[]{:S(2)}) collective-permute-start(bf16[6,17,512]{2,1,0:T(8,128)(2,1)S(1)} %pad_maximum_fusion.5), channel_id=1, source_target_pairs={{0,4},{4,0},{1,5},{5,1},{2,6},{6,2},{3,7},{7,3},{8,12},{12,8},{9,1... | collective-permute-start | bytes 313352 | tf_op jit(solution)/shard_map/ppermute | solution.py:19
  51.5 28.6 %all-to-all-start = ((bf16[16,6,512]{2,1,0:T(8,128)(2,1)}), bf16[16,6,512]{2,1,0:T(8,128)(2,1)S(1)}, u32[]{:S(2)}, u32[]{:S(2)}) async-start(bf16[16,6,512]{2,1,0:T(8,128)(2,1)} %copy.101), calls=%async_computation | async-start | bytes 262144 | tf_op jit(solution)/shard_map/all_to_all | solution.py:166
  82.1 7.6 %collective-permute-start.6 = (bf16[48,2048]{1,0:T(8,128)(2,1)S(1)}, bf16[48,2048]{1,0:T(8,128)(2,1)S(1)}, u32[]{:S(2)}, u32[]{:S(2)}) collective-permute-start(bf16[48,2048]{1,0:T(8,128)(2,1)S(1)} %select_convert_fusion.1), channel_id=1, source_target_pairs={{0,32},{32,0},{64,96},{96,64},{128,160},{160,128},{192,224},{224,1... | collective-permute-start | bytes 589832 | tf_op jit(solution)/shard_map/ppermute | solution.py:19
  89.8 8.5 %collective-permute-start.7 = (bf16[24,2048]{1,0:T(8,128)(2,1)S(1)}, bf16[24,2048]{1,0:T(8,128)(2,1)S(1)}, u32[]{:S(2)}, u32[]{:S(2)}) collective-permute-start(bf16[24,2048]{1,0:T(8,128)(2,1)S(1)} %select_convert_fusion.3), channel_id=1, source_target_pairs={{0,64},{64,0},{32,96},{96,32},{128,192},{192,128},{160,224},{224,1... | collective-permute-start | bytes 294920 | tf_op jit(solution)/shard_map/ppermute | solution.py:19
  98.3 11.7 %collective-permute-start.8 = (bf16[12,2048]{1,0:T(8,128)(2,1)S(1)}, bf16[12,2048]{1,0:T(8,128)(2,1)S(1)}, u32[]{:S(2)}, u32[]{:S(2)}) collective-permute-start(bf16[12,2048]{1,0:T(8,128)(2,1)S(1)} %select_convert_fusion.5), channel_id=1, source_target_pairs={{0,128},{128,0},{32,160},{160,32},{64,192},{192,64},{96,224},{224,... | collective-permute-start | bytes 147464 | tf_op jit(solution)/shard_map/ppermute | solution.py:19
  110.0 14.9 %collective-permute-start.9 = (bf16[6,2048]{1,0:T(8,128)(2,1)S(1)}, bf16[6,2048]{1,0:T(8,128)(2,1)S(1)}, u32[]{:S(2)}, u32[]{:S(2)}) collective-permute-start(bf16[6,2048]{1,0:T(8,128)(2,1)S(1)} %select_convert_fusion.6), channel_id=1, source_target_pairs={{0,256},{256,0},{32,288},{288,32},{64,320},{320,64},{96,352},{352,... | collective-permute-start | bytes 73736 | tf_op jit(solution)/shard_map/ppermute | solution.py:19

commit v4 on v3

--- a/solution.py
+++ b/solution.py
@@ -16,6 +16,12 @@
         high = low | 1 << bit
         if high != low and high < count:
             route += [(low, high), (high, low)]
+    return lax.ppermute(block, axis, route)
+
+
+def shifted(block, axis, group, shift):
+    count = lax.axis_size(axis)
+    route = [(i, (i // group) * group + (i % group + shift) % group) for i in range(count)]
     return lax.ppermute(block, axis, route)
 
 
@@ -174,7 +180,7 @@
     ).astype(jnp.bfloat16)
     rows_out = jnp.dot(head_rows, out_weight, preferred_element_type=jnp.float32)
     group = lax.axis_index("grp")
-    for bit_level in range(grp_size.bit_length() - 1):
+    for bit_level in range(2):
         half_rows = rows_out.shape[0] // 2
         upper_side = jnp.right_shift(group, bit_level) & 1 == 1
         lower, upper = rows_out[:half_rows], rows_out[half_rows:]
@@ -183,7 +189,20 @@
         rows_out = kept + from_partner(sent.astype(jnp.bfloat16), "grp", bit_level).astype(
             jnp.float32
         )
-    return rows_out.astype(jnp.bfloat16)
+    ring = grp_size // 4
+    blocks = rows_out.reshape(ring, token_count, rows_out.shape[1])
+    mine = group // 4
+
+    def block_for(member):
+        return lax.dynamic_index_in_dim(
+            blocks, (member & 1) * 2 + member // 2, 0, keepdims=False
+        )
+
+    total_rows = block_for(mine)
+    for step in range(1, ring):
+        sent = block_for((mine + step) % ring).astype(jnp.bfloat16)
+        total_rows = total_rows + shifted(sent, "grp", grp_size, 4 * step).astype(jnp.float32)
+    return total_rows.astype(jnp.bfloat16)
 
 
 def solution(mesh):

time: 126 us -> 125 us (level)
  waiting for transfers between devices: 62.4 us -> 54.1 us
  starting transfers between devices: 45.6 us -> 52.4 us
    ppermute x10 -> x8, waiting for transfers between devices: 48.9 us -> 29.4 us  [from_partner(): return lax.ppermute(block, axis, route)]
    ppermute x0 -> x3, starting transfers between devices: none -> 14 us  [shifted(): return lax.ppermute(block, axis, route)]
    ppermute x0 -> x3, waiting for transfers between devices: none -> 11.3 us  [shifted(): return lax.ppermute(block, axis, route)]
    ppermute x10 -> x8, starting transfers between devices: 30.4 us -> 23.3 us  [from_partner(): return lax.ppermute(block, axis, route)]
  transfers between devices with their start and end apart: 11 -> 12, of which waited for: 10 -> 9; matrix products, arithmetic and copies ran while one was open for 5% -> 5% of each run, Pallas kernels for 0% -> 0%
where the time goes in v4:
time: 125 us; the launch traced here: 124 us
  waiting for transfers between devices  54.1 us (43%)
  starting transfers between devices  52.4 us (42%)
  local copies, waits for them, and re-layouts  6.25 us (5%)
  other arithmetic  5.52 us (4%)
  matrix products  5.15 us (4%)
    ppermute x8, waiting for transfers between devices, from_partner(): return lax.ppermute(block, axis, route)  29.4 us
    ppermute x8, starting transfers between devices, from_partner(): return lax.ppermute(block, axis, route)  23.3 us
    all_to_all x1, starting transfers between devices, per_device(): lax.all_to_all(jnp.swapaxes(merged.astype(jnp.bfloat16), 0, 1), 'grp', sp...  15.2 us
    ppermute x3, starting transfers between devices, shifted(): return lax.ppermute(block, axis, route)  14 us
    all_to_all x1, waiting for transfers between devices, per_device(): lax.all_to_all(jnp.swapaxes(merged.astype(jnp.bfloat16), 0, 1), 'grp', sp...  13.4 us
    ppermute x3, waiting for transfers between devices, shifted(): return lax.ppermute(block, axis, route)  11.3 us
  transfers between devices with their start and end apart: 12, of which 9 were waited for; matrix products, arithmetic and copies ran while one was open for 5% of the time, Pallas kernels for 0%

profile of v4, /device:TPU:6, one launch (start us, length us, event | category | flops | bytes accessed | tf_op | source)
XLA Modules:
  0.0 124.3 jit_solution(10044783498399540569)
XLA Ops:
  1.6 5.1 %collective-permute-start = (bf16[6,3072]{1,0:T(8,128)(2,1)S(1)}, bf16[6,3072]{1,0:T(8,128)(2,1)S(1)}, u32[]{:S(2)}, u32[]{:S(2)}) collective-permute-start(bf16[6,3072]{1,0:T(8,128)(2,1)S(1)} %constant_dynamic-update-slice_fusion), channel_id=1, source_target_pairs={{0,4},{4,0},{1,5},{5,1},{2,6},{6,2},{3,7},{7,3},{8,12},{12,8},{9,1... | collective-permute-start | bytes 110600 | tf_op jit(solution)/shard_map/ppermute | solution.py:19
  6.8 1.2 dynamic_slice.24
  11.5 2.6 %collective-permute-start.1 = (bf16[12,3072]{1,0:T(8,128)(2,1)S(1)}, bf16[12,3072]{1,0:T(8,128)(2,1)S(1)}, u32[]{:S(2)}, u32[]{:S(2)}) collective-permute-start(bf16[12,3072]{1,0:T(8,128)(2,1)S(1)} %pad_maximum_fusion.7), channel_id=1, source_target_pairs={{0,2},{2,0},{1,3},{3,1},{4,6},{6,4},{5,7},{7,5},{8,10},{10,8},{9,1... | collective-permute-start | bytes 221192 | tf_op jit(solution)/shard_map/ppermute | solution.py:19
  15.4 2.7 %collective-permute-done.1 = bf16[12,3072]{1,0:T(8,128)(2,1)S(1)} collective-permute-done((bf16[12,3072]{1,0:T(8,128)(2,1)S(1)}, bf16[12,3072]{1,0:T(8,128)(2,1)S(1)}, u32[]{:S(2)}, u32[]{:S(2)}) %collective-permute-start.1) | collective-permute-done | bytes 73760 | tf_op jit(solution)/shard_map/ppermute | solution.py:19
  18.1 1.9 %collective-permute-start.2 = (bf16[24,3072]{1,0:T(8,128)(2,1)S(1)}, bf16[24,3072]{1,0:T(8,128)(2,1)S(1)}, u32[]{:S(2)}, u32[]{:S(2)}) collective-permute-start(bf16[24,3072]{1,0:T(8,128)(2,1)S(1)} %pad_maximum_fusion.4), channel_id=1, source_target_pairs={{0,1},{1,0},{2,3},{3,2},{4,5},{5,4},{6,7},{7,6},{8,9},{9,8},{10,11... | collective-permute-start | bytes 442376 | tf_op jit(solution)/shard_map/ppermute | solution.py:19
  20.1 1.3 %collective-permute-done.2 = bf16[24,3072]{1,0:T(8,128)(2,1)S(1)} collective-permute-done((bf16[24,3072]{1,0:T(8,128)(2,1)S(1)}, bf16[24,3072]{1,0:T(8,128)(2,1)S(1)}, u32[]{:S(2)}, u32[]{:S(2)}) %collective-permute-start.2) | collective-permute-done | bytes 147488 | tf_op jit(solution)/shard_map/ppermute | solution.py:19
  22.8 1.1 fusion
  26.2 2.0 %collective-permute-start.3 = (bf16[24,17,512]{2,0,1:T(8,128)(2,1)S(1)}, bf16[24,17,512]{2,0,1:T(8,128)(2,1)S(1)}, u32[]{:S(2)}, u32[]{:S(2)}) collective-permute-start(bf16[24,17,512]{2,0,1:T(8,128)(2,1)S(1)} %copy.96), channel_id=1, source_target_pairs={{0,1},{1,0},{2,3},{3,2},{4,5},{5,4},{6,7},{7,6},{8,9},{9,8},{10,11... | collective-permute-start | bytes 1253384 | tf_op jit(solution)/shard_map/ppermute | solution.py:19
  28.2 1.6 %collective-permute-done.3 = bf16[24,17,512]{2,0,1:T(8,128)(2,1)S(1)} collective-permute-done((bf16[24,17,512]{2,0,1:T(8,128)(2,1)S(1)}, bf16[24,17,512]{2,0,1:T(8,128)(2,1)S(1)}, u32[]{:S(2)}, u32[]{:S(2)}) %collective-permute-start.3) | collective-permute-done | bytes 417824 | tf_op jit(solution)/shard_map/ppermute | solution.py:19
  30.5 2.7 %collective-permute-start.4 = (bf16[12,17,512]{2,1,0:T(8,128)(2,1)S(1)}, bf16[12,17,512]{2,1,0:T(8,128)(2,1)S(1)}, u32[]{:S(2)}, u32[]{:S(2)}) collective-permute-start(bf16[12,17,512]{2,1,0:T(8,128)(2,1)S(1)} %pad_maximum_fusion.3), channel_id=1, source_target_pairs={{0,2},{2,0},{1,3},{3,1},{4,6},{6,4},{5,7},{7,5},{8,10},{10,8},{9,1... | collective-permute-start | bytes 626696 | tf_op jit(solution)/shard_map/ppermute | solution.py:19
  33.2 8.4 %collective-permute-done.4 = bf16[12,17,512]{2,1,0:T(8,128)(2,1)S(1)} collective-permute-done((bf16[12,17,512]{2,1,0:T(8,128)(2,1)S(1)}, bf16[12,17,512]{2,1,0:T(8,128)(2,1)S(1)}, u32[]{:S(2)}, u32[]{:S(2)}) %collective-permute-start.4) | collective-permute-done | bytes 208928 | tf_op jit(solution)/shard_map/ppermute | solution.py:19
  42.0 2.8 %collective-permute-start.5 = (bf16[6,17,512]{2,1,0:T(8,128)(2,1)S(1)}, bf16[6,17,512]{2,1,0:T(8,128)(2,1)S(1)}, u32[]{:S(2)}, u32[]{:S(2)}) collective-permute-start(bf16[6,17,512]{2,1,0:T(8,128)(2,1)S(1)} %pad_maximum_fusion.5), channel_id=1, source_target_pairs={{0,4},{4,0},{1,5},{5,1},{2,6},{6,2},{3,7},{7,3},{8,12},{12,8},{9,1... | collective-permute-start | bytes 313352 | tf_op jit(solution)/shard_map/ppermute | solution.py:19
  44.8 5.8 %collective-permute-done.5 = bf16[6,17,512]{2,1,0:T(8,128)(2,1)S(1)} collective-permute-done((bf16[6,17,512]{2,1,0:T(8,128)(2,1)S(1)}, bf16[6,17,512]{2,1,0:T(8,128)(2,1)S(1)}, u32[]{:S(2)}, u32[]{:S(2)}) %collective-permute-start.5) | collective-permute-done | bytes 104480 | tf_op jit(solution)/shard_map/ppermute | solution.py:19
  51.5 15.2 %all-to-all-start = ((bf16[16,6,512]{2,1,0:T(8,128)(2,1)}), bf16[16,6,512]{2,1,0:T(8,128)(2,1)S(1)}, u32[]{:S(2)}, u32[]{:S(2)}) async-start(bf16[16,6,512]{2,1,0:T(8,128)(2,1)} %copy.101), calls=%async_computation | async-start | bytes 262144 | tf_op jit(solution)/shard_map/all_to_all | solution.py:172
  66.7 13.4 %all-to-all-done = bf16[16,6,512]{2,1,0:T(8,128)(2,1)S(1)} async-done(((bf16[16,6,512]{2,1,0:T(8,128)(2,1)}), bf16[16,6,512]{2,1,0:T(8,128)(2,1)S(1)}, u32[]{:S(2)}, u32[]{:S(2)}) %all-to-all-start) | async-done | bytes 98336 | tf_op jit(solution)/shard_map/all_to_all | solution.py:172
  80.7 1.3 %fusion.4 = f32[96,2048]{1,0:T(8,128)S(1)} fusion(bf16[128,2048]{1,0:T(8,128)(2,1)S(1)} %copy-done.1, bf16[96,512]{1,0:T(8,128)(2,1)S(1)} %reshape.72, bf16[1,512,128]{2,1,0:T(8,128)(2,1)} %param.20), kind=kOutput, calls=%fused_computation.15 | convolution fusion | flops 62926848 | bytes 1540096 | tf_op jit(solution)/shard_map/dot_general | solution.py:181
  82.1 2.9 %collective-permute-start.6 = (bf16[48,2048]{1,0:T(8,128)(2,1)S(1)}, bf16[48,2048]{1,0:T(8,128)(2,1)S(1)}, u32[]{:S(2)}, u32[]{:S(2)}) collective-permute-start(bf16[48,2048]{1,0:T(8,128)(2,1)S(1)} %select_convert_fusion.1), channel_id=1, source_target_pairs={{0,32},{32,0},{64,96},{96,64},{128,160},{160,128},{192,224},{224,1... | collective-permute-start | bytes 589832 | tf_op jit(solution)/shard_map/ppermute | solution.py:19
  85.0 4.6 %collective-permute-done.6 = bf16[48,2048]{1,0:T(8,128)(2,1)S(1)} collective-permute-done((bf16[48,2048]{1,0:T(8,128)(2,1)S(1)}, bf16[48,2048]{1,0:T(8,128)(2,1)S(1)}, u32[]{:S(2)}, u32[]{:S(2)}) %collective-permute-start.6) | collective-permute-done | bytes 196640 | tf_op jit(solution)/shard_map/ppermute | solution.py:19
  89.7 3.2 %collective-permute-start.7 = (bf16[24,2048]{1,0:T(8,128)(2,1)S(1)}, bf16[24,2048]{1,0:T(8,128)(2,1)S(1)}, u32[]{:S(2)}, u32[]{:S(2)}) collective-permute-start(bf16[24,2048]{1,0:T(8,128)(2,1)S(1)} %select_convert_fusion.3), channel_id=1, source_target_pairs={{0,64},{64,0},{32,96},{96,32},{128,192},{192,128},{160,224},{224,1... | collective-permute-start | bytes 294920 | tf_op jit(solution)/shard_map/ppermute | solution.py:19
  93.1 5.1 %collective-permute-done.7 = bf16[24,2048]{1,0:T(8,128)(2,1)S(1)} collective-permute-done((bf16[24,2048]{1,0:T(8,128)(2,1)S(1)}, bf16[24,2048]{1,0:T(8,128)(2,1)S(1)}, u32[]{:S(2)}, u32[]{:S(2)}) %collective-permute-start.7) | collective-permute-done | bytes 98336 | tf_op jit(solution)/shard_map/ppermute | solution.py:19
  98.3 3.5 %collective-permute-start.8 = (bf16[6,2048]{1,0:T(8,128)(2,1)S(1)}, bf16[6,2048]{1,0:T(8,128)(2,1)S(1)}, u32[]{:S(2)}, u32[]{:S(2)}) collective-permute-start(bf16[6,2048]{1,0:T(8,128)(2,1)S(1)} %get-tuple-element.24), channel_id=1, source_target_pairs={{0,128},{32,160},{64,192},{96,224},{128,256},{160,288},{192,320},{... | collective-permute-start | bytes 73736 | tf_op jit(solution)/shard_map/ppermute | solution.py:25
  101.8 6.3 %collective-permute-start.10 = (bf16[6,2048]{1,0:T(8,128)(2,1)S(1)}, bf16[6,2048]{1,0:T(8,128)(2,1)S(1)}, u32[]{:S(2)}, u32[]{:S(2)}) collective-permute-start(bf16[6,2048]{1,0:T(8,128)(2,1)S(1)} %get-tuple-element.25), channel_id=1, source_target_pairs={{0,384},{32,416},{64,448},{96,480},{128,0},{160,32},{192,64},{224,... | collective-permute-start | bytes 73736 | tf_op jit(solution)/shard_map/ppermute | solution.py:25
  108.1 4.2 %collective-permute-start.9 = (bf16[6,2048]{1,0:T(8,128)(2,1)S(1)}, bf16[6,2048]{1,0:T(8,128)(2,1)S(1)}, u32[]{:S(2)}, u32[]{:S(2)}) collective-permute-start(bf16[6,2048]{1,0:T(8,128)(2,1)S(1)} %get-tuple-element.26), channel_id=1, source_target_pairs={{0,256},{32,288},{64,320},{96,352},{128,384},{160,416},{192,448},{... | collective-permute-start | bytes 73736 | tf_op jit(solution)/shard_map/ppermute | solution.py:25
  112.4 11.3 %collective-permute-done.9 = bf16[6,2048]{1,0:T(8,128)(2,1)S(1)} collective-permute-done((bf16[6,2048]{1,0:T(8,128)(2,1)S(1)}, bf16[6,2048]{1,0:T(8,128)(2,1)S(1)}, u32[]{:S(2)}, u32[]{:S(2)}) %collective-permute-start.9) | collective-permute-done | bytes 24608 | tf_op jit(solution)/shard_map/ppermute | solution.py:25
  (88 shorter events, 13.2 us)
Async XLA Ops:
  0.0 21.7 %copy-start = (bf16[16,512,128]{2,1,0:T(8,128)(2,1)S(1)}, bf16[16,512,128]{2,1,0:T(8,128)(2,1)}, u32[]{:S(2)}) copy-start(bf16[16,512,128]{2,1,0:T(8,128)(2,1)} %param.19) | copy-start | bytes 6291460
  1.6 9.8 %collective-permute-start = (bf16[6,3072]{1,0:T(8,128)(2,1)S(1)}, bf16[6,3072]{1,0:T(8,128)(2,1)S(1)}, u32[]{:S(2)}, u32[]{:S(2)}) collective-permute-start(bf16[6,3072]{1,0:T(8,128)(2,1)S(1)} %constant_dynamic-update-slice_fusion), channel_id=1, source_target_pairs={{0,4},{4,0},{1,5},{5,1},{2,6},{6,2},{3,7},{7,3},{8,12},{12,8},{9,1... | collective-permute-start | bytes 110600 | tf_op jit(solution)/shard_map/ppermute | solution.py:19
  11.5 6.5 %collective-permute-start.1 = (bf16[12,3072]{1,0:T(8,128)(2,1)S(1)}, bf16[12,3072]{1,0:T(8,128)(2,1)S(1)}, u32[]{:S(2)}, u32[]{:S(2)}) collective-permute-start(bf16[12,3072]{1,0:T(8,128)(2,1)S(1)} %pad_maximum_fusion.7), channel_id=1, source_target_pairs={{0,2},{2,0},{1,3},{3,1},{4,6},{6,4},{5,7},{7,5},{8,10},{10,8},{9,1... | collective-permute-start | bytes 221192 | tf_op jit(solution)/shard_map/ppermute | solution.py:19
  18.1 3.3 %collective-permute-start.2 = (bf16[24,3072]{1,0:T(8,128)(2,1)S(1)}, bf16[24,3072]{1,0:T(8,128)(2,1)S(1)}, u32[]{:S(2)}, u32[]{:S(2)}) collective-permute-start(bf16[24,3072]{1,0:T(8,128)(2,1)S(1)} %pad_maximum_fusion.4), channel_id=1, source_target_pairs={{0,1},{1,0},{2,3},{3,2},{4,5},{5,4},{6,7},{7,6},{8,9},{9,8},{10,11... | collective-permute-start | bytes 442376 | tf_op jit(solution)/shard_map/ppermute | solution.py:19
  21.7 1.1 copy-start.3
  21.7 1.1 copy-start.4
  26.2 3.7 %collective-permute-start.3 = (bf16[24,17,512]{2,0,1:T(8,128)(2,1)S(1)}, bf16[24,17,512]{2,0,1:T(8,128)(2,1)S(1)}, u32[]{:S(2)}, u32[]{:S(2)}) collective-permute-start(bf16[24,17,512]{2,0,1:T(8,128)(2,1)S(1)} %copy.96), channel_id=1, source_target_pairs={{0,1},{1,0},{2,3},{3,2},{4,5},{5,4},{6,7},{7,6},{8,9},{9,8},{10,11... | collective-permute-start | bytes 1253384 | tf_op jit(solution)/shard_map/ppermute | solution.py:19
  30.4 36.3 %copy-start.2 = (s32[16]{0:T(128)S(1)}, s32[16]{0:T(128)}, u32[]{:S(2)}) copy-start(s32[16]{0:T(128)} %constant.169) | copy-start | bytes 196
  30.5 50.3 %copy-start.1 = (bf16[128,2048]{1,0:T(8,128)(2,1)S(1)}, bf16[128,2048]{1,0:T(8,128)(2,1)}, u32[]{:S(2)}) copy-start(bf16[128,2048]{1,0:T(8,128)(2,1)} %param.21) | copy-start | bytes 1572868
  30.5 11.1 %collective-permute-start.4 = (bf16[12,17,512]{2,1,0:T(8,128)(2,1)S(1)}, bf16[12,17,512]{2,1,0:T(8,128)(2,1)S(1)}, u32[]{:S(2)}, u32[]{:S(2)}) collective-permute-start(bf16[12,17,512]{2,1,0:T(8,128)(2,1)S(1)} %pad_maximum_fusion.3), channel_id=1, source_target_pairs={{0,2},{2,0},{1,3},{3,1},{4,6},{6,4},{5,7},{7,5},{8,10},{10,8},{9,1... | collective-permute-start | bytes 626696 | tf_op jit(solution)/shard_map/ppermute | solution.py:19
  42.0 8.5 %collective-permute-start.5 = (bf16[6,17,512]{2,1,0:T(8,128)(2,1)S(1)}, bf16[6,17,512]{2,1,0:T(8,128)(2,1)S(1)}, u32[]{:S(2)}, u32[]{:S(2)}) collective-permute-start(bf16[6,17,512]{2,1,0:T(8,128)(2,1)S(1)} %pad_maximum_fusion.5), channel_id=1, source_target_pairs={{0,4},{4,0},{1,5},{5,1},{2,6},{6,2},{3,7},{7,3},{8,12},{12,8},{9,1... | collective-permute-start | bytes 313352 | tf_op jit(solution)/shard_map/ppermute | solution.py:19
  51.5 28.6 %all-to-all-start = ((bf16[16,6,512]{2,1,0:T(8,128)(2,1)}), bf16[16,6,512]{2,1,0:T(8,128)(2,1)S(1)}, u32[]{:S(2)}, u32[]{:S(2)}) async-start(bf16[16,6,512]{2,1,0:T(8,128)(2,1)} %copy.101), calls=%async_computation | async-start | bytes 262144 | tf_op jit(solution)/shard_map/all_to_all | solution.py:172
  82.1 7.6 %collective-permute-start.6 = (bf16[48,2048]{1,0:T(8,128)(2,1)S(1)}, bf16[48,2048]{1,0:T(8,128)(2,1)S(1)}, u32[]{:S(2)}, u32[]{:S(2)}) collective-permute-start(bf16[48,2048]{1,0:T(8,128)(2,1)S(1)} %select_convert_fusion.1), channel_id=1, source_target_pairs={{0,32},{32,0},{64,96},{96,64},{128,160},{160,128},{192,224},{224,1... | collective-permute-start | bytes 589832 | tf_op jit(solution)/shard_map/ppermute | solution.py:19
  89.7 8.5 %collective-permute-start.7 = (bf16[24,2048]{1,0:T(8,128)(2,1)S(1)}, bf16[24,2048]{1,0:T(8,128)(2,1)S(1)}, u32[]{:S(2)}, u32[]{:S(2)}) collective-permute-start(bf16[24,2048]{1,0:T(8,128)(2,1)S(1)} %select_convert_fusion.3), channel_id=1, source_target_pairs={{0,64},{64,0},{32,96},{96,32},{128,192},{192,128},{160,224},{224,1... | collective-permute-start | bytes 294920 | tf_op jit(solution)/shard_map/ppermute | solution.py:19
  98.3 14.0 %collective-permute-start.8 = (bf16[6,2048]{1,0:T(8,128)(2,1)S(1)}, bf16[6,2048]{1,0:T(8,128)(2,1)S(1)}, u32[]{:S(2)}, u32[]{:S(2)}) collective-permute-start(bf16[6,2048]{1,0:T(8,128)(2,1)S(1)} %get-tuple-element.24), channel_id=1, source_target_pairs={{0,128},{32,160},{64,192},{96,224},{128,256},{160,288},{192,320},{... | collective-permute-start | bytes 73736 | tf_op jit(solution)/shard_map/ppermute | solution.py:25
  101.8 10.6 %collective-permute-start.10 = (bf16[6,2048]{1,0:T(8,128)(2,1)S(1)}, bf16[6,2048]{1,0:T(8,128)(2,1)S(1)}, u32[]{:S(2)}, u32[]{:S(2)}) collective-permute-start(bf16[6,2048]{1,0:T(8,128)(2,1)S(1)} %get-tuple-element.25), channel_id=1, source_target_pairs={{0,384},{32,416},{64,448},{96,480},{128,0},{160,32},{192,64},{224,... | collective-permute-start | bytes 73736 | tf_op jit(solution)/shard_map/ppermute | solution.py:25
  108.1 15.6 %collective-permute-start.9 = (bf16[6,2048]{1,0:T(8,128)(2,1)S(1)}, bf16[6,2048]{1,0:T(8,128)(2,1)S(1)}, u32[]{:S(2)}, u32[]{:S(2)}) collective-permute-start(bf16[6,2048]{1,0:T(8,128)(2,1)S(1)} %get-tuple-element.26), channel_id=1, source_target_pairs={{0,256},{32,288},{64,320},{96,352},{128,384},{160,416},{192,448},{... | collective-permute-start | bytes 73736 | tf_op jit(solution)/shard_map/ppermute | solution.py:25

commit v5 on v4

--- a/solution.py
+++ b/solution.py
@@ -63,14 +63,18 @@
     high_hi, high_lo = split_high(part_high)
     stats = jnp.concatenate([high_hi, high_lo, part_total.astype(jnp.bfloat16)], axis=1)
     stats = jnp.pad(stats, ((0, 0), (0, width - stats.shape[1])))
-    return jnp.concatenate([part_sum.astype(jnp.bfloat16), stats[:, None, :]], axis=1)
+    rows, heads = part_sum.shape[0], part_sum.shape[1]
+    flat_sum = part_sum.astype(jnp.bfloat16).reshape(rows * heads, width)
+    return jnp.concatenate([flat_sum, stats], axis=0)
 
 
 def unpack_part(packed, heads):
-    stats = packed[:, heads].astype(jnp.float32)
+    rows = packed.shape[0] // (heads + 1)
+    stats = packed[rows * heads :].astype(jnp.float32)
     high = stats[:, :heads] + stats[:, heads : 2 * heads]
     total = stats[:, 2 * heads : 3 * heads]
-    return packed[:, :heads].astype(jnp.float32), high, total
+    part_sum = packed[: rows * heads].reshape(rows, heads, packed.shape[1])
+    return part_sum.astype(jnp.float32), high, total
 
 
 def combine_parts(kept_part, received):

time: 125 us -> 122 us (0.976)
  waiting for transfers between devices: 54.1 us -> 51.9 us
    ppermute x8, waiting for transfers between devices: 29.4 us -> 27.2 us  [from_partner(): return lax.ppermute(block, axis, route)]
where the time goes in v5:
time: 122 us
  starting transfers between devices  52.3 us (43%)
  waiting for transfers between devices  51.9 us (43%)
  local copies, waits for them, and re-layouts  6.04 us (5%)
  other arithmetic  5.4 us (4%)
  matrix products  5.14 us (4%)
    ppermute x8, waiting for transfers between devices, from_partner(): return lax.ppermute(block, axis, route)  27.2 us
    ppermute x8, starting transfers between devices, from_partner(): return lax.ppermute(block, axis, route)  23.2 us
    all_to_all x1, starting transfers between devices, per_device(): lax.all_to_all(jnp.swapaxes(merged.astype(jnp.bfloat16), 0, 1), 'grp', sp...  15.2 us
    ppermute x3, starting transfers between devices, shifted(): return lax.ppermute(block, axis, route)  14 us
    all_to_all x1, waiting for transfers between devices, per_device(): lax.all_to_all(jnp.swapaxes(merged.astype(jnp.bfloat16), 0, 1), 'grp', sp...  13.4 us
    ppermute x3, waiting for transfers between devices, shifted(): return lax.ppermute(block, axis, route)  11.3 us
  transfers between devices with their start and end apart: 12, of which 9 were waited for; matrix products, arithmetic and copies ran while one was open for 5% of the time, Pallas kernels for 0%

profile of v5, /device:TPU:6, one launch (start us, length us, event | category | flops | bytes accessed | tf_op | source)
XLA Modules:
  0.0 121.6 jit_solution(15212464599472108258)
XLA Ops:
  1.6 5.1 %collective-permute-start = (bf16[6,3072]{1,0:T(8,128)(2,1)S(1)}, bf16[6,3072]{1,0:T(8,128)(2,1)S(1)}, u32[]{:S(2)}, u32[]{:S(2)}) collective-permute-start(bf16[6,3072]{1,0:T(8,128)(2,1)S(1)} %constant_dynamic-update-slice_fusion), channel_id=1, source_target_pairs={{0,4},{4,0},{1,5},{5,1},{2,6},{6,2},{3,7},{7,3},{8,12},{12,8},{9,1... | collective-permute-start | bytes 110600 | tf_op jit(solution)/shard_map/ppermute | solution.py:19
  6.8 1.2 %dynamic_slice.24 = s32[1]{0:T(128)} dynamic-slice(s32[4]{0:T(128)} %param.17, s32[]{:T(128)S(6)} %select_n.241), dynamic_slice_sizes={1} | dynamic-slice | bytes 12 | tf_op jit(solution)/shard_map/jit(dynamic_index_in_dim)/dynamic_slice | solution.py:135
  11.5 2.6 %collective-permute-start.1 = (bf16[12,3072]{1,0:T(8,128)(2,1)S(1)}, bf16[12,3072]{1,0:T(8,128)(2,1)S(1)}, u32[]{:S(2)}, u32[]{:S(2)}) collective-permute-start(bf16[12,3072]{1,0:T(8,128)(2,1)S(1)} %pad_maximum_fusion.7), channel_id=1, source_target_pairs={{0,2},{2,0},{1,3},{3,1},{4,6},{6,4},{5,7},{7,5},{8,10},{10,8},{9,1... | collective-permute-start | bytes 221192 | tf_op jit(solution)/shard_map/ppermute | solution.py:19
  15.4 2.7 %collective-permute-done.1 = bf16[12,3072]{1,0:T(8,128)(2,1)S(1)} collective-permute-done((bf16[12,3072]{1,0:T(8,128)(2,1)S(1)}, bf16[12,3072]{1,0:T(8,128)(2,1)S(1)}, u32[]{:S(2)}, u32[]{:S(2)}) %collective-permute-start.1) | collective-permute-done | bytes 73760 | tf_op jit(solution)/shard_map/ppermute | solution.py:19
  18.1 1.9 %collective-permute-start.2 = (bf16[24,3072]{1,0:T(8,128)(2,1)S(1)}, bf16[24,3072]{1,0:T(8,128)(2,1)S(1)}, u32[]{:S(2)}, u32[]{:S(2)}) collective-permute-start(bf16[24,3072]{1,0:T(8,128)(2,1)S(1)} %pad_maximum_fusion.4), channel_id=1, source_target_pairs={{0,1},{1,0},{2,3},{3,2},{4,5},{5,4},{6,7},{7,6},{8,9},{9,8},{10,11... | collective-permute-start | bytes 442376 | tf_op jit(solution)/shard_map/ppermute | solution.py:19
  20.1 1.3 %collective-permute-done.2 = bf16[24,3072]{1,0:T(8,128)(2,1)S(1)} collective-permute-done((bf16[24,3072]{1,0:T(8,128)(2,1)S(1)}, bf16[24,3072]{1,0:T(8,128)(2,1)S(1)}, u32[]{:S(2)}, u32[]{:S(2)}) %collective-permute-start.2) | collective-permute-done | bytes 147488 | tf_op jit(solution)/shard_map/ppermute | solution.py:19
  22.8 1.1 fusion
  25.9 2.0 %collective-permute-start.3 = (bf16[408,512]{1,0:T(8,128)(2,1)S(1)}, bf16[408,512]{1,0:T(8,128)(2,1)S(1)}, u32[]{:S(2)}, u32[]{:S(2)}) collective-permute-start(bf16[408,512]{1,0:T(8,128)(2,1)S(1)} %pad_maximum_fusion.2), channel_id=1, source_target_pairs={{0,1},{1,0},{2,3},{3,2},{4,5},{5,4},{6,7},{7,6},{8,9},{9,8},{10,11... | collective-permute-start | bytes 1253384 | tf_op jit(solution)/shard_map/ppermute | solution.py:19
  28.0 1.6 %collective-permute-done.3 = bf16[408,512]{1,0:T(8,128)(2,1)S(1)} collective-permute-done((bf16[408,512]{1,0:T(8,128)(2,1)S(1)}, bf16[408,512]{1,0:T(8,128)(2,1)S(1)}, u32[]{:S(2)}, u32[]{:S(2)}) %collective-permute-start.3) | collective-permute-done | bytes 417824 | tf_op jit(solution)/shard_map/ppermute | solution.py:19
  30.2 2.6 %collective-permute-start.4 = (bf16[204,512]{1,0:T(8,128)(2,1)S(1)}, bf16[204,512]{1,0:T(8,128)(2,1)S(1)}, u32[]{:S(2)}, u32[]{:S(2)}) collective-permute-start(bf16[204,512]{1,0:T(8,128)(2,1)S(1)} %pad_maximum_fusion.3), channel_id=1, source_target_pairs={{0,2},{2,0},{1,3},{3,1},{4,6},{6,4},{5,7},{7,5},{8,10},{10,8},{9,1... | collective-permute-start | bytes 626696 | tf_op jit(solution)/shard_map/ppermute | solution.py:19
  32.7 6.6 %collective-permute-done.4 = bf16[204,512]{1,0:T(8,128)(2,1)S(1)} collective-permute-done((bf16[204,512]{1,0:T(8,128)(2,1)S(1)}, bf16[204,512]{1,0:T(8,128)(2,1)S(1)}, u32[]{:S(2)}, u32[]{:S(2)}) %collective-permute-start.4) | collective-permute-done | bytes 208928 | tf_op jit(solution)/shard_map/ppermute | solution.py:19
  39.8 2.8 %collective-permute-start.5 = (bf16[102,512]{1,0:T(8,128)(2,1)S(1)}, bf16[102,512]{1,0:T(8,128)(2,1)S(1)}, u32[]{:S(2)}, u32[]{:S(2)}) collective-permute-start(bf16[102,512]{1,0:T(8,128)(2,1)S(1)} %pad_maximum_fusion.5), channel_id=1, source_target_pairs={{0,4},{4,0},{1,5},{5,1},{2,6},{6,2},{3,7},{7,3},{8,12},{12,8},{9,1... | collective-permute-start | bytes 313352 | tf_op jit(solution)/shard_map/ppermute | solution.py:19
  42.5 5.3 %collective-permute-done.5 = bf16[102,512]{1,0:T(8,128)(2,1)S(1)} collective-permute-done((bf16[102,512]{1,0:T(8,128)(2,1)S(1)}, bf16[102,512]{1,0:T(8,128)(2,1)S(1)}, u32[]{:S(2)}, u32[]{:S(2)}) %collective-permute-start.5) | collective-permute-done | bytes 104480 | tf_op jit(solution)/shard_map/ppermute | solution.py:19
  48.8 15.2 %all-to-all-start = ((bf16[16,6,512]{2,1,0:T(8,128)(2,1)}), bf16[16,6,512]{2,1,0:T(8,128)(2,1)S(1)}, u32[]{:S(2)}, u32[]{:S(2)}) async-start(bf16[16,6,512]{2,1,0:T(8,128)(2,1)} %copy.49), calls=%async_computation | async-start | bytes 262144 | tf_op jit(solution)/shard_map/all_to_all | solution.py:176
  64.0 13.4 %all-to-all-done = bf16[16,6,512]{2,1,0:T(8,128)(2,1)S(1)} async-done(((bf16[16,6,512]{2,1,0:T(8,128)(2,1)}), bf16[16,6,512]{2,1,0:T(8,128)(2,1)S(1)}, u32[]{:S(2)}, u32[]{:S(2)}) %all-to-all-start) | async-done | bytes 98336 | tf_op jit(solution)/shard_map/all_to_all | solution.py:176
  78.1 1.3 %fusion.4 = f32[96,2048]{1,0:T(8,128)S(1)} fusion(bf16[128,2048]{1,0:T(8,128)(2,1)S(1)} %copy-done.1, bf16[96,512]{1,0:T(8,128)(2,1)S(1)} %reshape.87, bf16[1,512,128]{2,1,0:T(8,128)(2,1)} %param.20), kind=kOutput, calls=%fused_computation.15 | convolution fusion | flops 62926848 | bytes 1540096 | tf_op jit(solution)/shard_map/dot_general | solution.py:185
  79.4 2.9 %collective-permute-start.6 = (bf16[48,2048]{1,0:T(8,128)(2,1)S(1)}, bf16[48,2048]{1,0:T(8,128)(2,1)S(1)}, u32[]{:S(2)}, u32[]{:S(2)}) collective-permute-start(bf16[48,2048]{1,0:T(8,128)(2,1)S(1)} %select_convert_fusion.1), channel_id=1, source_target_pairs={{0,32},{32,0},{64,96},{96,64},{128,160},{160,128},{192,224},{224,1... | collective-permute-start | bytes 589832 | tf_op jit(solution)/shard_map/ppermute | solution.py:19
  82.3 4.6 %collective-permute-done.6 = bf16[48,2048]{1,0:T(8,128)(2,1)S(1)} collective-permute-done((bf16[48,2048]{1,0:T(8,128)(2,1)S(1)}, bf16[48,2048]{1,0:T(8,128)(2,1)S(1)}, u32[]{:S(2)}, u32[]{:S(2)}) %collective-permute-start.6) | collective-permute-done | bytes 196640 | tf_op jit(solution)/shard_map/ppermute | solution.py:19
  87.0 3.2 %collective-permute-start.7 = (bf16[24,2048]{1,0:T(8,128)(2,1)S(1)}, bf16[24,2048]{1,0:T(8,128)(2,1)S(1)}, u32[]{:S(2)}, u32[]{:S(2)}) collective-permute-start(bf16[24,2048]{1,0:T(8,128)(2,1)S(1)} %select_convert_fusion.3), channel_id=1, source_target_pairs={{0,64},{64,0},{32,96},{96,32},{128,192},{192,128},{160,224},{224,1... | collective-permute-start | bytes 294920 | tf_op jit(solution)/shard_map/ppermute | solution.py:19
  90.4 5.1 %collective-permute-done.7 = bf16[24,2048]{1,0:T(8,128)(2,1)S(1)} collective-permute-done((bf16[24,2048]{1,0:T(8,128)(2,1)S(1)}, bf16[24,2048]{1,0:T(8,128)(2,1)S(1)}, u32[]{:S(2)}, u32[]{:S(2)}) %collective-permute-start.7) | collective-permute-done | bytes 98336 | tf_op jit(solution)/shard_map/ppermute | solution.py:19
  95.6 3.5 %collective-permute-start.8 = (bf16[6,2048]{1,0:T(8,128)(2,1)S(1)}, bf16[6,2048]{1,0:T(8,128)(2,1)S(1)}, u32[]{:S(2)}, u32[]{:S(2)}) collective-permute-start(bf16[6,2048]{1,0:T(8,128)(2,1)S(1)} %get-tuple-element.24), channel_id=1, source_target_pairs={{0,128},{32,160},{64,192},{96,224},{128,256},{160,288},{192,320},{... | collective-permute-start | bytes 73736 | tf_op jit(solution)/shard_map/ppermute | solution.py:25
  99.1 6.3 %collective-permute-start.10 = (bf16[6,2048]{1,0:T(8,128)(2,1)S(1)}, bf16[6,2048]{1,0:T(8,128)(2,1)S(1)}, u32[]{:S(2)}, u32[]{:S(2)}) collective-permute-start(bf16[6,2048]{1,0:T(8,128)(2,1)S(1)} %get-tuple-element.25), channel_id=1, source_target_pairs={{0,384},{32,416},{64,448},{96,480},{128,0},{160,32},{192,64},{224,... | collective-permute-start | bytes 73736 | tf_op jit(solution)/shard_map/ppermute | solution.py:25
  105.4 4.2 %collective-permute-start.9 = (bf16[6,2048]{1,0:T(8,128)(2,1)S(1)}, bf16[6,2048]{1,0:T(8,128)(2,1)S(1)}, u32[]{:S(2)}, u32[]{:S(2)}) collective-permute-start(bf16[6,2048]{1,0:T(8,128)(2,1)S(1)} %get-tuple-element.26), channel_id=1, source_target_pairs={{0,256},{32,288},{64,320},{96,352},{128,384},{160,416},{192,448},{... | collective-permute-start | bytes 73736 | tf_op jit(solution)/shard_map/ppermute | solution.py:25
  109.7 11.3 %collective-permute-done.9 = bf16[6,2048]{1,0:T(8,128)(2,1)S(1)} collective-permute-done((bf16[6,2048]{1,0:T(8,128)(2,1)S(1)}, bf16[6,2048]{1,0:T(8,128)(2,1)S(1)}, u32[]{:S(2)}, u32[]{:S(2)}) %collective-permute-start.9) | collective-permute-done | bytes 24608 | tf_op jit(solution)/shard_map/ppermute | solution.py:25
  (84 shorter events, 12.9 us)
Async XLA Ops:
  0.0 21.7 %copy-start = (bf16[16,512,128]{2,1,0:T(8,128)(2,1)S(1)}, bf16[16,512,128]{2,1,0:T(8,128)(2,1)}, u32[]{:S(2)}) copy-start(bf16[16,512,128]{2,1,0:T(8,128)(2,1)} %param.19) | copy-start | bytes 6291460
  1.6 9.8 %collective-permute-start = (bf16[6,3072]{1,0:T(8,128)(2,1)S(1)}, bf16[6,3072]{1,0:T(8,128)(2,1)S(1)}, u32[]{:S(2)}, u32[]{:S(2)}) collective-permute-start(bf16[6,3072]{1,0:T(8,128)(2,1)S(1)} %constant_dynamic-update-slice_fusion), channel_id=1, source_target_pairs={{0,4},{4,0},{1,5},{5,1},{2,6},{6,2},{3,7},{7,3},{8,12},{12,8},{9,1... | collective-permute-start | bytes 110600 | tf_op jit(solution)/shard_map/ppermute | solution.py:19
  11.5 6.5 %collective-permute-start.1 = (bf16[12,3072]{1,0:T(8,128)(2,1)S(1)}, bf16[12,3072]{1,0:T(8,128)(2,1)S(1)}, u32[]{:S(2)}, u32[]{:S(2)}) collective-permute-start(bf16[12,3072]{1,0:T(8,128)(2,1)S(1)} %pad_maximum_fusion.7), channel_id=1, source_target_pairs={{0,2},{2,0},{1,3},{3,1},{4,6},{6,4},{5,7},{7,5},{8,10},{10,8},{9,1... | collective-permute-start | bytes 221192 | tf_op jit(solution)/shard_map/ppermute | solution.py:19
  18.1 3.3 %collective-permute-start.2 = (bf16[24,3072]{1,0:T(8,128)(2,1)S(1)}, bf16[24,3072]{1,0:T(8,128)(2,1)S(1)}, u32[]{:S(2)}, u32[]{:S(2)}) collective-permute-start(bf16[24,3072]{1,0:T(8,128)(2,1)S(1)} %pad_maximum_fusion.4), channel_id=1, source_target_pairs={{0,1},{1,0},{2,3},{3,2},{4,5},{5,4},{6,7},{7,6},{8,9},{9,8},{10,11... | collective-permute-start | bytes 442376 | tf_op jit(solution)/shard_map/ppermute | solution.py:19
  21.7 1.1 copy-start.3
  21.7 1.1 copy-start.4
  25.9 3.7 %collective-permute-start.3 = (bf16[408,512]{1,0:T(8,128)(2,1)S(1)}, bf16[408,512]{1,0:T(8,128)(2,1)S(1)}, u32[]{:S(2)}, u32[]{:S(2)}) collective-permute-start(bf16[408,512]{1,0:T(8,128)(2,1)S(1)} %pad_maximum_fusion.2), channel_id=1, source_target_pairs={{0,1},{1,0},{2,3},{3,2},{4,5},{5,4},{6,7},{7,6},{8,9},{9,8},{10,11... | collective-permute-start | bytes 1253384 | tf_op jit(solution)/shard_map/ppermute | solution.py:19
  30.1 33.9 %copy-start.2 = (s32[16]{0:T(128)S(1)}, s32[16]{0:T(128)}, u32[]{:S(2)}) copy-start(s32[16]{0:T(128)} %constant.169) | copy-start | bytes 196
  30.2 9.2 %collective-permute-start.4 = (bf16[204,512]{1,0:T(8,128)(2,1)S(1)}, bf16[204,512]{1,0:T(8,128)(2,1)S(1)}, u32[]{:S(2)}, u32[]{:S(2)}) collective-permute-start(bf16[204,512]{1,0:T(8,128)(2,1)S(1)} %pad_maximum_fusion.3), channel_id=1, source_target_pairs={{0,2},{2,0},{1,3},{3,1},{4,6},{6,4},{5,7},{7,5},{8,10},{10,8},{9,1... | collective-permute-start | bytes 626696 | tf_op jit(solution)/shard_map/ppermute | solution.py:19
  39.5 38.6 %copy-start.1 = (bf16[128,2048]{1,0:T(8,128)(2,1)S(1)}, bf16[128,2048]{1,0:T(8,128)(2,1)}, u32[]{:S(2)}) copy-start(bf16[128,2048]{1,0:T(8,128)(2,1)} %param.21) | copy-start | bytes 1572868
  39.8 8.1 %collective-permute-start.5 = (bf16[102,512]{1,0:T(8,128)(2,1)S(1)}, bf16[102,512]{1,0:T(8,128)(2,1)S(1)}, u32[]{:S(2)}, u32[]{:S(2)}) collective-permute-start(bf16[102,512]{1,0:T(8,128)(2,1)S(1)} %pad_maximum_fusion.5), channel_id=1, source_target_pairs={{0,4},{4,0},{1,5},{5,1},{2,6},{6,2},{3,7},{7,3},{8,12},{12,8},{9,1... | collective-permute-start | bytes 313352 | tf_op jit(solution)/shard_map/ppermute | solution.py:19
  48.8 28.6 %all-to-all-start = ((bf16[16,6,512]{2,1,0:T(8,128)(2,1)}), bf16[16,6,512]{2,1,0:T(8,128)(2,1)S(1)}, u32[]{:S(2)}, u32[]{:S(2)}) async-start(bf16[16,6,512]{2,1,0:T(8,128)(2,1)} %copy.49), calls=%async_computation | async-start | bytes 262144 | tf_op jit(solution)/shard_map/all_to_all | solution.py:176
  79.4 7.6 %collective-permute-start.6 = (bf16[48,2048]{1,0:T(8,128)(2,1)S(1)}, bf16[48,2048]{1,0:T(8,128)(2,1)S(1)}, u32[]{:S(2)}, u32[]{:S(2)}) collective-permute-start(bf16[48,2048]{1,0:T(8,128)(2,1)S(1)} %select_convert_fusion.1), channel_id=1, source_target_pairs={{0,32},{32,0},{64,96},{96,64},{128,160},{160,128},{192,224},{224,1... | collective-permute-start | bytes 589832 | tf_op jit(solution)/shard_map/ppermute | solution.py:19
  87.0 8.5 %collective-permute-start.7 = (bf16[24,2048]{1,0:T(8,128)(2,1)S(1)}, bf16[24,2048]{1,0:T(8,128)(2,1)S(1)}, u32[]{:S(2)}, u32[]{:S(2)}) collective-permute-start(bf16[24,2048]{1,0:T(8,128)(2,1)S(1)} %select_convert_fusion.3), channel_id=1, source_target_pairs={{0,64},{64,0},{32,96},{96,32},{128,192},{192,128},{160,224},{224,1... | collective-permute-start | bytes 294920 | tf_op jit(solution)/shard_map/ppermute | solution.py:19
  95.6 14.0 %collective-permute-start.8 = (bf16[6,2048]{1,0:T(8,128)(2,1)S(1)}, bf16[6,2048]{1,0:T(8,128)(2,1)S(1)}, u32[]{:S(2)}, u32[]{:S(2)}) collective-permute-start(bf16[6,2048]{1,0:T(8,128)(2,1)S(1)} %get-tuple-element.24), channel_id=1, source_target_pairs={{0,128},{32,160},{64,192},{96,224},{128,256},{160,288},{192,320},{... | collective-permute-start | bytes 73736 | tf_op jit(solution)/shard_map/ppermute | solution.py:25
  99.1 10.6 %collective-permute-start.10 = (bf16[6,2048]{1,0:T(8,128)(2,1)S(1)}, bf16[6,2048]{1,0:T(8,128)(2,1)S(1)}, u32[]{:S(2)}, u32[]{:S(2)}) collective-permute-start(bf16[6,2048]{1,0:T(8,128)(2,1)S(1)} %get-tuple-element.25), channel_id=1, source_target_pairs={{0,384},{32,416},{64,448},{96,480},{128,0},{160,32},{192,64},{224,... | collective-permute-start | bytes 73736 | tf_op jit(solution)/shard_map/ppermute | solution.py:25
  105.4 15.6 %collective-permute-start.9 = (bf16[6,2048]{1,0:T(8,128)(2,1)S(1)}, bf16[6,2048]{1,0:T(8,128)(2,1)S(1)}, u32[]{:S(2)}, u32[]{:S(2)}) collective-permute-start(bf16[6,2048]{1,0:T(8,128)(2,1)S(1)} %get-tuple-element.26), channel_id=1, source_target_pairs={{0,256},{32,288},{64,320},{96,352},{128,384},{160,416},{192,448},{... | collective-permute-start | bytes 73736 | tf_op jit(solution)/shard_map/ppermute | solution.py:25

commit v6 on v5

--- a/solution.py
+++ b/solution.py
@@ -176,26 +176,38 @@
     spread = lax.all_to_all(
         jnp.swapaxes(merged.astype(jnp.bfloat16), 0, 1), "grp", split_axis=0, concat_axis=0, tiled=True
     )
-    spread = spread.reshape(grp_size, token_count, latent_width)[jnp.array(bit_reversed(grp_size))]
+    group = lax.axis_index("grp")
+    core = position & 1
+    label = (group - core) % grp_size
+    spread = jnp.take(
+        spread.reshape(grp_size, token_count, latent_width),
+        (jnp.array(bit_reversed(grp_size)) + core) % grp_size,
+        axis=0,
+    )
     head_rows = jnp.dot(
         spread.reshape(grp_size * token_count, latent_width),
         w_value[0],
         preferred_element_type=jnp.float32,
     ).astype(jnp.bfloat16)
     rows_out = jnp.dot(head_rows, out_weight, preferred_element_type=jnp.float32)
-    group = lax.axis_index("grp")
+    ep_size = lax.axis_size("ep")
     for bit_level in range(2):
         half_rows = rows_out.shape[0] // 2
-        upper_side = jnp.right_shift(group, bit_level) & 1 == 1
+        upper_side = jnp.right_shift(label, bit_level) & 1 == 1
         lower, upper = rows_out[:half_rows], rows_out[half_rows:]
         kept = jnp.where(upper_side, upper, lower)
         sent = jnp.where(upper_side, lower, upper)
-        rows_out = kept + from_partner(sent.astype(jnp.bfloat16), "grp", bit_level).astype(
-            jnp.float32
-        )
+        route = []
+        for plane in range(grp_size):
+            for column in range(ep_size):
+                shift = column & 1
+                other = ((((plane - shift) % grp_size) ^ (1 << bit_level)) + shift) % grp_size
+                route.append((plane * ep_size + column, other * ep_size + column))
+        got = lax.ppermute(sent.astype(jnp.bfloat16), ("grp", "ep"), route)
+        rows_out = kept + got.astype(jnp.float32)
     ring = grp_size // 4
     blocks = rows_out.reshape(ring, token_count, rows_out.shape[1])
-    mine = group // 4
+    mine = label // 4
 
     def block_for(member):
         return lax.dynamic_index_in_dim(

time: 122 us -> 122 us (level)
    ppermute x8 -> x6, waiting for transfers between devices: 27.2 us -> 17.5 us  [from_partner(): return lax.ppermute(block, axis, route)]
    ppermute x0 -> x2, waiting for transfers between devices: none -> 9.71 us  [per_device(): got = lax.ppermute(sent.astype(jnp.bfloat16), ('grp', 'ep'), route)]
    ppermute x0 -> x2, starting transfers between devices: none -> 6.15 us  [per_device(): got = lax.ppermute(sent.astype(jnp.bfloat16), ('grp', 'ep'), route)]
    ppermute x8 -> x6, starting transfers between devices: 23.2 us -> 17 us  [from_partner(): return lax.ppermute(block, axis, route)]
where the time goes in v6:
time: 122 us
  starting transfers between devices  52.3 us (43%)
  waiting for transfers between devices  51.9 us (43%)
  local copies, waits for them, and re-layouts  6.03 us (5%)
  other arithmetic  5.5 us (5%)
  matrix products  5.14 us (4%)
    ppermute x6, waiting for transfers between devices, from_partner(): return lax.ppermute(block, axis, route)  17.5 us
    ppermute x6, starting transfers between devices, from_partner(): return lax.ppermute(block, axis, route)  17 us
    all_to_all x1, starting transfers between devices, per_device(): lax.all_to_all(jnp.swapaxes(merged.astype(jnp.bfloat16), 0, 1), 'grp', sp...  15.2 us
    ppermute x3, starting transfers between devices, shifted(): return lax.ppermute(block, axis, route)  14 us
    all_to_all x1, waiting for transfers between devices, per_device(): lax.all_to_all(jnp.swapaxes(merged.astype(jnp.bfloat16), 0, 1), 'grp', sp...  13.4 us
    ppermute x3, waiting for transfers between devices, shifted(): return lax.ppermute(block, axis, route)  11.3 us
    ppermute x2, waiting for transfers between devices, per_device(): got = lax.ppermute(sent.astype(jnp.bfloat16), ('grp', 'ep'), route)  9.71 us
    ppermute x2, starting transfers between devices, per_device(): got = lax.ppermute(sent.astype(jnp.bfloat16), ('grp', 'ep'), route)  6.15 us
  transfers between devices with their start and end apart: 12, of which 9 were waited for; matrix products, arithmetic and copies ran while one was open for 5% of the time, Pallas kernels for 0%

profile of v6, /device:TPU:6, one launch (start us, length us, event | category | flops | bytes accessed | tf_op | source)
XLA Modules:
  0.0 121.7 jit_solution(1398105744288505801)
XLA Ops:
  1.6 5.1 %collective-permute-start = (bf16[6,3072]{1,0:T(8,128)(2,1)S(1)}, bf16[6,3072]{1,0:T(8,128)(2,1)S(1)}, u32[]{:S(2)}, u32[]{:S(2)}) collective-permute-start(bf16[6,3072]{1,0:T(8,128)(2,1)S(1)} %constant_dynamic-update-slice_fusion), channel_id=1, source_target_pairs={{0,4},{4,0},{1,5},{5,1},{2,6},{6,2},{3,7},{7,3},{8,12},{12,8},{9,1... | collective-permute-start | bytes 110600 | tf_op jit(solution)/shard_map/ppermute | solution.py:19
  6.8 1.2 %dynamic_slice.24 = s32[1]{0:T(128)} dynamic-slice(s32[4]{0:T(128)} %param.17, s32[]{:T(128)S(6)} %select_n.270), dynamic_slice_sizes={1} | dynamic-slice | bytes 12 | tf_op jit(solution)/shard_map/jit(dynamic_index_in_dim)/dynamic_slice | solution.py:135
  11.5 2.6 %collective-permute-start.1 = (bf16[12,3072]{1,0:T(8,128)(2,1)S(1)}, bf16[12,3072]{1,0:T(8,128)(2,1)S(1)}, u32[]{:S(2)}, u32[]{:S(2)}) collective-permute-start(bf16[12,3072]{1,0:T(8,128)(2,1)S(1)} %pad_maximum_fusion.7), channel_id=1, source_target_pairs={{0,2},{2,0},{1,3},{3,1},{4,6},{6,4},{5,7},{7,5},{8,10},{10,8},{9,1... | collective-permute-start | bytes 221192 | tf_op jit(solution)/shard_map/ppermute | solution.py:19
  15.4 2.7 %collective-permute-done.1 = bf16[12,3072]{1,0:T(8,128)(2,1)S(1)} collective-permute-done((bf16[12,3072]{1,0:T(8,128)(2,1)S(1)}, bf16[12,3072]{1,0:T(8,128)(2,1)S(1)}, u32[]{:S(2)}, u32[]{:S(2)}) %collective-permute-start.1) | collective-permute-done | bytes 73760 | tf_op jit(solution)/shard_map/ppermute | solution.py:19
  18.1 1.9 %collective-permute-start.2 = (bf16[24,3072]{1,0:T(8,128)(2,1)S(1)}, bf16[24,3072]{1,0:T(8,128)(2,1)S(1)}, u32[]{:S(2)}, u32[]{:S(2)}) collective-permute-start(bf16[24,3072]{1,0:T(8,128)(2,1)S(1)} %pad_maximum_fusion.4), channel_id=1, source_target_pairs={{0,1},{1,0},{2,3},{3,2},{4,5},{5,4},{6,7},{7,6},{8,9},{9,8},{10,11... | collective-permute-start | bytes 442376 | tf_op jit(solution)/shard_map/ppermute | solution.py:19
  20.1 1.3 %collective-permute-done.2 = bf16[24,3072]{1,0:T(8,128)(2,1)S(1)} collective-permute-done((bf16[24,3072]{1,0:T(8,128)(2,1)S(1)}, bf16[24,3072]{1,0:T(8,128)(2,1)S(1)}, u32[]{:S(2)}, u32[]{:S(2)}) %collective-permute-start.2) | collective-permute-done | bytes 147488 | tf_op jit(solution)/shard_map/ppermute | solution.py:19
  22.8 1.1 fusion
  25.9 2.0 %collective-permute-start.3 = (bf16[408,512]{1,0:T(8,128)(2,1)S(1)}, bf16[408,512]{1,0:T(8,128)(2,1)S(1)}, u32[]{:S(2)}, u32[]{:S(2)}) collective-permute-start(bf16[408,512]{1,0:T(8,128)(2,1)S(1)} %pad_maximum_fusion.2), channel_id=1, source_target_pairs={{0,1},{1,0},{2,3},{3,2},{4,5},{5,4},{6,7},{7,6},{8,9},{9,8},{10,11... | collective-permute-start | bytes 1253384 | tf_op jit(solution)/shard_map/ppermute | solution.py:19
  28.0 1.6 %collective-permute-done.3 = bf16[408,512]{1,0:T(8,128)(2,1)S(1)} collective-permute-done((bf16[408,512]{1,0:T(8,128)(2,1)S(1)}, bf16[408,512]{1,0:T(8,128)(2,1)S(1)}, u32[]{:S(2)}, u32[]{:S(2)}) %collective-permute-start.3) | collective-permute-done | bytes 417824 | tf_op jit(solution)/shard_map/ppermute | solution.py:19
  30.2 2.6 %collective-permute-start.4 = (bf16[204,512]{1,0:T(8,128)(2,1)S(1)}, bf16[204,512]{1,0:T(8,128)(2,1)S(1)}, u32[]{:S(2)}, u32[]{:S(2)}) collective-permute-start(bf16[204,512]{1,0:T(8,128)(2,1)S(1)} %pad_maximum_fusion.3), channel_id=1, source_target_pairs={{0,2},{2,0},{1,3},{3,1},{4,6},{6,4},{5,7},{7,5},{8,10},{10,8},{9,1... | collective-permute-start | bytes 626696 | tf_op jit(solution)/shard_map/ppermute | solution.py:19
  32.7 6.6 %collective-permute-done.4 = bf16[204,512]{1,0:T(8,128)(2,1)S(1)} collective-permute-done((bf16[204,512]{1,0:T(8,128)(2,1)S(1)}, bf16[204,512]{1,0:T(8,128)(2,1)S(1)}, u32[]{:S(2)}, u32[]{:S(2)}) %collective-permute-start.4) | collective-permute-done | bytes 208928 | tf_op jit(solution)/shard_map/ppermute | solution.py:19
  39.8 2.8 %collective-permute-start.5 = (bf16[102,512]{1,0:T(8,128)(2,1)S(1)}, bf16[102,512]{1,0:T(8,128)(2,1)S(1)}, u32[]{:S(2)}, u32[]{:S(2)}) collective-permute-start(bf16[102,512]{1,0:T(8,128)(2,1)S(1)} %pad_maximum_fusion.5), channel_id=1, source_target_pairs={{0,4},{4,0},{1,5},{5,1},{2,6},{6,2},{3,7},{7,3},{8,12},{12,8},{9,1... | collective-permute-start | bytes 313352 | tf_op jit(solution)/shard_map/ppermute | solution.py:19
  42.5 5.3 %collective-permute-done.5 = bf16[102,512]{1,0:T(8,128)(2,1)S(1)} collective-permute-done((bf16[102,512]{1,0:T(8,128)(2,1)S(1)}, bf16[102,512]{1,0:T(8,128)(2,1)S(1)}, u32[]{:S(2)}, u32[]{:S(2)}) %collective-permute-start.5) | collective-permute-done | bytes 104480 | tf_op jit(solution)/shard_map/ppermute | solution.py:19
  48.8 15.2 %all-to-all-start = ((bf16[16,6,512]{2,1,0:T(8,128)(2,1)}), bf16[16,6,512]{2,1,0:T(8,128)(2,1)S(1)}, u32[]{:S(2)}, u32[]{:S(2)}) async-start(bf16[16,6,512]{2,1,0:T(8,128)(2,1)} %copy.49), calls=%async_computation | async-start | bytes 262144 | tf_op jit(solution)/shard_map/all_to_all | solution.py:176
  64.1 13.4 %all-to-all-done = bf16[16,6,512]{2,1,0:T(8,128)(2,1)S(1)} async-done(((bf16[16,6,512]{2,1,0:T(8,128)(2,1)}), bf16[16,6,512]{2,1,0:T(8,128)(2,1)S(1)}, u32[]{:S(2)}, u32[]{:S(2)}) %all-to-all-start) | async-done | bytes 98336 | tf_op jit(solution)/shard_map/all_to_all | solution.py:176
  78.1 1.3 %fusion.4 = f32[96,2048]{1,0:T(8,128)S(1)} fusion(bf16[128,2048]{1,0:T(8,128)(2,1)S(1)} %copy-done.1, bf16[96,512]{1,0:T(8,128)(2,1)S(1)} %select_n.306, bf16[1,512,128]{2,1,0:T(8,128)(2,1)} %param.20), kind=kOutput, calls=%fused_computation.15 | convolution fusion | flops 62926848 | bytes 1540096 | tf_op jit(solution)/shard_map/dot_general | solution.py:192
  79.5 2.9 %collective-permute-start.6 = (bf16[48,2048]{1,0:T(8,128)(2,1)S(1)}, bf16[48,2048]{1,0:T(8,128)(2,1)S(1)}, u32[]{:S(2)}, u32[]{:S(2)}) collective-permute-start(bf16[48,2048]{1,0:T(8,128)(2,1)S(1)} %select_convert_fusion.1), channel_id=1, source_target_pairs={{0,32},{1,481},{2,34},{3,483},{4,36},{5,485},{6,38},{7,487},{8,40}... | collective-permute-start | bytes 589832 | tf_op jit(solution)/shard_map/ppermute | solution.py:206
  82.4 4.6 %collective-permute-done.6 = bf16[48,2048]{1,0:T(8,128)(2,1)S(1)} collective-permute-done((bf16[48,2048]{1,0:T(8,128)(2,1)S(1)}, bf16[48,2048]{1,0:T(8,128)(2,1)S(1)}, u32[]{:S(2)}, u32[]{:S(2)}) %collective-permute-start.6) | collective-permute-done | bytes 196640 | tf_op jit(solution)/shard_map/ppermute | solution.py:206
  87.1 3.2 %collective-permute-start.7 = (bf16[24,2048]{1,0:T(8,128)(2,1)S(1)}, bf16[24,2048]{1,0:T(8,128)(2,1)S(1)}, u32[]{:S(2)}, u32[]{:S(2)}) collective-permute-start(bf16[24,2048]{1,0:T(8,128)(2,1)S(1)} %select_convert_fusion.3), channel_id=1, source_target_pairs={{0,64},{1,449},{2,66},{3,451},{4,68},{5,453},{6,70},{7,455},{8,72}... | collective-permute-start | bytes 294920 | tf_op jit(solution)/shard_map/ppermute | solution.py:206
  90.5 5.1 %collective-permute-done.7 = bf16[24,2048]{1,0:T(8,128)(2,1)S(1)} collective-permute-done((bf16[24,2048]{1,0:T(8,128)(2,1)S(1)}, bf16[24,2048]{1,0:T(8,128)(2,1)S(1)}, u32[]{:S(2)}, u32[]{:S(2)}) %collective-permute-start.7) | collective-permute-done | bytes 98336 | tf_op jit(solution)/shard_map/ppermute | solution.py:206
  95.7 3.5 %collective-permute-start.8 = (bf16[6,2048]{1,0:T(8,128)(2,1)S(1)}, bf16[6,2048]{1,0:T(8,128)(2,1)S(1)}, u32[]{:S(2)}, u32[]{:S(2)}) collective-permute-start(bf16[6,2048]{1,0:T(8,128)(2,1)S(1)} %get-tuple-element.26), channel_id=1, source_target_pairs={{0,128},{32,160},{64,192},{96,224},{128,256},{160,288},{192,320},{... | collective-permute-start | bytes 73736 | tf_op jit(solution)/shard_map/ppermute | solution.py:25
  99.2 6.3 %collective-permute-start.10 = (bf16[6,2048]{1,0:T(8,128)(2,1)S(1)}, bf16[6,2048]{1,0:T(8,128)(2,1)S(1)}, u32[]{:S(2)}, u32[]{:S(2)}) collective-permute-start(bf16[6,2048]{1,0:T(8,128)(2,1)S(1)} %get-tuple-element.27), channel_id=1, source_target_pairs={{0,384},{32,416},{64,448},{96,480},{128,0},{160,32},{192,64},{224,... | collective-permute-start | bytes 73736 | tf_op jit(solution)/shard_map/ppermute | solution.py:25
  105.5 4.2 %collective-permute-start.9 = (bf16[6,2048]{1,0:T(8,128)(2,1)S(1)}, bf16[6,2048]{1,0:T(8,128)(2,1)S(1)}, u32[]{:S(2)}, u32[]{:S(2)}) collective-permute-start(bf16[6,2048]{1,0:T(8,128)(2,1)S(1)} %get-tuple-element.28), channel_id=1, source_target_pairs={{0,256},{32,288},{64,320},{96,352},{128,384},{160,416},{192,448},{... | collective-permute-start | bytes 73736 | tf_op jit(solution)/shard_map/ppermute | solution.py:25
  109.7 11.3 %collective-permute-done.9 = bf16[6,2048]{1,0:T(8,128)(2,1)S(1)} collective-permute-done((bf16[6,2048]{1,0:T(8,128)(2,1)S(1)}, bf16[6,2048]{1,0:T(8,128)(2,1)S(1)}, u32[]{:S(2)}, u32[]{:S(2)}) %collective-permute-start.9) | collective-permute-done | bytes 24608 | tf_op jit(solution)/shard_map/ppermute | solution.py:25
  (86 shorter events, 13.0 us)
Async XLA Ops:
  0.0 21.7 %copy-start = (bf16[16,512,128]{2,1,0:T(8,128)(2,1)S(1)}, bf16[16,512,128]{2,1,0:T(8,128)(2,1)}, u32[]{:S(2)}) copy-start(bf16[16,512,128]{2,1,0:T(8,128)(2,1)} %param.19) | copy-start | bytes 6291460
  1.6 9.8 %collective-permute-start = (bf16[6,3072]{1,0:T(8,128)(2,1)S(1)}, bf16[6,3072]{1,0:T(8,128)(2,1)S(1)}, u32[]{:S(2)}, u32[]{:S(2)}) collective-permute-start(bf16[6,3072]{1,0:T(8,128)(2,1)S(1)} %constant_dynamic-update-slice_fusion), channel_id=1, source_target_pairs={{0,4},{4,0},{1,5},{5,1},{2,6},{6,2},{3,7},{7,3},{8,12},{12,8},{9,1... | collective-permute-start | bytes 110600 | tf_op jit(solution)/shard_map/ppermute | solution.py:19
  11.5 6.5 %collective-permute-start.1 = (bf16[12,3072]{1,0:T(8,128)(2,1)S(1)}, bf16[12,3072]{1,0:T(8,128)(2,1)S(1)}, u32[]{:S(2)}, u32[]{:S(2)}) collective-permute-start(bf16[12,3072]{1,0:T(8,128)(2,1)S(1)} %pad_maximum_fusion.7), channel_id=1, source_target_pairs={{0,2},{2,0},{1,3},{3,1},{4,6},{6,4},{5,7},{7,5},{8,10},{10,8},{9,1... | collective-permute-start | bytes 221192 | tf_op jit(solution)/shard_map/ppermute | solution.py:19
  18.1 3.3 %collective-permute-start.2 = (bf16[24,3072]{1,0:T(8,128)(2,1)S(1)}, bf16[24,3072]{1,0:T(8,128)(2,1)S(1)}, u32[]{:S(2)}, u32[]{:S(2)}) collective-permute-start(bf16[24,3072]{1,0:T(8,128)(2,1)S(1)} %pad_maximum_fusion.4), channel_id=1, source_target_pairs={{0,1},{1,0},{2,3},{3,2},{4,5},{5,4},{6,7},{7,6},{8,9},{9,8},{10,11... | collective-permute-start | bytes 442376 | tf_op jit(solution)/shard_map/ppermute | solution.py:19
  21.7 1.1 copy-start.3
  21.7 1.1 copy-start.4
  25.9 3.7 %collective-permute-start.3 = (bf16[408,512]{1,0:T(8,128)(2,1)S(1)}, bf16[408,512]{1,0:T(8,128)(2,1)S(1)}, u32[]{:S(2)}, u32[]{:S(2)}) collective-permute-start(bf16[408,512]{1,0:T(8,128)(2,1)S(1)} %pad_maximum_fusion.2), channel_id=1, source_target_pairs={{0,1},{1,0},{2,3},{3,2},{4,5},{5,4},{6,7},{7,6},{8,9},{9,8},{10,11... | collective-permute-start | bytes 1253384 | tf_op jit(solution)/shard_map/ppermute | solution.py:19
  30.1 33.9 %copy-start.2 = (s32[16]{0:T(128)S(1)}, s32[16]{0:T(128)}, u32[]{:S(2)}) copy-start(s32[16]{0:T(128)} %constant.173.clone) | copy-start | bytes 196
  30.2 9.2 %collective-permute-start.4 = (bf16[204,512]{1,0:T(8,128)(2,1)S(1)}, bf16[204,512]{1,0:T(8,128)(2,1)S(1)}, u32[]{:S(2)}, u32[]{:S(2)}) collective-permute-start(bf16[204,512]{1,0:T(8,128)(2,1)S(1)} %pad_maximum_fusion.3), channel_id=1, source_target_pairs={{0,2},{2,0},{1,3},{3,1},{4,6},{6,4},{5,7},{7,5},{8,10},{10,8},{9,1... | collective-permute-start | bytes 626696 | tf_op jit(solution)/shard_map/ppermute | solution.py:19
  39.5 38.6 %copy-start.1 = (bf16[128,2048]{1,0:T(8,128)(2,1)S(1)}, bf16[128,2048]{1,0:T(8,128)(2,1)}, u32[]{:S(2)}) copy-start(bf16[128,2048]{1,0:T(8,128)(2,1)} %param.21) | copy-start | bytes 1572868
  39.8 8.1 %collective-permute-start.5 = (bf16[102,512]{1,0:T(8,128)(2,1)S(1)}, bf16[102,512]{1,0:T(8,128)(2,1)S(1)}, u32[]{:S(2)}, u32[]{:S(2)}) collective-permute-start(bf16[102,512]{1,0:T(8,128)(2,1)S(1)} %pad_maximum_fusion.5), channel_id=1, source_target_pairs={{0,4},{4,0},{1,5},{5,1},{2,6},{6,2},{3,7},{7,3},{8,12},{12,8},{9,1... | collective-permute-start | bytes 313352 | tf_op jit(solution)/shard_map/ppermute | solution.py:19
  48.8 28.6 %all-to-all-start = ((bf16[16,6,512]{2,1,0:T(8,128)(2,1)}), bf16[16,6,512]{2,1,0:T(8,128)(2,1)S(1)}, u32[]{:S(2)}, u32[]{:S(2)}) async-start(bf16[16,6,512]{2,1,0:T(8,128)(2,1)} %copy.49), calls=%async_computation | async-start | bytes 262144 | tf_op jit(solution)/shard_map/all_to_all | solution.py:176
  79.5 7.6 %collective-permute-start.6 = (bf16[48,2048]{1,0:T(8,128)(2,1)S(1)}, bf16[48,2048]{1,0:T(8,128)(2,1)S(1)}, u32[]{:S(2)}, u32[]{:S(2)}) collective-permute-start(bf16[48,2048]{1,0:T(8,128)(2,1)S(1)} %select_convert_fusion.1), channel_id=1, source_target_pairs={{0,32},{1,481},{2,34},{3,483},{4,36},{5,485},{6,38},{7,487},{8,40}... | collective-permute-start | bytes 589832 | tf_op jit(solution)/shard_map/ppermute | solution.py:206
  87.1 8.5 %collective-permute-start.7 = (bf16[24,2048]{1,0:T(8,128)(2,1)S(1)}, bf16[24,2048]{1,0:T(8,128)(2,1)S(1)}, u32[]{:S(2)}, u32[]{:S(2)}) collective-permute-start(bf16[24,2048]{1,0:T(8,128)(2,1)S(1)} %select_convert_fusion.3), channel_id=1, source_target_pairs={{0,64},{1,449},{2,66},{3,451},{4,68},{5,453},{6,70},{7,455},{8,72}... | collective-permute-start | bytes 294920 | tf_op jit(solution)/shard_map/ppermute | solution.py:206
  95.7 14.0 %collective-permute-start.8 = (bf16[6,2048]{1,0:T(8,128)(2,1)S(1)}, bf16[6,2048]{1,0:T(8,128)(2,1)S(1)}, u32[]{:S(2)}, u32[]{:S(2)}) collective-permute-start(bf16[6,2048]{1,0:T(8,128)(2,1)S(1)} %get-tuple-element.26), channel_id=1, source_target_pairs={{0,128},{32,160},{64,192},{96,224},{128,256},{160,288},{192,320},{... | collective-permute-start | bytes 73736 | tf_op jit(solution)/shard_map/ppermute | solution.py:25
  99.2 10.5 %collective-permute-start.10 = (bf16[6,2048]{1,0:T(8,128)(2,1)S(1)}, bf16[6,2048]{1,0:T(8,128)(2,1)S(1)}, u32[]{:S(2)}, u32[]{:S(2)}) collective-permute-start(bf16[6,2048]{1,0:T(8,128)(2,1)S(1)} %get-tuple-element.27), channel_id=1, source_target_pairs={{0,384},{32,416},{64,448},{96,480},{128,0},{160,32},{192,64},{224,... | collective-permute-start | bytes 73736 | tf_op jit(solution)/shard_map/ppermute | solution.py:25
  105.5 15.6 %collective-permute-start.9 = (bf16[6,2048]{1,0:T(8,128)(2,1)S(1)}, bf16[6,2048]{1,0:T(8,128)(2,1)S(1)}, u32[]{:S(2)}, u32[]{:S(2)}) collective-permute-start(bf16[6,2048]{1,0:T(8,128)(2,1)S(1)} %get-tuple-element.28), channel_id=1, source_target_pairs={{0,256},{32,288},{64,320},{96,352},{128,384},{160,416},{192,448},{... | collective-permute-start | bytes 73736 | tf_op jit(solution)/shard_map/ppermute | solution.py:25

commit v7 on v5

--- a/solution.py
+++ b/solution.py
@@ -173,9 +173,8 @@
         state = combine_parts(kept_part, unpack_part(received, head_count))
     merged_sum, merged_high, merged_total = state
     merged = merged_sum / merged_total[..., None]
-    spread = lax.all_to_all(
-        jnp.swapaxes(merged.astype(jnp.bfloat16), 0, 1), "grp", split_axis=0, concat_axis=0, tiled=True
-    )
+    chunk = jnp.swapaxes(merged.astype(jnp.bfloat16), 0, 1).reshape(grp_size, -1, 128)
+    spread = lax.all_to_all(chunk, "grp", split_axis=0, concat_axis=0, tiled=True)
     spread = spread.reshape(grp_size, token_count, latent_width)[jnp.array(bit_reversed(grp_size))]
     head_rows = jnp.dot(
         spread.reshape(grp_size * token_count, latent_width),

time: 122 us -> 122 us (level)
  no operation moved by 1% of the time
where the time goes in v7:
time: 122 us; the launch traced here: 121 us
  waiting for transfers between devices  52.2 us (43%)
  starting transfers between devices  51.7 us (42%)
  local copies, waits for them, and re-layouts  6.17 us (5%)
  other arithmetic  5.4 us (4%)
  matrix products  5.14 us (4%)
    ppermute x8, waiting for transfers between devices, from_partner(): return lax.ppermute(block, axis, route)  27.4 us
    ppermute x8, starting transfers between devices, from_partner(): return lax.ppermute(block, axis, route)  23 us
    all_to_all x1, starting transfers between devices, per_device(): lax.all_to_all(chunk, 'grp', split_axis=0, concat_axis=0, tiled=True)  15.2 us
    ppermute x3, starting transfers between devices, shifted(): return lax.ppermute(block, axis, route)  13.6 us
    all_to_all x1, waiting for transfers between devices, per_device(): lax.all_to_all(chunk, 'grp', split_axis=0, concat_axis=0, tiled=True)  13.1 us
    ppermute x3, waiting for transfers between devices, shifted(): return lax.ppermute(block, axis, route)  11.7 us
  transfers between devices with their start and end apart: 12, of which 9 were waited for; matrix products, arithmetic and copies ran while one was open for 5% of the time, Pallas kernels for 0%

profile of v7, /device:TPU:6, one launch (start us, length us, event | category | flops | bytes accessed | tf_op | source)
XLA Modules:
  0.0 121.4 jit_solution(16114028932068358849)
XLA Ops:
  1.6 5.1 %collective-permute-start = (bf16[6,3072]{1,0:T(8,128)(2,1)S(1)}, bf16[6,3072]{1,0:T(8,128)(2,1)S(1)}, u32[]{:S(2)}, u32[]{:S(2)}) collective-permute-start(bf16[6,3072]{1,0:T(8,128)(2,1)S(1)} %constant_dynamic-update-slice_fusion), channel_id=1, source_target_pairs={{0,4},{4,0},{1,5},{5,1},{2,6},{6,2},{3,7},{7,3},{8,12},{12,8},{9,1... | collective-permute-start | bytes 110600 | tf_op jit(solution)/shard_map/ppermute | solution.py:19
  6.8 1.2 %dynamic_slice.24 = s32[1]{0:T(128)} dynamic-slice(s32[4]{0:T(128)} %param.17, s32[]{:T(128)S(6)} %select_n.241), dynamic_slice_sizes={1} | dynamic-slice | bytes 12 | tf_op jit(solution)/shard_map/jit(dynamic_index_in_dim)/dynamic_slice | solution.py:135
  11.5 2.6 %collective-permute-start.1 = (bf16[12,3072]{1,0:T(8,128)(2,1)S(1)}, bf16[12,3072]{1,0:T(8,128)(2,1)S(1)}, u32[]{:S(2)}, u32[]{:S(2)}) collective-permute-start(bf16[12,3072]{1,0:T(8,128)(2,1)S(1)} %pad_maximum_fusion.7), channel_id=1, source_target_pairs={{0,2},{2,0},{1,3},{3,1},{4,6},{6,4},{5,7},{7,5},{8,10},{10,8},{9,1... | collective-permute-start | bytes 221192 | tf_op jit(solution)/shard_map/ppermute | solution.py:19
  15.4 2.7 %collective-permute-done.1 = bf16[12,3072]{1,0:T(8,128)(2,1)S(1)} collective-permute-done((bf16[12,3072]{1,0:T(8,128)(2,1)S(1)}, bf16[12,3072]{1,0:T(8,128)(2,1)S(1)}, u32[]{:S(2)}, u32[]{:S(2)}) %collective-permute-start.1) | collective-permute-done | bytes 73760 | tf_op jit(solution)/shard_map/ppermute | solution.py:19
  18.1 1.9 %collective-permute-start.2 = (bf16[24,3072]{1,0:T(8,128)(2,1)S(1)}, bf16[24,3072]{1,0:T(8,128)(2,1)S(1)}, u32[]{:S(2)}, u32[]{:S(2)}) collective-permute-start(bf16[24,3072]{1,0:T(8,128)(2,1)S(1)} %pad_maximum_fusion.4), channel_id=1, source_target_pairs={{0,1},{1,0},{2,3},{3,2},{4,5},{5,4},{6,7},{7,6},{8,9},{9,8},{10,11... | collective-permute-start | bytes 442376 | tf_op jit(solution)/shard_map/ppermute | solution.py:19
  20.1 1.3 %collective-permute-done.2 = bf16[24,3072]{1,0:T(8,128)(2,1)S(1)} collective-permute-done((bf16[24,3072]{1,0:T(8,128)(2,1)S(1)}, bf16[24,3072]{1,0:T(8,128)(2,1)S(1)}, u32[]{:S(2)}, u32[]{:S(2)}) %collective-permute-start.2) | collective-permute-done | bytes 147488 | tf_op jit(solution)/shard_map/ppermute | solution.py:19
  22.8 1.1 fusion
  25.9 2.0 %collective-permute-start.3 = (bf16[408,512]{1,0:T(8,128)(2,1)S(1)}, bf16[408,512]{1,0:T(8,128)(2,1)S(1)}, u32[]{:S(2)}, u32[]{:S(2)}) collective-permute-start(bf16[408,512]{1,0:T(8,128)(2,1)S(1)} %pad_maximum_fusion.2), channel_id=1, source_target_pairs={{0,1},{1,0},{2,3},{3,2},{4,5},{5,4},{6,7},{7,6},{8,9},{9,8},{10,11... | collective-permute-start | bytes 1253384 | tf_op jit(solution)/shard_map/ppermute | solution.py:19
  28.0 1.6 %collective-permute-done.3 = bf16[408,512]{1,0:T(8,128)(2,1)S(1)} collective-permute-done((bf16[408,512]{1,0:T(8,128)(2,1)S(1)}, bf16[408,512]{1,0:T(8,128)(2,1)S(1)}, u32[]{:S(2)}, u32[]{:S(2)}) %collective-permute-start.3) | collective-permute-done | bytes 417824 | tf_op jit(solution)/shard_map/ppermute | solution.py:19
  30.1 2.6 %collective-permute-start.4 = (bf16[204,512]{1,0:T(8,128)(2,1)S(1)}, bf16[204,512]{1,0:T(8,128)(2,1)S(1)}, u32[]{:S(2)}, u32[]{:S(2)}) collective-permute-start(bf16[204,512]{1,0:T(8,128)(2,1)S(1)} %pad_maximum_fusion.3), channel_id=1, source_target_pairs={{0,2},{2,0},{1,3},{3,1},{4,6},{6,4},{5,7},{7,5},{8,10},{10,8},{9,1... | collective-permute-start | bytes 626696 | tf_op jit(solution)/shard_map/ppermute | solution.py:19
  32.7 6.6 %collective-permute-done.4 = bf16[204,512]{1,0:T(8,128)(2,1)S(1)} collective-permute-done((bf16[204,512]{1,0:T(8,128)(2,1)S(1)}, bf16[204,512]{1,0:T(8,128)(2,1)S(1)}, u32[]{:S(2)}, u32[]{:S(2)}) %collective-permute-start.4) | collective-permute-done | bytes 208928 | tf_op jit(solution)/shard_map/ppermute | solution.py:19
  39.8 2.8 %collective-permute-start.5 = (bf16[102,512]{1,0:T(8,128)(2,1)S(1)}, bf16[102,512]{1,0:T(8,128)(2,1)S(1)}, u32[]{:S(2)}, u32[]{:S(2)}) collective-permute-start(bf16[102,512]{1,0:T(8,128)(2,1)S(1)} %pad_maximum_fusion.5), channel_id=1, source_target_pairs={{0,4},{4,0},{1,5},{5,1},{2,6},{6,2},{3,7},{7,3},{8,12},{12,8},{9,1... | collective-permute-start | bytes 313352 | tf_op jit(solution)/shard_map/ppermute | solution.py:19
  42.5 5.3 %collective-permute-done.5 = bf16[102,512]{1,0:T(8,128)(2,1)S(1)} collective-permute-done((bf16[102,512]{1,0:T(8,128)(2,1)S(1)}, bf16[102,512]{1,0:T(8,128)(2,1)S(1)}, u32[]{:S(2)}, u32[]{:S(2)}) %collective-permute-start.5) | collective-permute-done | bytes 104480 | tf_op jit(solution)/shard_map/ppermute | solution.py:19
  48.9 15.2 %all-to-all-start = ((bf16[16,24,128]{2,1,0:T(8,128)(2,1)}), bf16[16,24,128]{2,1,0:T(8,128)(2,1)S(1)}, u32[]{:S(2)}, u32[]{:S(2)}) async-start(bf16[16,24,128]{2,1,0:T(8,128)(2,1)} %reshape.93), calls=%async_computation | async-start | bytes 196608 | tf_op jit(solution)/shard_map/all_to_all | solution.py:177
  64.1 13.1 %all-to-all-done = bf16[16,24,128]{2,1,0:T(8,128)(2,1)S(1)} async-done(((bf16[16,24,128]{2,1,0:T(8,128)(2,1)}), bf16[16,24,128]{2,1,0:T(8,128)(2,1)S(1)}, u32[]{:S(2)}, u32[]{:S(2)}) %all-to-all-start) | async-done | bytes 98336 | tf_op jit(solution)/shard_map/all_to_all | solution.py:177
  77.9 1.3 %fusion.4 = f32[96,2048]{1,0:T(8,128)S(1)} fusion(bf16[128,2048]{1,0:T(8,128)(2,1)S(1)} %copy-done.1, bf16[96,512]{1,0:T(8,128)(2,1)S(1)} %reshape.95, bf16[1,512,128]{2,1,0:T(8,128)(2,1)} %param.20), kind=kOutput, calls=%fused_computation.15 | convolution fusion | flops 62926848 | bytes 1540096 | tf_op jit(solution)/shard_map/dot_general | solution.py:184
  79.2 2.9 %collective-permute-start.6 = (bf16[48,2048]{1,0:T(8,128)(2,1)S(1)}, bf16[48,2048]{1,0:T(8,128)(2,1)S(1)}, u32[]{:S(2)}, u32[]{:S(2)}) collective-permute-start(bf16[48,2048]{1,0:T(8,128)(2,1)S(1)} %select_convert_fusion.1), channel_id=1, source_target_pairs={{0,32},{32,0},{64,96},{96,64},{128,160},{160,128},{192,224},{224,1... | collective-permute-start | bytes 589832 | tf_op jit(solution)/shard_map/ppermute | solution.py:19
  82.2 4.6 %collective-permute-done.6 = bf16[48,2048]{1,0:T(8,128)(2,1)S(1)} collective-permute-done((bf16[48,2048]{1,0:T(8,128)(2,1)S(1)}, bf16[48,2048]{1,0:T(8,128)(2,1)S(1)}, u32[]{:S(2)}, u32[]{:S(2)}) %collective-permute-start.6) | collective-permute-done | bytes 196640 | tf_op jit(solution)/shard_map/ppermute | solution.py:19
  86.9 3.0 %collective-permute-start.7 = (bf16[24,2048]{1,0:T(8,128)(2,1)S(1)}, bf16[24,2048]{1,0:T(8,128)(2,1)S(1)}, u32[]{:S(2)}, u32[]{:S(2)}) collective-permute-start(bf16[24,2048]{1,0:T(8,128)(2,1)S(1)} %select_convert_fusion.3), channel_id=1, source_target_pairs={{0,64},{64,0},{32,96},{96,32},{128,192},{192,128},{160,224},{224,1... | collective-permute-start | bytes 294920 | tf_op jit(solution)/shard_map/ppermute | solution.py:19
  90.1 5.3 %collective-permute-done.7 = bf16[24,2048]{1,0:T(8,128)(2,1)S(1)} collective-permute-done((bf16[24,2048]{1,0:T(8,128)(2,1)S(1)}, bf16[24,2048]{1,0:T(8,128)(2,1)S(1)}, u32[]{:S(2)}, u32[]{:S(2)}) %collective-permute-start.7) | collective-permute-done | bytes 98336 | tf_op jit(solution)/shard_map/ppermute | solution.py:19
  95.5 3.5 %collective-permute-start.8 = (bf16[6,2048]{1,0:T(8,128)(2,1)S(1)}, bf16[6,2048]{1,0:T(8,128)(2,1)S(1)}, u32[]{:S(2)}, u32[]{:S(2)}) collective-permute-start(bf16[6,2048]{1,0:T(8,128)(2,1)S(1)} %get-tuple-element.24), channel_id=1, source_target_pairs={{0,128},{32,160},{64,192},{96,224},{128,256},{160,288},{192,320},{... | collective-permute-start | bytes 73736 | tf_op jit(solution)/shard_map/ppermute | solution.py:25
  99.0 6.3 %collective-permute-start.10 = (bf16[6,2048]{1,0:T(8,128)(2,1)S(1)}, bf16[6,2048]{1,0:T(8,128)(2,1)S(1)}, u32[]{:S(2)}, u32[]{:S(2)}) collective-permute-start(bf16[6,2048]{1,0:T(8,128)(2,1)S(1)} %get-tuple-element.25), channel_id=1, source_target_pairs={{0,384},{32,416},{64,448},{96,480},{128,0},{160,32},{192,64},{224,... | collective-permute-start | bytes 73736 | tf_op jit(solution)/shard_map/ppermute | solution.py:25
  105.2 3.8 %collective-permute-start.9 = (bf16[6,2048]{1,0:T(8,128)(2,1)S(1)}, bf16[6,2048]{1,0:T(8,128)(2,1)S(1)}, u32[]{:S(2)}, u32[]{:S(2)}) collective-permute-start(bf16[6,2048]{1,0:T(8,128)(2,1)S(1)} %get-tuple-element.26), channel_id=1, source_target_pairs={{0,256},{32,288},{64,320},{96,352},{128,384},{160,416},{192,448},{... | collective-permute-start | bytes 73736 | tf_op jit(solution)/shard_map/ppermute | solution.py:25
  109.1 11.7 %collective-permute-done.9 = bf16[6,2048]{1,0:T(8,128)(2,1)S(1)} collective-permute-done((bf16[6,2048]{1,0:T(8,128)(2,1)S(1)}, bf16[6,2048]{1,0:T(8,128)(2,1)S(1)}, u32[]{:S(2)}, u32[]{:S(2)}) %collective-permute-start.9) | collective-permute-done | bytes 24608 | tf_op jit(solution)/shard_map/ppermute | solution.py:25
  (86 shorter events, 13.0 us)
Async XLA Ops:
  0.0 21.7 %copy-start = (bf16[16,512,128]{2,1,0:T(8,128)(2,1)S(1)}, bf16[16,512,128]{2,1,0:T(8,128)(2,1)}, u32[]{:S(2)}) copy-start(bf16[16,512,128]{2,1,0:T(8,128)(2,1)} %param.19) | copy-start | bytes 6291460
  1.6 9.8 %collective-permute-start = (bf16[6,3072]{1,0:T(8,128)(2,1)S(1)}, bf16[6,3072]{1,0:T(8,128)(2,1)S(1)}, u32[]{:S(2)}, u32[]{:S(2)}) collective-permute-start(bf16[6,3072]{1,0:T(8,128)(2,1)S(1)} %constant_dynamic-update-slice_fusion), channel_id=1, source_target_pairs={{0,4},{4,0},{1,5},{5,1},{2,6},{6,2},{3,7},{7,3},{8,12},{12,8},{9,1... | collective-permute-start | bytes 110600 | tf_op jit(solution)/shard_map/ppermute | solution.py:19
  11.5 6.5 %collective-permute-start.1 = (bf16[12,3072]{1,0:T(8,128)(2,1)S(1)}, bf16[12,3072]{1,0:T(8,128)(2,1)S(1)}, u32[]{:S(2)}, u32[]{:S(2)}) collective-permute-start(bf16[12,3072]{1,0:T(8,128)(2,1)S(1)} %pad_maximum_fusion.7), channel_id=1, source_target_pairs={{0,2},{2,0},{1,3},{3,1},{4,6},{6,4},{5,7},{7,5},{8,10},{10,8},{9,1... | collective-permute-start | bytes 221192 | tf_op jit(solution)/shard_map/ppermute | solution.py:19
  18.1 3.3 %collective-permute-start.2 = (bf16[24,3072]{1,0:T(8,128)(2,1)S(1)}, bf16[24,3072]{1,0:T(8,128)(2,1)S(1)}, u32[]{:S(2)}, u32[]{:S(2)}) collective-permute-start(bf16[24,3072]{1,0:T(8,128)(2,1)S(1)} %pad_maximum_fusion.4), channel_id=1, source_target_pairs={{0,1},{1,0},{2,3},{3,2},{4,5},{5,4},{6,7},{7,6},{8,9},{9,8},{10,11... | collective-permute-start | bytes 442376 | tf_op jit(solution)/shard_map/ppermute | solution.py:19
  21.7 1.1 copy-start.3
  21.7 1.1 copy-start.4
  25.9 3.7 %collective-permute-start.3 = (bf16[408,512]{1,0:T(8,128)(2,1)S(1)}, bf16[408,512]{1,0:T(8,128)(2,1)S(1)}, u32[]{:S(2)}, u32[]{:S(2)}) collective-permute-start(bf16[408,512]{1,0:T(8,128)(2,1)S(1)} %pad_maximum_fusion.2), channel_id=1, source_target_pairs={{0,1},{1,0},{2,3},{3,2},{4,5},{5,4},{6,7},{7,6},{8,9},{9,8},{10,11... | collective-permute-start | bytes 1253384 | tf_op jit(solution)/shard_map/ppermute | solution.py:19
  30.1 9.2 %collective-permute-start.4 = (bf16[204,512]{1,0:T(8,128)(2,1)S(1)}, bf16[204,512]{1,0:T(8,128)(2,1)S(1)}, u32[]{:S(2)}, u32[]{:S(2)}) collective-permute-start(bf16[204,512]{1,0:T(8,128)(2,1)S(1)} %pad_maximum_fusion.3), channel_id=1, source_target_pairs={{0,2},{2,0},{1,3},{3,1},{4,6},{6,4},{5,7},{7,5},{8,10},{10,8},{9,1... | collective-permute-start | bytes 626696 | tf_op jit(solution)/shard_map/ppermute | solution.py:19
  39.4 24.6 %copy-start.2 = (s32[16]{0:T(128)S(1)}, s32[16]{0:T(128)}, u32[]{:S(2)}) copy-start(s32[16]{0:T(128)} %constant.169) | copy-start | bytes 196
  39.5 38.4 %copy-start.1 = (bf16[128,2048]{1,0:T(8,128)(2,1)S(1)}, bf16[128,2048]{1,0:T(8,128)(2,1)}, u32[]{:S(2)}) copy-start(bf16[128,2048]{1,0:T(8,128)(2,1)} %param.21) | copy-start | bytes 1572868
  39.8 8.1 %collective-permute-start.5 = (bf16[102,512]{1,0:T(8,128)(2,1)S(1)}, bf16[102,512]{1,0:T(8,128)(2,1)S(1)}, u32[]{:S(2)}, u32[]{:S(2)}) collective-permute-start(bf16[102,512]{1,0:T(8,128)(2,1)S(1)} %pad_maximum_fusion.5), channel_id=1, source_target_pairs={{0,4},{4,0},{1,5},{5,1},{2,6},{6,2},{3,7},{7,3},{8,12},{12,8},{9,1... | collective-permute-start | bytes 313352 | tf_op jit(solution)/shard_map/ppermute | solution.py:19
  48.9 28.3 %all-to-all-start = ((bf16[16,24,128]{2,1,0:T(8,128)(2,1)}), bf16[16,24,128]{2,1,0:T(8,128)(2,1)S(1)}, u32[]{:S(2)}, u32[]{:S(2)}) async-start(bf16[16,24,128]{2,1,0:T(8,128)(2,1)} %reshape.93), calls=%async_computation | async-start | bytes 196608 | tf_op jit(solution)/shard_map/all_to_all | solution.py:177
  79.2 7.6 %collective-permute-start.6 = (bf16[48,2048]{1,0:T(8,128)(2,1)S(1)}, bf16[48,2048]{1,0:T(8,128)(2,1)S(1)}, u32[]{:S(2)}, u32[]{:S(2)}) collective-permute-start(bf16[48,2048]{1,0:T(8,128)(2,1)S(1)} %select_convert_fusion.1), channel_id=1, source_target_pairs={{0,32},{32,0},{64,96},{96,64},{128,160},{160,128},{192,224},{224,1... | collective-permute-start | bytes 589832 | tf_op jit(solution)/shard_map/ppermute | solution.py:19
  86.9 8.5 %collective-permute-start.7 = (bf16[24,2048]{1,0:T(8,128)(2,1)S(1)}, bf16[24,2048]{1,0:T(8,128)(2,1)S(1)}, u32[]{:S(2)}, u32[]{:S(2)}) collective-permute-start(bf16[24,2048]{1,0:T(8,128)(2,1)S(1)} %select_convert_fusion.3), channel_id=1, source_target_pairs={{0,64},{64,0},{32,96},{96,32},{128,192},{192,128},{160,224},{224,1... | collective-permute-start | bytes 294920 | tf_op jit(solution)/shard_map/ppermute | solution.py:19
  95.5 13.6 %collective-permute-start.8 = (bf16[6,2048]{1,0:T(8,128)(2,1)S(1)}, bf16[6,2048]{1,0:T(8,128)(2,1)S(1)}, u32[]{:S(2)}, u32[]{:S(2)}) collective-permute-start(bf16[6,2048]{1,0:T(8,128)(2,1)S(1)} %get-tuple-element.24), channel_id=1, source_target_pairs={{0,128},{32,160},{64,192},{96,224},{128,256},{160,288},{192,320},{... | collective-permute-start | bytes 73736 | tf_op jit(solution)/shard_map/ppermute | solution.py:25
  99.0 10.1 %collective-permute-start.10 = (bf16[6,2048]{1,0:T(8,128)(2,1)S(1)}, bf16[6,2048]{1,0:T(8,128)(2,1)S(1)}, u32[]{:S(2)}, u32[]{:S(2)}) collective-permute-start(bf16[6,2048]{1,0:T(8,128)(2,1)S(1)} %get-tuple-element.25), channel_id=1, source_target_pairs={{0,384},{32,416},{64,448},{96,480},{128,0},{160,32},{192,64},{224,... | collective-permute-start | bytes 73736 | tf_op jit(solution)/shard_map/ppermute | solution.py:25
  105.2 15.6 %collective-permute-start.9 = (bf16[6,2048]{1,0:T(8,128)(2,1)S(1)}, bf16[6,2048]{1,0:T(8,128)(2,1)S(1)}, u32[]{:S(2)}, u32[]{:S(2)}) collective-permute-start(bf16[6,2048]{1,0:T(8,128)(2,1)S(1)} %get-tuple-element.26), channel_id=1, source_target_pairs={{0,256},{32,288},{64,320},{96,352},{128,384},{160,416},{192,448},{... | collective-permute-start | bytes 73736 | tf_op jit(solution)/shard_map/ppermute | solution.py:25

commit v8 on v5

--- a/solution.py
+++ b/solution.py
@@ -158,7 +158,7 @@
         preferred_element_type=jnp.float32,
     )
     state = (partial_value, highest, total)
-    for bit_level in range(doublings):
+    for bit_level in range(1):
         half_rows = state[0].shape[0] // 2
         upper_side = jnp.right_shift(position, bit_level) & 1 == 1
         lower_part = tuple((member[:half_rows] for member in state))
@@ -171,7 +171,27 @@
         )
         received = from_partner(pack_part(*sent_part, latent_width), "ep", bit_level)
         state = combine_parts(kept_part, unpack_part(received, head_count))
-    merged_sum, merged_high, merged_total = state
+    chips = per_request // 2
+    chip = local_rank // 2
+    chip_blocks = tuple(
+        member.reshape((chips, token_count) + member.shape[1:]) for member in state
+    )
+
+    def block_of(member_chip):
+        index = (member_chip & 1) * 2 + member_chip // 2
+        return tuple(lax.dynamic_index_in_dim(member, index, 0, keepdims=False) for member in chip_blocks)
+
+    parts = [block_of(chip)]
+    for step in range(1, chips):
+        sent = block_of((chip + step) % chips)
+        got = shifted(pack_part(*sent, latent_width), "ep", per_request, 2 * step)
+        parts.append(unpack_part(got, head_count))
+    merged_high = parts[0][1]
+    for part in parts[1:]:
+        merged_high = jnp.maximum(merged_high, part[1])
+    factors = [jnp.exp(part[1] - merged_high) for part in parts]
+    merged_sum = sum(part[0] * factor[..., None] for part, factor in zip(parts, factors))
+    merged_total = sum(part[2] * factor for part, factor in zip(parts, factors))
     merged = merged_sum / merged_total[..., None]
     spread = lax.all_to_all(
         jnp.swapaxes(merged.astype(jnp.bfloat16), 0, 1), "grp", split_axis=0, concat_axis=0, tiled=True

time: 122 us -> 123 us (level)
  waiting for transfers between devices: 51.9 us -> 45.6 us
  starting transfers between devices: 52.3 us -> 56.2 us
  other arithmetic: 5.4 us -> 7.59 us
    ppermute x8 -> x6, waiting for transfers between devices: 27.2 us -> 15.1 us  [from_partner(): return lax.ppermute(block, axis, route)]
    ppermute x3 -> x6, starting transfers between devices: 14 us -> 23.2 us  [shifted(): return lax.ppermute(block, axis, route)]
    ppermute x3 -> x6, waiting for transfers between devices: 11.3 us -> 17 us  [shifted(): return lax.ppermute(block, axis, route)]
    ppermute x8 -> x6, starting transfers between devices: 23.2 us -> 17.8 us  [from_partner(): return lax.ppermute(block, axis, route)]
  transfers between devices with their start and end apart: 12 -> 13, of which waited for: 9 -> 9; matrix products, arithmetic and copies ran while one was open for 5% -> 5% of each run, Pallas kernels for 0% -> 0%
where the time goes in v8:
time: 123 us; the launch traced here: 122 us
  starting transfers between devices  56.2 us (46%)
  waiting for transfers between devices  45.6 us (37%)
  other arithmetic  7.59 us (6%)
  local copies, waits for them, and re-layouts  6.98 us (6%)
  matrix products  5.15 us (4%)
    ppermute x6, starting transfers between devices, shifted(): return lax.ppermute(block, axis, route)  23.2 us
    ppermute x6, starting transfers between devices, from_partner(): return lax.ppermute(block, axis, route)  17.8 us
    ppermute x6, waiting for transfers between devices, shifted(): return lax.ppermute(block, axis, route)  17 us
    all_to_all x1, starting transfers between devices, per_device(): lax.all_to_all(jnp.swapaxes(merged.astype(jnp.bfloat16), 0, 1), 'grp', sp...  15.2 us
    ppermute x6, waiting for transfers between devices, from_partner(): return lax.ppermute(block, axis, route)  15.1 us
    all_to_all x1, waiting for transfers between devices, per_device(): lax.all_to_all(jnp.swapaxes(merged.astype(jnp.bfloat16), 0, 1), 'grp', sp...  13.4 us
  transfers between devices with their start and end apart: 13, of which 9 were waited for; matrix products, arithmetic and copies ran while one was open for 5% of the time, Pallas kernels for 0%

profile of v8, /device:TPU:6, one launch (start us, length us, event | category | flops | bytes accessed | tf_op | source)
XLA Modules:
  0.0 122.5 jit_solution(97382542198206477)
XLA Ops:
  1.6 5.1 %collective-permute-start = (bf16[6,3072]{1,0:T(8,128)(2,1)S(1)}, bf16[6,3072]{1,0:T(8,128)(2,1)S(1)}, u32[]{:S(2)}, u32[]{:S(2)}) collective-permute-start(bf16[6,3072]{1,0:T(8,128)(2,1)S(1)} %constant_dynamic-update-slice_fusion), channel_id=1, source_target_pairs={{0,4},{4,0},{1,5},{5,1},{2,6},{6,2},{3,7},{7,3},{8,12},{12,8},{9,1... | collective-permute-start | bytes 110600 | tf_op jit(solution)/shard_map/ppermute | solution.py:19
  6.8 1.2 %dynamic_slice.62 = s32[1]{0:T(128)} dynamic-slice(s32[4]{0:T(128)} %param.17, s32[]{:T(128)S(6)} %select_n.224), dynamic_slice_sizes={1} | dynamic-slice | bytes 12 | tf_op jit(solution)/shard_map/jit(dynamic_index_in_dim)/dynamic_slice | solution.py:135
  11.5 2.6 %collective-permute-start.1 = (bf16[12,3072]{1,0:T(8,128)(2,1)S(1)}, bf16[12,3072]{1,0:T(8,128)(2,1)S(1)}, u32[]{:S(2)}, u32[]{:S(2)}) collective-permute-start(bf16[12,3072]{1,0:T(8,128)(2,1)S(1)} %pad_maximum_fusion.8), channel_id=1, source_target_pairs={{0,2},{2,0},{1,3},{3,1},{4,6},{6,4},{5,7},{7,5},{8,10},{10,8},{9,1... | collective-permute-start | bytes 221192 | tf_op jit(solution)/shard_map/ppermute | solution.py:19
  15.4 2.7 %collective-permute-done.1 = bf16[12,3072]{1,0:T(8,128)(2,1)S(1)} collective-permute-done((bf16[12,3072]{1,0:T(8,128)(2,1)S(1)}, bf16[12,3072]{1,0:T(8,128)(2,1)S(1)}, u32[]{:S(2)}, u32[]{:S(2)}) %collective-permute-start.1) | collective-permute-done | bytes 73760 | tf_op jit(solution)/shard_map/ppermute | solution.py:19
  18.1 1.9 %collective-permute-start.2 = (bf16[24,3072]{1,0:T(8,128)(2,1)S(1)}, bf16[24,3072]{1,0:T(8,128)(2,1)S(1)}, u32[]{:S(2)}, u32[]{:S(2)}) collective-permute-start(bf16[24,3072]{1,0:T(8,128)(2,1)S(1)} %pad_maximum_fusion.3), channel_id=1, source_target_pairs={{0,1},{1,0},{2,3},{3,2},{4,5},{5,4},{6,7},{7,6},{8,9},{9,8},{10,11... | collective-permute-start | bytes 442376 | tf_op jit(solution)/shard_map/ppermute | solution.py:19
  20.1 1.3 %collective-permute-done.2 = bf16[24,3072]{1,0:T(8,128)(2,1)S(1)} collective-permute-done((bf16[24,3072]{1,0:T(8,128)(2,1)S(1)}, bf16[24,3072]{1,0:T(8,128)(2,1)S(1)}, u32[]{:S(2)}, u32[]{:S(2)}) %collective-permute-start.2) | collective-permute-done | bytes 147488 | tf_op jit(solution)/shard_map/ppermute | solution.py:19
  27.1 2.0 %collective-permute-start.3 = (bf16[408,512]{1,0:T(8,128)(2,1)S(1)}, bf16[408,512]{1,0:T(8,128)(2,1)S(1)}, u32[]{:S(2)}, u32[]{:S(2)}) collective-permute-start(bf16[408,512]{1,0:T(8,128)(2,1)S(1)} %pad_maximum_fusion.2), channel_id=1, source_target_pairs={{0,1},{1,0},{2,3},{3,2},{4,5},{5,4},{6,7},{7,6},{8,9},{9,8},{10,11... | collective-permute-start | bytes 1253384 | tf_op jit(solution)/shard_map/ppermute | solution.py:19
  29.3 1.4 %collective-permute-done.3 = bf16[408,512]{1,0:T(8,128)(2,1)S(1)} collective-permute-done((bf16[408,512]{1,0:T(8,128)(2,1)S(1)}, bf16[408,512]{1,0:T(8,128)(2,1)S(1)}, u32[]{:S(2)}, u32[]{:S(2)}) %collective-permute-start.3) | collective-permute-done | bytes 417824 | tf_op jit(solution)/shard_map/ppermute | solution.py:19
  30.9 1.6 %fusion.14 = f32[24,16,512]{2,1,0:T(8,128)S(1)} fusion(bf16[24,16,512]{2,1,0:T(8,128)(2,1)S(1)} %bitcast.127, f32[48,16,512]{2,1,0:T(8,128)} %copy-done.1, f32[24,16]{1,0:T(8,128)S(1)} %get-tuple-element.18, f32[24,16]{1,0:T(8,128)S(1)} %get-tuple-element.17, pred[]{:T(512)S(6)} %eq.57), kind=kLoop, calls=%fused_computation.28 | loop fusion | flops 983040 | bytes 2755585 | tf_op jit(solution)/shard_map/add | solution.py:86
  32.7 2.8 %collective-permute-start.5 = (bf16[102,512]{1,0:T(8,128)(2,1)S(1)}, bf16[102,512]{1,0:T(8,128)(2,1)S(1)}, u32[]{:S(2)}, u32[]{:S(2)}) collective-permute-start(bf16[102,512]{1,0:T(8,128)(2,1)S(1)} %pad_maximum_fusion.5), channel_id=1, source_target_pairs={{0,4},{1,5},{2,6},{3,7},{4,0},{5,1},{6,2},{7,3},{8,12},{9,13},{10,... | collective-permute-start | bytes 313352 | tf_op jit(solution)/shard_map/ppermute | solution.py:25
  35.6 4.4 %collective-permute-start.6 = (bf16[102,512]{1,0:T(8,128)(2,1)S(1)}, bf16[102,512]{1,0:T(8,128)(2,1)S(1)}, u32[]{:S(2)}, u32[]{:S(2)}) collective-permute-start(bf16[102,512]{1,0:T(8,128)(2,1)S(1)} %pad_maximum_fusion.6), channel_id=1, source_target_pairs={{0,6},{1,7},{2,0},{3,1},{4,2},{5,3},{6,4},{7,5},{8,14},{9,15},{10,... | collective-permute-start | bytes 313352 | tf_op jit(solution)/shard_map/ppermute | solution.py:25
  40.1 2.1 %collective-permute-start.4 = (bf16[102,512]{1,0:T(8,128)(2,1)S(1)}, bf16[102,512]{1,0:T(8,128)(2,1)S(1)}, u32[]{:S(2)}, u32[]{:S(2)}) collective-permute-start(bf16[102,512]{1,0:T(8,128)(2,1)S(1)} %pad_maximum_fusion.4), channel_id=1, source_target_pairs={{0,2},{1,3},{2,4},{3,5},{4,6},{5,7},{6,0},{7,1},{8,10},{9,11},{10,... | collective-permute-start | bytes 313352 | tf_op jit(solution)/shard_map/ppermute | solution.py:25
  42.3 5.7 %collective-permute-done.4 = bf16[102,512]{1,0:T(8,128)(2,1)S(1)} collective-permute-done((bf16[102,512]{1,0:T(8,128)(2,1)S(1)}, bf16[102,512]{1,0:T(8,128)(2,1)S(1)}, u32[]{:S(2)}, u32[]{:S(2)}) %collective-permute-start.4) | collective-permute-done | bytes 104480 | tf_op jit(solution)/shard_map/ppermute | solution.py:25
  49.7 15.2 %all-to-all-start = ((bf16[16,6,512]{2,1,0:T(8,128)(2,1)}), bf16[16,6,512]{2,1,0:T(8,128)(2,1)S(1)}, u32[]{:S(2)}, u32[]{:S(2)}) async-start(bf16[16,6,512]{2,1,0:T(8,128)(2,1)} %fusion.32), calls=%async_computation | async-start | bytes 262144 | tf_op jit(solution)/shard_map/all_to_all | solution.py:196
  64.9 13.4 %all-to-all-done = bf16[16,6,512]{2,1,0:T(8,128)(2,1)S(1)} async-done(((bf16[16,6,512]{2,1,0:T(8,128)(2,1)}), bf16[16,6,512]{2,1,0:T(8,128)(2,1)S(1)}, u32[]{:S(2)}, u32[]{:S(2)}) %all-to-all-start) | async-done | bytes 98336 | tf_op jit(solution)/shard_map/all_to_all | solution.py:196
  78.9 1.3 %fusion.4 = f32[96,2048]{1,0:T(8,128)S(1)} fusion(bf16[128,2048]{1,0:T(8,128)(2,1)S(1)} %copy-done.2, bf16[96,512]{1,0:T(8,128)(2,1)S(1)} %reshape.106, bf16[1,512,128]{2,1,0:T(8,128)(2,1)} %param.20), kind=kOutput, calls=%fused_computation.15 | convolution fusion | flops 62926848 | bytes 1540096 | tf_op jit(solution)/shard_map/dot_general | solution.py:205
  80.3 2.9 %collective-permute-start.7 = (bf16[48,2048]{1,0:T(8,128)(2,1)S(1)}, bf16[48,2048]{1,0:T(8,128)(2,1)S(1)}, u32[]{:S(2)}, u32[]{:S(2)}) collective-permute-start(bf16[48,2048]{1,0:T(8,128)(2,1)S(1)} %select_convert_fusion.1), channel_id=1, source_target_pairs={{0,32},{32,0},{64,96},{96,64},{128,160},{160,128},{192,224},{224,1... | collective-permute-start | bytes 589832 | tf_op jit(solution)/shard_map/ppermute | solution.py:19
  83.2 4.6 %collective-permute-done.7 = bf16[48,2048]{1,0:T(8,128)(2,1)S(1)} collective-permute-done((bf16[48,2048]{1,0:T(8,128)(2,1)S(1)}, bf16[48,2048]{1,0:T(8,128)(2,1)S(1)}, u32[]{:S(2)}, u32[]{:S(2)}) %collective-permute-start.7) | collective-permute-done | bytes 196640 | tf_op jit(solution)/shard_map/ppermute | solution.py:19
  87.9 3.2 %collective-permute-start.8 = (bf16[24,2048]{1,0:T(8,128)(2,1)S(1)}, bf16[24,2048]{1,0:T(8,128)(2,1)S(1)}, u32[]{:S(2)}, u32[]{:S(2)}) collective-permute-start(bf16[24,2048]{1,0:T(8,128)(2,1)S(1)} %select_convert_fusion.2), channel_id=1, source_target_pairs={{0,64},{64,0},{32,96},{96,32},{128,192},{192,128},{160,224},{224,1... | collective-permute-start | bytes 294920 | tf_op jit(solution)/shard_map/ppermute | solution.py:19
  91.3 5.1 %collective-permute-done.8 = bf16[24,2048]{1,0:T(8,128)(2,1)S(1)} collective-permute-done((bf16[24,2048]{1,0:T(8,128)(2,1)S(1)}, bf16[24,2048]{1,0:T(8,128)(2,1)S(1)}, u32[]{:S(2)}, u32[]{:S(2)}) %collective-permute-start.8) | collective-permute-done | bytes 98336 | tf_op jit(solution)/shard_map/ppermute | solution.py:19
  96.5 3.8 %collective-permute-start.9 = (bf16[6,2048]{1,0:T(8,128)(2,1)S(1)}, bf16[6,2048]{1,0:T(8,128)(2,1)S(1)}, u32[]{:S(2)}, u32[]{:S(2)}) collective-permute-start(bf16[6,2048]{1,0:T(8,128)(2,1)S(1)} %get-tuple-element.27), channel_id=1, source_target_pairs={{0,128},{32,160},{64,192},{96,224},{128,256},{160,288},{192,320},{... | collective-permute-start | bytes 73736 | tf_op jit(solution)/shard_map/ppermute | solution.py:25
  100.3 5.9 %collective-permute-start.11 = (bf16[6,2048]{1,0:T(8,128)(2,1)S(1)}, bf16[6,2048]{1,0:T(8,128)(2,1)S(1)}, u32[]{:S(2)}, u32[]{:S(2)}) collective-permute-start(bf16[6,2048]{1,0:T(8,128)(2,1)S(1)} %get-tuple-element.28), channel_id=1, source_target_pairs={{0,384},{32,416},{64,448},{96,480},{128,0},{160,32},{192,64},{224,... | collective-permute-start | bytes 73736 | tf_op jit(solution)/shard_map/ppermute | solution.py:25
  106.3 4.2 %collective-permute-start.10 = (bf16[6,2048]{1,0:T(8,128)(2,1)S(1)}, bf16[6,2048]{1,0:T(8,128)(2,1)S(1)}, u32[]{:S(2)}, u32[]{:S(2)}) collective-permute-start(bf16[6,2048]{1,0:T(8,128)(2,1)S(1)} %get-tuple-element.29), channel_id=1, source_target_pairs={{0,256},{32,288},{64,320},{96,352},{128,384},{160,416},{192,448},{... | collective-permute-start | bytes 73736 | tf_op jit(solution)/shard_map/ppermute | solution.py:25
  110.5 11.3 %collective-permute-done.10 = bf16[6,2048]{1,0:T(8,128)(2,1)S(1)} collective-permute-done((bf16[6,2048]{1,0:T(8,128)(2,1)S(1)}, bf16[6,2048]{1,0:T(8,128)(2,1)S(1)}, u32[]{:S(2)}, u32[]{:S(2)}) %collective-permute-start.10) | collective-permute-done | bytes 24608 | tf_op jit(solution)/shard_map/ppermute | solution.py:25
  (97 shorter events, 15.7 us)
Async XLA Ops:
  0.0 21.7 %copy-start = (bf16[16,512,128]{2,1,0:T(8,128)(2,1)S(1)}, bf16[16,512,128]{2,1,0:T(8,128)(2,1)}, u32[]{:S(2)}) copy-start(bf16[16,512,128]{2,1,0:T(8,128)(2,1)} %param.19) | copy-start | bytes 6291460
  1.6 9.8 %collective-permute-start = (bf16[6,3072]{1,0:T(8,128)(2,1)S(1)}, bf16[6,3072]{1,0:T(8,128)(2,1)S(1)}, u32[]{:S(2)}, u32[]{:S(2)}) collective-permute-start(bf16[6,3072]{1,0:T(8,128)(2,1)S(1)} %constant_dynamic-update-slice_fusion), channel_id=1, source_target_pairs={{0,4},{4,0},{1,5},{5,1},{2,6},{6,2},{3,7},{7,3},{8,12},{12,8},{9,1... | collective-permute-start | bytes 110600 | tf_op jit(solution)/shard_map/ppermute | solution.py:19
  11.5 6.5 %collective-permute-start.1 = (bf16[12,3072]{1,0:T(8,128)(2,1)S(1)}, bf16[12,3072]{1,0:T(8,128)(2,1)S(1)}, u32[]{:S(2)}, u32[]{:S(2)}) collective-permute-start(bf16[12,3072]{1,0:T(8,128)(2,1)S(1)} %pad_maximum_fusion.8), channel_id=1, source_target_pairs={{0,2},{2,0},{1,3},{3,1},{4,6},{6,4},{5,7},{7,5},{8,10},{10,8},{9,1... | collective-permute-start | bytes 221192 | tf_op jit(solution)/shard_map/ppermute | solution.py:19
  18.1 3.3 %collective-permute-start.2 = (bf16[24,3072]{1,0:T(8,128)(2,1)S(1)}, bf16[24,3072]{1,0:T(8,128)(2,1)S(1)}, u32[]{:S(2)}, u32[]{:S(2)}) collective-permute-start(bf16[24,3072]{1,0:T(8,128)(2,1)S(1)} %pad_maximum_fusion.3), channel_id=1, source_target_pairs={{0,1},{1,0},{2,3},{3,2},{4,5},{5,4},{6,7},{7,6},{8,9},{9,8},{10,11... | collective-permute-start | bytes 442376 | tf_op jit(solution)/shard_map/ppermute | solution.py:19
  21.7 1.1 copy-start.4
  21.7 1.1 copy-start.5
  25.7 1.2 copy-start.1
  27.1 3.7 %collective-permute-start.3 = (bf16[408,512]{1,0:T(8,128)(2,1)S(1)}, bf16[408,512]{1,0:T(8,128)(2,1)S(1)}, u32[]{:S(2)}, u32[]{:S(2)}) collective-permute-start(bf16[408,512]{1,0:T(8,128)(2,1)S(1)} %pad_maximum_fusion.2), channel_id=1, source_target_pairs={{0,1},{1,0},{2,3},{3,2},{4,5},{5,4},{6,7},{7,6},{8,9},{9,8},{10,11... | collective-permute-start | bytes 1253384 | tf_op jit(solution)/shard_map/ppermute | solution.py:19
  32.7 32.2 %copy-start.3 = (s32[16]{0:T(128)S(1)}, s32[16]{0:T(128)}, u32[]{:S(2)}) copy-start(s32[16]{0:T(128)} %constant.246) | copy-start | bytes 196
  32.7 9.5 %collective-permute-start.5 = (bf16[102,512]{1,0:T(8,128)(2,1)S(1)}, bf16[102,512]{1,0:T(8,128)(2,1)S(1)}, u32[]{:S(2)}, u32[]{:S(2)}) collective-permute-start(bf16[102,512]{1,0:T(8,128)(2,1)S(1)} %pad_maximum_fusion.5), channel_id=1, source_target_pairs={{0,4},{1,5},{2,6},{3,7},{4,0},{5,1},{6,2},{7,3},{8,12},{9,13},{10,... | collective-permute-start | bytes 313352 | tf_op jit(solution)/shard_map/ppermute | solution.py:25
  35.6 6.7 %collective-permute-start.6 = (bf16[102,512]{1,0:T(8,128)(2,1)S(1)}, bf16[102,512]{1,0:T(8,128)(2,1)S(1)}, u32[]{:S(2)}, u32[]{:S(2)}) collective-permute-start(bf16[102,512]{1,0:T(8,128)(2,1)S(1)} %pad_maximum_fusion.6), channel_id=1, source_target_pairs={{0,6},{1,7},{2,0},{3,1},{4,2},{5,3},{6,4},{7,5},{8,14},{9,15},{10,... | collective-permute-start | bytes 313352 | tf_op jit(solution)/shard_map/ppermute | solution.py:25
  40.0 38.9 %copy-start.2 = (bf16[128,2048]{1,0:T(8,128)(2,1)S(1)}, bf16[128,2048]{1,0:T(8,128)(2,1)}, u32[]{:S(2)}) copy-start(bf16[128,2048]{1,0:T(8,128)(2,1)} %param.21) | copy-start | bytes 1572868
  40.1 7.9 %collective-permute-start.4 = (bf16[102,512]{1,0:T(8,128)(2,1)S(1)}, bf16[102,512]{1,0:T(8,128)(2,1)S(1)}, u32[]{:S(2)}, u32[]{:S(2)}) collective-permute-start(bf16[102,512]{1,0:T(8,128)(2,1)S(1)} %pad_maximum_fusion.4), channel_id=1, source_target_pairs={{0,2},{1,3},{2,4},{3,5},{4,6},{5,7},{6,0},{7,1},{8,10},{9,11},{10,... | collective-permute-start | bytes 313352 | tf_op jit(solution)/shard_map/ppermute | solution.py:25
  49.7 28.6 %all-to-all-start = ((bf16[16,6,512]{2,1,0:T(8,128)(2,1)}), bf16[16,6,512]{2,1,0:T(8,128)(2,1)S(1)}, u32[]{:S(2)}, u32[]{:S(2)}) async-start(bf16[16,6,512]{2,1,0:T(8,128)(2,1)} %fusion.32), calls=%async_computation | async-start | bytes 262144 | tf_op jit(solution)/shard_map/all_to_all | solution.py:196
  80.3 7.6 %collective-permute-start.7 = (bf16[48,2048]{1,0:T(8,128)(2,1)S(1)}, bf16[48,2048]{1,0:T(8,128)(2,1)S(1)}, u32[]{:S(2)}, u32[]{:S(2)}) collective-permute-start(bf16[48,2048]{1,0:T(8,128)(2,1)S(1)} %select_convert_fusion.1), channel_id=1, source_target_pairs={{0,32},{32,0},{64,96},{96,64},{128,160},{160,128},{192,224},{224,1... | collective-permute-start | bytes 589832 | tf_op jit(solution)/shard_map/ppermute | solution.py:19
  87.9 8.5 %collective-permute-start.8 = (bf16[24,2048]{1,0:T(8,128)(2,1)S(1)}, bf16[24,2048]{1,0:T(8,128)(2,1)S(1)}, u32[]{:S(2)}, u32[]{:S(2)}) collective-permute-start(bf16[24,2048]{1,0:T(8,128)(2,1)S(1)} %select_convert_fusion.2), channel_id=1, source_target_pairs={{0,64},{64,0},{32,96},{96,32},{128,192},{192,128},{160,224},{224,1... | collective-permute-start | bytes 294920 | tf_op jit(solution)/shard_map/ppermute | solution.py:19
  96.5 14.0 %collective-permute-start.9 = (bf16[6,2048]{1,0:T(8,128)(2,1)S(1)}, bf16[6,2048]{1,0:T(8,128)(2,1)S(1)}, u32[]{:S(2)}, u32[]{:S(2)}) collective-permute-start(bf16[6,2048]{1,0:T(8,128)(2,1)S(1)} %get-tuple-element.27), channel_id=1, source_target_pairs={{0,128},{32,160},{64,192},{96,224},{128,256},{160,288},{192,320},{... | collective-permute-start | bytes 73736 | tf_op jit(solution)/shard_map/ppermute | solution.py:25
  100.3 10.2 %collective-permute-start.11 = (bf16[6,2048]{1,0:T(8,128)(2,1)S(1)}, bf16[6,2048]{1,0:T(8,128)(2,1)S(1)}, u32[]{:S(2)}, u32[]{:S(2)}) collective-permute-start(bf16[6,2048]{1,0:T(8,128)(2,1)S(1)} %get-tuple-element.28), channel_id=1, source_target_pairs={{0,384},{32,416},{64,448},{96,480},{128,0},{160,32},{192,64},{224,... | collective-permute-start | bytes 73736 | tf_op jit(solution)/shard_map/ppermute | solution.py:25
  106.3 15.6 %collective-permute-start.10 = (bf16[6,2048]{1,0:T(8,128)(2,1)S(1)}, bf16[6,2048]{1,0:T(8,128)(2,1)S(1)}, u32[]{:S(2)}, u32[]{:S(2)}) collective-permute-start(bf16[6,2048]{1,0:T(8,128)(2,1)S(1)} %get-tuple-element.29), channel_id=1, source_target_pairs={{0,256},{32,288},{64,320},{96,352},{128,384},{160,416},{192,448},{... | collective-permute-start | bytes 73736 | tf_op jit(solution)/shard_map/ppermute | solution.py:25

commit v9 on v5

--- a/solution.py
+++ b/solution.py
@@ -203,7 +203,7 @@
         )
 
     total_rows = block_for(mine)
-    for step in range(1, ring):
+    for step in sorted(range(1, ring), key=lambda s: -min(s, ring - s)):
         sent = block_for((mine + step) % ring).astype(jnp.bfloat16)
         total_rows = total_rows + shifted(sent, "grp", grp_size, 4 * step).astype(jnp.float32)
     return total_rows.astype(jnp.bfloat16)

time: 122 us -> 117 us (0.959)
  waiting for transfers between devices: 51.9 us -> 47.1 us
    ppermute x3, waiting for transfers between devices: 11.3 us -> 6.46 us  [shifted(): return lax.ppermute(block, axis, route)]
  transfers between devices with their start and end apart: 12 -> 12, of which waited for: 9 -> 10; matrix products, arithmetic and copies ran while one was open for 5% -> 5% of each run, Pallas kernels for 0% -> 0%
where the time goes in v9:
time: 117 us
  starting transfers between devices  52.3 us (45%)
  waiting for transfers between devices  47.1 us (40%)
  local copies, waits for them, and re-layouts  6.04 us (5%)
  other arithmetic  5.4 us (5%)
  matrix products  5.14 us (4%)
    ppermute x8, waiting for transfers between devices, from_partner(): return lax.ppermute(block, axis, route)  27.2 us
    ppermute x8, starting transfers between devices, from_partner(): return lax.ppermute(block, axis, route)  23.2 us
    all_to_all x1, starting transfers between devices, per_device(): lax.all_to_all(jnp.swapaxes(merged.astype(jnp.bfloat16), 0, 1), 'grp', sp...  15.2 us
    ppermute x3, starting transfers between devices, shifted(): return lax.ppermute(block, axis, route)  14 us
    all_to_all x1, waiting for transfers between devices, per_device(): lax.all_to_all(jnp.swapaxes(merged.astype(jnp.bfloat16), 0, 1), 'grp', sp...  13.4 us
    ppermute x3, waiting for transfers between devices, shifted(): return lax.ppermute(block, axis, route)  6.46 us
  transfers between devices with their start and end apart: 12, of which 10 were waited for; matrix products, arithmetic and copies ran while one was open for 5% of the time, Pallas kernels for 0%

profile of v9, /device:TPU:6, one launch (start us, length us, event | category | flops | bytes accessed | tf_op | source)
XLA Modules:
  0.0 116.7 jit_solution(6813315712462101770)
XLA Ops:
  1.6 5.1 %collective-permute-start = (bf16[6,3072]{1,0:T(8,128)(2,1)S(1)}, bf16[6,3072]{1,0:T(8,128)(2,1)S(1)}, u32[]{:S(2)}, u32[]{:S(2)}) collective-permute-start(bf16[6,3072]{1,0:T(8,128)(2,1)S(1)} %constant_dynamic-update-slice_fusion), channel_id=1, source_target_pairs={{0,4},{4,0},{1,5},{5,1},{2,6},{6,2},{3,7},{7,3},{8,12},{12,8},{9,1... | collective-permute-start | bytes 110600 | tf_op jit(solution)/shard_map/ppermute | solution.py:19
  6.8 1.2 %dynamic_slice.24 = s32[1]{0:T(128)} dynamic-slice(s32[4]{0:T(128)} %param.17, s32[]{:T(128)S(6)} %select_n.241), dynamic_slice_sizes={1} | dynamic-slice | bytes 12 | tf_op jit(solution)/shard_map/jit(dynamic_index_in_dim)/dynamic_slice | solution.py:135
  11.5 2.6 %collective-permute-start.1 = (bf16[12,3072]{1,0:T(8,128)(2,1)S(1)}, bf16[12,3072]{1,0:T(8,128)(2,1)S(1)}, u32[]{:S(2)}, u32[]{:S(2)}) collective-permute-start(bf16[12,3072]{1,0:T(8,128)(2,1)S(1)} %pad_maximum_fusion.7), channel_id=1, source_target_pairs={{0,2},{2,0},{1,3},{3,1},{4,6},{6,4},{5,7},{7,5},{8,10},{10,8},{9,1... | collective-permute-start | bytes 221192 | tf_op jit(solution)/shard_map/ppermute | solution.py:19
  15.4 2.7 %collective-permute-done.1 = bf16[12,3072]{1,0:T(8,128)(2,1)S(1)} collective-permute-done((bf16[12,3072]{1,0:T(8,128)(2,1)S(1)}, bf16[12,3072]{1,0:T(8,128)(2,1)S(1)}, u32[]{:S(2)}, u32[]{:S(2)}) %collective-permute-start.1) | collective-permute-done | bytes 73760 | tf_op jit(solution)/shard_map/ppermute | solution.py:19
  18.1 1.9 %collective-permute-start.2 = (bf16[24,3072]{1,0:T(8,128)(2,1)S(1)}, bf16[24,3072]{1,0:T(8,128)(2,1)S(1)}, u32[]{:S(2)}, u32[]{:S(2)}) collective-permute-start(bf16[24,3072]{1,0:T(8,128)(2,1)S(1)} %pad_maximum_fusion.4), channel_id=1, source_target_pairs={{0,1},{1,0},{2,3},{3,2},{4,5},{5,4},{6,7},{7,6},{8,9},{9,8},{10,11... | collective-permute-start | bytes 442376 | tf_op jit(solution)/shard_map/ppermute | solution.py:19
  20.1 1.3 %collective-permute-done.2 = bf16[24,3072]{1,0:T(8,128)(2,1)S(1)} collective-permute-done((bf16[24,3072]{1,0:T(8,128)(2,1)S(1)}, bf16[24,3072]{1,0:T(8,128)(2,1)S(1)}, u32[]{:S(2)}, u32[]{:S(2)}) %collective-permute-start.2) | collective-permute-done | bytes 147488 | tf_op jit(solution)/shard_map/ppermute | solution.py:19
  25.9 2.0 %collective-permute-start.3 = (bf16[408,512]{1,0:T(8,128)(2,1)S(1)}, bf16[408,512]{1,0:T(8,128)(2,1)S(1)}, u32[]{:S(2)}, u32[]{:S(2)}) collective-permute-start(bf16[408,512]{1,0:T(8,128)(2,1)S(1)} %pad_maximum_fusion.2), channel_id=1, source_target_pairs={{0,1},{1,0},{2,3},{3,2},{4,5},{5,4},{6,7},{7,6},{8,9},{9,8},{10,11... | collective-permute-start | bytes 1253384 | tf_op jit(solution)/shard_map/ppermute | solution.py:19
  28.0 1.6 %collective-permute-done.3 = bf16[408,512]{1,0:T(8,128)(2,1)S(1)} collective-permute-done((bf16[408,512]{1,0:T(8,128)(2,1)S(1)}, bf16[408,512]{1,0:T(8,128)(2,1)S(1)}, u32[]{:S(2)}, u32[]{:S(2)}) %collective-permute-start.3) | collective-permute-done | bytes 417824 | tf_op jit(solution)/shard_map/ppermute | solution.py:19
  30.2 2.6 %collective-permute-start.4 = (bf16[204,512]{1,0:T(8,128)(2,1)S(1)}, bf16[204,512]{1,0:T(8,128)(2,1)S(1)}, u32[]{:S(2)}, u32[]{:S(2)}) collective-permute-start(bf16[204,512]{1,0:T(8,128)(2,1)S(1)} %pad_maximum_fusion.3), channel_id=1, source_target_pairs={{0,2},{2,0},{1,3},{3,1},{4,6},{6,4},{5,7},{7,5},{8,10},{10,8},{9,1... | collective-permute-start | bytes 626696 | tf_op jit(solution)/shard_map/ppermute | solution.py:19
  32.7 6.6 %collective-permute-done.4 = bf16[204,512]{1,0:T(8,128)(2,1)S(1)} collective-permute-done((bf16[204,512]{1,0:T(8,128)(2,1)S(1)}, bf16[204,512]{1,0:T(8,128)(2,1)S(1)}, u32[]{:S(2)}, u32[]{:S(2)}) %collective-permute-start.4) | collective-permute-done | bytes 208928 | tf_op jit(solution)/shard_map/ppermute | solution.py:19
  39.8 2.8 %collective-permute-start.5 = (bf16[102,512]{1,0:T(8,128)(2,1)S(1)}, bf16[102,512]{1,0:T(8,128)(2,1)S(1)}, u32[]{:S(2)}, u32[]{:S(2)}) collective-permute-start(bf16[102,512]{1,0:T(8,128)(2,1)S(1)} %pad_maximum_fusion.5), channel_id=1, source_target_pairs={{0,4},{4,0},{1,5},{5,1},{2,6},{6,2},{3,7},{7,3},{8,12},{12,8},{9,1... | collective-permute-start | bytes 313352 | tf_op jit(solution)/shard_map/ppermute | solution.py:19
  42.5 5.3 %collective-permute-done.5 = bf16[102,512]{1,0:T(8,128)(2,1)S(1)} collective-permute-done((bf16[102,512]{1,0:T(8,128)(2,1)S(1)}, bf16[102,512]{1,0:T(8,128)(2,1)S(1)}, u32[]{:S(2)}, u32[]{:S(2)}) %collective-permute-start.5) | collective-permute-done | bytes 104480 | tf_op jit(solution)/shard_map/ppermute | solution.py:19
  48.8 15.2 %all-to-all-start = ((bf16[16,6,512]{2,1,0:T(8,128)(2,1)}), bf16[16,6,512]{2,1,0:T(8,128)(2,1)S(1)}, u32[]{:S(2)}, u32[]{:S(2)}) async-start(bf16[16,6,512]{2,1,0:T(8,128)(2,1)} %copy.49), calls=%async_computation | async-start | bytes 262144 | tf_op jit(solution)/shard_map/all_to_all | solution.py:176
  64.0 13.4 %all-to-all-done = bf16[16,6,512]{2,1,0:T(8,128)(2,1)S(1)} async-done(((bf16[16,6,512]{2,1,0:T(8,128)(2,1)}), bf16[16,6,512]{2,1,0:T(8,128)(2,1)S(1)}, u32[]{:S(2)}, u32[]{:S(2)}) %all-to-all-start) | async-done | bytes 98336 | tf_op jit(solution)/shard_map/all_to_all | solution.py:176
  78.1 1.3 %fusion.4 = f32[96,2048]{1,0:T(8,128)S(1)} fusion(bf16[128,2048]{1,0:T(8,128)(2,1)S(1)} %copy-done.1, bf16[96,512]{1,0:T(8,128)(2,1)S(1)} %reshape.87, bf16[1,512,128]{2,1,0:T(8,128)(2,1)} %param.20), kind=kOutput, calls=%fused_computation.15 | convolution fusion | flops 62926848 | bytes 1540096 | tf_op jit(solution)/shard_map/dot_general | solution.py:185
  79.4 2.9 %collective-permute-start.6 = (bf16[48,2048]{1,0:T(8,128)(2,1)S(1)}, bf16[48,2048]{1,0:T(8,128)(2,1)S(1)}, u32[]{:S(2)}, u32[]{:S(2)}) collective-permute-start(bf16[48,2048]{1,0:T(8,128)(2,1)S(1)} %select_convert_fusion.1), channel_id=1, source_target_pairs={{0,32},{32,0},{64,96},{96,64},{128,160},{160,128},{192,224},{224,1... | collective-permute-start | bytes 589832 | tf_op jit(solution)/shard_map/ppermute | solution.py:19
  82.3 4.6 %collective-permute-done.6 = bf16[48,2048]{1,0:T(8,128)(2,1)S(1)} collective-permute-done((bf16[48,2048]{1,0:T(8,128)(2,1)S(1)}, bf16[48,2048]{1,0:T(8,128)(2,1)S(1)}, u32[]{:S(2)}, u32[]{:S(2)}) %collective-permute-start.6) | collective-permute-done | bytes 196640 | tf_op jit(solution)/shard_map/ppermute | solution.py:19
  87.0 3.2 %collective-permute-start.7 = (bf16[24,2048]{1,0:T(8,128)(2,1)S(1)}, bf16[24,2048]{1,0:T(8,128)(2,1)S(1)}, u32[]{:S(2)}, u32[]{:S(2)}) collective-permute-start(bf16[24,2048]{1,0:T(8,128)(2,1)S(1)} %select_convert_fusion.3), channel_id=1, source_target_pairs={{0,64},{64,0},{32,96},{96,32},{128,192},{192,128},{160,224},{224,1... | collective-permute-start | bytes 294920 | tf_op jit(solution)/shard_map/ppermute | solution.py:19
  90.4 5.1 %collective-permute-done.7 = bf16[24,2048]{1,0:T(8,128)(2,1)S(1)} collective-permute-done((bf16[24,2048]{1,0:T(8,128)(2,1)S(1)}, bf16[24,2048]{1,0:T(8,128)(2,1)S(1)}, u32[]{:S(2)}, u32[]{:S(2)}) %collective-permute-start.7) | collective-permute-done | bytes 98336 | tf_op jit(solution)/shard_map/ppermute | solution.py:19
  95.6 4.2 %collective-permute-start.8 = (bf16[6,2048]{1,0:T(8,128)(2,1)S(1)}, bf16[6,2048]{1,0:T(8,128)(2,1)S(1)}, u32[]{:S(2)}, u32[]{:S(2)}) collective-permute-start(bf16[6,2048]{1,0:T(8,128)(2,1)S(1)} %get-tuple-element.24), channel_id=1, source_target_pairs={{0,256},{32,288},{64,320},{96,352},{128,384},{160,416},{192,448},{... | collective-permute-start | bytes 73736 | tf_op jit(solution)/shard_map/ppermute | solution.py:25
  99.8 6.5 %collective-permute-start.10 = (bf16[6,2048]{1,0:T(8,128)(2,1)S(1)}, bf16[6,2048]{1,0:T(8,128)(2,1)S(1)}, u32[]{:S(2)}, u32[]{:S(2)}) collective-permute-start(bf16[6,2048]{1,0:T(8,128)(2,1)S(1)} %get-tuple-element.25), channel_id=1, source_target_pairs={{0,384},{32,416},{64,448},{96,480},{128,0},{160,32},{192,64},{224,... | collective-permute-start | bytes 73736 | tf_op jit(solution)/shard_map/ppermute | solution.py:25
  106.4 3.2 %collective-permute-start.9 = (bf16[6,2048]{1,0:T(8,128)(2,1)S(1)}, bf16[6,2048]{1,0:T(8,128)(2,1)S(1)}, u32[]{:S(2)}, u32[]{:S(2)}) collective-permute-start(bf16[6,2048]{1,0:T(8,128)(2,1)S(1)} %get-tuple-element.26), channel_id=1, source_target_pairs={{0,128},{32,160},{64,192},{96,224},{128,256},{160,288},{192,320},{... | collective-permute-start | bytes 73736 | tf_op jit(solution)/shard_map/ppermute | solution.py:25
  109.6 1.6 %collective-permute-done.8 = bf16[6,2048]{1,0:T(8,128)(2,1)S(1)} collective-permute-done((bf16[6,2048]{1,0:T(8,128)(2,1)S(1)}, bf16[6,2048]{1,0:T(8,128)(2,1)S(1)}, u32[]{:S(2)}, u32[]{:S(2)}) %collective-permute-start.8) | collective-permute-done | bytes 24608 | tf_op jit(solution)/shard_map/ppermute | solution.py:25
  111.2 4.9 %collective-permute-done.9 = bf16[6,2048]{1,0:T(8,128)(2,1)S(1)} collective-permute-done((bf16[6,2048]{1,0:T(8,128)(2,1)S(1)}, bf16[6,2048]{1,0:T(8,128)(2,1)S(1)}, u32[]{:S(2)}, u32[]{:S(2)}) %collective-permute-start.9) | collective-permute-done | bytes 24608 | tf_op jit(solution)/shard_map/ppermute | solution.py:25
  (84 shorter events, 14.1 us)
Async XLA Ops:
  0.0 21.7 %copy-start = (bf16[16,512,128]{2,1,0:T(8,128)(2,1)S(1)}, bf16[16,512,128]{2,1,0:T(8,128)(2,1)}, u32[]{:S(2)}) copy-start(bf16[16,512,128]{2,1,0:T(8,128)(2,1)} %param.19) | copy-start | bytes 6291460
  1.6 9.8 %collective-permute-start = (bf16[6,3072]{1,0:T(8,128)(2,1)S(1)}, bf16[6,3072]{1,0:T(8,128)(2,1)S(1)}, u32[]{:S(2)}, u32[]{:S(2)}) collective-permute-start(bf16[6,3072]{1,0:T(8,128)(2,1)S(1)} %constant_dynamic-update-slice_fusion), channel_id=1, source_target_pairs={{0,4},{4,0},{1,5},{5,1},{2,6},{6,2},{3,7},{7,3},{8,12},{12,8},{9,1... | collective-permute-start | bytes 110600 | tf_op jit(solution)/shard_map/ppermute | solution.py:19
  11.5 6.5 %collective-permute-start.1 = (bf16[12,3072]{1,0:T(8,128)(2,1)S(1)}, bf16[12,3072]{1,0:T(8,128)(2,1)S(1)}, u32[]{:S(2)}, u32[]{:S(2)}) collective-permute-start(bf16[12,3072]{1,0:T(8,128)(2,1)S(1)} %pad_maximum_fusion.7), channel_id=1, source_target_pairs={{0,2},{2,0},{1,3},{3,1},{4,6},{6,4},{5,7},{7,5},{8,10},{10,8},{9,1... | collective-permute-start | bytes 221192 | tf_op jit(solution)/shard_map/ppermute | solution.py:19
  18.1 3.3 %collective-permute-start.2 = (bf16[24,3072]{1,0:T(8,128)(2,1)S(1)}, bf16[24,3072]{1,0:T(8,128)(2,1)S(1)}, u32[]{:S(2)}, u32[]{:S(2)}) collective-permute-start(bf16[24,3072]{1,0:T(8,128)(2,1)S(1)} %pad_maximum_fusion.4), channel_id=1, source_target_pairs={{0,1},{1,0},{2,3},{3,2},{4,5},{5,4},{6,7},{7,6},{8,9},{9,8},{10,11... | collective-permute-start | bytes 442376 | tf_op jit(solution)/shard_map/ppermute | solution.py:19
  21.7 1.1 copy-start.3
  21.7 1.1 copy-start.4
  25.9 3.7 %collective-permute-start.3 = (bf16[408,512]{1,0:T(8,128)(2,1)S(1)}, bf16[408,512]{1,0:T(8,128)(2,1)S(1)}, u32[]{:S(2)}, u32[]{:S(2)}) collective-permute-start(bf16[408,512]{1,0:T(8,128)(2,1)S(1)} %pad_maximum_fusion.2), channel_id=1, source_target_pairs={{0,1},{1,0},{2,3},{3,2},{4,5},{5,4},{6,7},{7,6},{8,9},{9,8},{10,11... | collective-permute-start | bytes 1253384 | tf_op jit(solution)/shard_map/ppermute | solution.py:19
  30.1 33.9 %copy-start.2 = (s32[16]{0:T(128)S(1)}, s32[16]{0:T(128)}, u32[]{:S(2)}) copy-start(s32[16]{0:T(128)} %constant.169) | copy-start | bytes 196
  30.2 9.2 %collective-permute-start.4 = (bf16[204,512]{1,0:T(8,128)(2,1)S(1)}, bf16[204,512]{1,0:T(8,128)(2,1)S(1)}, u32[]{:S(2)}, u32[]{:S(2)}) collective-permute-start(bf16[204,512]{1,0:T(8,128)(2,1)S(1)} %pad_maximum_fusion.3), channel_id=1, source_target_pairs={{0,2},{2,0},{1,3},{3,1},{4,6},{6,4},{5,7},{7,5},{8,10},{10,8},{9,1... | collective-permute-start | bytes 626696 | tf_op jit(solution)/shard_map/ppermute | solution.py:19
  39.5 38.6 %copy-start.1 = (bf16[128,2048]{1,0:T(8,128)(2,1)S(1)}, bf16[128,2048]{1,0:T(8,128)(2,1)}, u32[]{:S(2)}) copy-start(bf16[128,2048]{1,0:T(8,128)(2,1)} %param.21) | copy-start | bytes 1572868
  39.8 8.1 %collective-permute-start.5 = (bf16[102,512]{1,0:T(8,128)(2,1)S(1)}, bf16[102,512]{1,0:T(8,128)(2,1)S(1)}, u32[]{:S(2)}, u32[]{:S(2)}) collective-permute-start(bf16[102,512]{1,0:T(8,128)(2,1)S(1)} %pad_maximum_fusion.5), channel_id=1, source_target_pairs={{0,4},{4,0},{1,5},{5,1},{2,6},{6,2},{3,7},{7,3},{8,12},{12,8},{9,1... | collective-permute-start | bytes 313352 | tf_op jit(solution)/shard_map/ppermute | solution.py:19
  48.8 28.6 %all-to-all-start = ((bf16[16,6,512]{2,1,0:T(8,128)(2,1)}), bf16[16,6,512]{2,1,0:T(8,128)(2,1)S(1)}, u32[]{:S(2)}, u32[]{:S(2)}) async-start(bf16[16,6,512]{2,1,0:T(8,128)(2,1)} %copy.49), calls=%async_computation | async-start | bytes 262144 | tf_op jit(solution)/shard_map/all_to_all | solution.py:176
  79.4 7.6 %collective-permute-start.6 = (bf16[48,2048]{1,0:T(8,128)(2,1)S(1)}, bf16[48,2048]{1,0:T(8,128)(2,1)S(1)}, u32[]{:S(2)}, u32[]{:S(2)}) collective-permute-start(bf16[48,2048]{1,0:T(8,128)(2,1)S(1)} %select_convert_fusion.1), channel_id=1, source_target_pairs={{0,32},{32,0},{64,96},{96,64},{128,160},{160,128},{192,224},{224,1... | collective-permute-start | bytes 589832 | tf_op jit(solution)/shard_map/ppermute | solution.py:19
  87.0 8.5 %collective-permute-start.7 = (bf16[24,2048]{1,0:T(8,128)(2,1)S(1)}, bf16[24,2048]{1,0:T(8,128)(2,1)S(1)}, u32[]{:S(2)}, u32[]{:S(2)}) collective-permute-start(bf16[24,2048]{1,0:T(8,128)(2,1)S(1)} %select_convert_fusion.3), channel_id=1, source_target_pairs={{0,64},{64,0},{32,96},{96,32},{128,192},{192,128},{160,224},{224,1... | collective-permute-start | bytes 294920 | tf_op jit(solution)/shard_map/ppermute | solution.py:19
  95.6 15.6 %collective-permute-start.8 = (bf16[6,2048]{1,0:T(8,128)(2,1)S(1)}, bf16[6,2048]{1,0:T(8,128)(2,1)S(1)}, u32[]{:S(2)}, u32[]{:S(2)}) collective-permute-start(bf16[6,2048]{1,0:T(8,128)(2,1)S(1)} %get-tuple-element.24), channel_id=1, source_target_pairs={{0,256},{32,288},{64,320},{96,352},{128,384},{160,416},{192,448},{... | collective-permute-start | bytes 73736 | tf_op jit(solution)/shard_map/ppermute | solution.py:25
  99.8 11.4 %collective-permute-start.10 = (bf16[6,2048]{1,0:T(8,128)(2,1)S(1)}, bf16[6,2048]{1,0:T(8,128)(2,1)S(1)}, u32[]{:S(2)}, u32[]{:S(2)}) collective-permute-start(bf16[6,2048]{1,0:T(8,128)(2,1)S(1)} %get-tuple-element.25), channel_id=1, source_target_pairs={{0,384},{32,416},{64,448},{96,480},{128,0},{160,32},{192,64},{224,... | collective-permute-start | bytes 73736 | tf_op jit(solution)/shard_map/ppermute | solution.py:25
  106.4 9.7 %collective-permute-start.9 = (bf16[6,2048]{1,0:T(8,128)(2,1)S(1)}, bf16[6,2048]{1,0:T(8,128)(2,1)S(1)}, u32[]{:S(2)}, u32[]{:S(2)}) collective-permute-start(bf16[6,2048]{1,0:T(8,128)(2,1)S(1)} %get-tuple-element.26), channel_id=1, source_target_pairs={{0,128},{32,160},{64,192},{96,224},{128,256},{160,288},{192,320},{... | collective-permute-start | bytes 73736 | tf_op jit(solution)/shard_map/ppermute | solution.py:25

commit v10 on v8

--- a/solution.py
+++ b/solution.py
@@ -182,7 +182,13 @@
         return tuple(lax.dynamic_index_in_dim(member, index, 0, keepdims=False) for member in chip_blocks)
 
     parts = [block_of(chip)]
+    far_step = chips // 2
+    far_packet = pack_part(*block_of((chip + far_step) % chips), latent_width)
+    far_packet, chip_blocks = lax.optimization_barrier((far_packet, chip_blocks))
+    parts.append(unpack_part(shifted(far_packet, "ep", per_request, 2 * far_step), head_count))
     for step in range(1, chips):
+        if step == far_step:
+            continue
         sent = block_of((chip + step) % chips)
         got = shifted(pack_part(*sent, latent_width), "ep", per_request, 2 * step)
         parts.append(unpack_part(got, head_count))
@@ -223,7 +229,7 @@
         )
 
     total_rows = block_for(mine)
-    for step in range(1, ring):
+    for step in sorted(range(1, ring), key=lambda s: -min(s, ring - s)):
         sent = block_for((mine + step) % ring).astype(jnp.bfloat16)
         total_rows = total_rows + shifted(sent, "grp", grp_size, 4 * step).astype(jnp.float32)
     return total_rows.astype(jnp.bfloat16)

time: 123 us -> 119 us (0.967)
  waiting for transfers between devices: 45.6 us -> 41.1 us
    ppermute x6, waiting for transfers between devices: 17 us -> 12.6 us  [shifted(): return lax.ppermute(block, axis, route)]
  transfers between devices with their start and end apart: 13 -> 13, of which waited for: 9 -> 10; matrix products, arithmetic and copies ran while one was open for 5% -> 5% of each run, Pallas kernels for 0% -> 0%
where the time goes in v10:
time: 119 us; the launch traced here: 118 us
  starting transfers between devices  56.2 us (47%)
  waiting for transfers between devices  41.1 us (35%)
  other arithmetic  7.6 us (6%)
  local copies, waits for them, and re-layouts  7 us (6%)
  matrix products  5.14 us (4%)
    ppermute x6, starting transfers between devices, shifted(): return lax.ppermute(block, axis, route)  23.2 us
    ppermute x6, starting transfers between devices, from_partner(): return lax.ppermute(block, axis, route)  17.8 us
    all_to_all x1, starting transfers between devices, per_device(): lax.all_to_all(jnp.swapaxes(merged.astype(jnp.bfloat16), 0, 1), 'grp', sp...  15.2 us
    ppermute x6, waiting for transfers between devices, from_partner(): return lax.ppermute(block, axis, route)  15.1 us
    all_to_all x1, waiting for transfers between devices, per_device(): lax.all_to_all(jnp.swapaxes(merged.astype(jnp.bfloat16), 0, 1), 'grp', sp...  13.4 us
    ppermute x6, waiting for transfers between devices, shifted(): return lax.ppermute(block, axis, route)  12.6 us
  transfers between devices with their start and end apart: 13, of which 10 were waited for; matrix products, arithmetic and copies ran while one was open for 5% of the time, Pallas kernels for 0%

profile of v10, /device:TPU:6, one launch (start us, length us, event | category | flops | bytes accessed | tf_op | source)
XLA Modules:
  0.0 118.0 jit_solution(13023172196200623049)
XLA Ops:
  1.6 5.1 %collective-permute-start = (bf16[6,3072]{1,0:T(8,128)(2,1)S(1)}, bf16[6,3072]{1,0:T(8,128)(2,1)S(1)}, u32[]{:S(2)}, u32[]{:S(2)}) collective-permute-start(bf16[6,3072]{1,0:T(8,128)(2,1)S(1)} %constant_dynamic-update-slice_fusion), channel_id=1, source_target_pairs={{0,4},{4,0},{1,5},{5,1},{2,6},{6,2},{3,7},{7,3},{8,12},{12,8},{9,1... | collective-permute-start | bytes 110600 | tf_op jit(solution)/shard_map/ppermute | solution.py:19
  11.5 2.6 %collective-permute-start.1 = (bf16[12,3072]{1,0:T(8,128)(2,1)S(1)}, bf16[12,3072]{1,0:T(8,128)(2,1)S(1)}, u32[]{:S(2)}, u32[]{:S(2)}) collective-permute-start(bf16[12,3072]{1,0:T(8,128)(2,1)S(1)} %pad_maximum_fusion.8), channel_id=1, source_target_pairs={{0,2},{2,0},{1,3},{3,1},{4,6},{6,4},{5,7},{7,5},{8,10},{10,8},{9,1... | collective-permute-start | bytes 221192 | tf_op jit(solution)/shard_map/ppermute | solution.py:19
  15.4 2.7 %collective-permute-done.1 = bf16[12,3072]{1,0:T(8,128)(2,1)S(1)} collective-permute-done((bf16[12,3072]{1,0:T(8,128)(2,1)S(1)}, bf16[12,3072]{1,0:T(8,128)(2,1)S(1)}, u32[]{:S(2)}, u32[]{:S(2)}) %collective-permute-start.1) | collective-permute-done | bytes 73760 | tf_op jit(solution)/shard_map/ppermute | solution.py:19
  18.1 1.9 %collective-permute-start.2 = (bf16[24,3072]{1,0:T(8,128)(2,1)S(1)}, bf16[24,3072]{1,0:T(8,128)(2,1)S(1)}, u32[]{:S(2)}, u32[]{:S(2)}) collective-permute-start(bf16[24,3072]{1,0:T(8,128)(2,1)S(1)} %pad_maximum_fusion.3), channel_id=1, source_target_pairs={{0,1},{1,0},{2,3},{3,2},{4,5},{5,4},{6,7},{7,6},{8,9},{9,8},{10,11... | collective-permute-start | bytes 442376 | tf_op jit(solution)/shard_map/ppermute | solution.py:19
  20.1 1.3 %collective-permute-done.2 = bf16[24,3072]{1,0:T(8,128)(2,1)S(1)} collective-permute-done((bf16[24,3072]{1,0:T(8,128)(2,1)S(1)}, bf16[24,3072]{1,0:T(8,128)(2,1)S(1)}, u32[]{:S(2)}, u32[]{:S(2)}) %collective-permute-start.2) | collective-permute-done | bytes 147488 | tf_op jit(solution)/shard_map/ppermute | solution.py:19
  27.1 2.0 %collective-permute-start.3 = (bf16[408,512]{1,0:T(8,128)(2,1)S(1)}, bf16[408,512]{1,0:T(8,128)(2,1)S(1)}, u32[]{:S(2)}, u32[]{:S(2)}) collective-permute-start(bf16[408,512]{1,0:T(8,128)(2,1)S(1)} %pad_maximum_fusion.2), channel_id=1, source_target_pairs={{0,1},{1,0},{2,3},{3,2},{4,5},{5,4},{6,7},{7,6},{8,9},{9,8},{10,11... | collective-permute-start | bytes 1253384 | tf_op jit(solution)/shard_map/ppermute | solution.py:19
  29.3 1.4 %collective-permute-done.3 = bf16[408,512]{1,0:T(8,128)(2,1)S(1)} collective-permute-done((bf16[408,512]{1,0:T(8,128)(2,1)S(1)}, bf16[408,512]{1,0:T(8,128)(2,1)S(1)}, u32[]{:S(2)}, u32[]{:S(2)}) %collective-permute-start.3) | collective-permute-done | bytes 417824 | tf_op jit(solution)/shard_map/ppermute | solution.py:19
  30.9 1.6 %fusion.14 = f32[24,16,512]{2,1,0:T(8,128)S(1)} fusion(bf16[24,16,512]{2,1,0:T(8,128)(2,1)S(1)} %bitcast.128, f32[48,16,512]{2,1,0:T(8,128)} %copy-done.1, f32[24,16]{1,0:T(8,128)S(1)} %get-tuple-element.26, f32[24,16]{1,0:T(8,128)S(1)} %get-tuple-element.25, pred[]{:T(512)S(6)} %eq.57), kind=kLoop, calls=%fused_computation.28 | loop fusion | flops 983040 | bytes 2755585 | tf_op jit(solution)/shard_map/add | solution.py:86
  32.7 2.8 %collective-permute-start.4 = (bf16[102,512]{1,0:T(8,128)(2,1)S(1)}, bf16[102,512]{1,0:T(8,128)(2,1)S(1)}, u32[]{:S(2)}, u32[]{:S(2)}) collective-permute-start(bf16[102,512]{1,0:T(8,128)(2,1)S(1)} %pad_maximum_fusion.4), channel_id=1, source_target_pairs={{0,4},{1,5},{2,6},{3,7},{4,0},{5,1},{6,2},{7,3},{8,12},{9,13},{10,... | collective-permute-start | bytes 313352 | tf_op jit(solution)/shard_map/ppermute | solution.py:25
  35.6 4.4 %collective-permute-start.6 = (bf16[102,512]{1,0:T(8,128)(2,1)S(1)}, bf16[102,512]{1,0:T(8,128)(2,1)S(1)}, u32[]{:S(2)}, u32[]{:S(2)}) collective-permute-start(bf16[102,512]{1,0:T(8,128)(2,1)S(1)} %pad_maximum_fusion.6), channel_id=1, source_target_pairs={{0,6},{1,7},{2,0},{3,1},{4,2},{5,3},{6,4},{7,5},{8,14},{9,15},{10,... | collective-permute-start | bytes 313352 | tf_op jit(solution)/shard_map/ppermute | solution.py:25
  40.1 2.1 %collective-permute-start.5 = (bf16[102,512]{1,0:T(8,128)(2,1)S(1)}, bf16[102,512]{1,0:T(8,128)(2,1)S(1)}, u32[]{:S(2)}, u32[]{:S(2)}) collective-permute-start(bf16[102,512]{1,0:T(8,128)(2,1)S(1)} %pad_maximum_fusion.5), channel_id=1, source_target_pairs={{0,2},{1,3},{2,4},{3,5},{4,6},{5,7},{6,0},{7,1},{8,10},{9,11},{10,... | collective-permute-start | bytes 313352 | tf_op jit(solution)/shard_map/ppermute | solution.py:25
  42.4 5.7 %collective-permute-done.5 = bf16[102,512]{1,0:T(8,128)(2,1)S(1)} collective-permute-done((bf16[102,512]{1,0:T(8,128)(2,1)S(1)}, bf16[102,512]{1,0:T(8,128)(2,1)S(1)}, u32[]{:S(2)}, u32[]{:S(2)}) %collective-permute-start.5) | collective-permute-done | bytes 104480 | tf_op jit(solution)/shard_map/ppermute | solution.py:25
  49.7 15.2 %all-to-all-start = ((bf16[16,6,512]{2,1,0:T(8,128)(2,1)}), bf16[16,6,512]{2,1,0:T(8,128)(2,1)S(1)}, u32[]{:S(2)}, u32[]{:S(2)}) async-start(bf16[16,6,512]{2,1,0:T(8,128)(2,1)} %fusion.32), calls=%async_computation | async-start | bytes 262144 | tf_op jit(solution)/shard_map/all_to_all | solution.py:202
  65.0 13.4 %all-to-all-done = bf16[16,6,512]{2,1,0:T(8,128)(2,1)S(1)} async-done(((bf16[16,6,512]{2,1,0:T(8,128)(2,1)}), bf16[16,6,512]{2,1,0:T(8,128)(2,1)S(1)}, u32[]{:S(2)}, u32[]{:S(2)}) %all-to-all-start) | async-done | bytes 98336 | tf_op jit(solution)/shard_map/all_to_all | solution.py:202
  79.0 1.3 %fusion.4 = f32[96,2048]{1,0:T(8,128)S(1)} fusion(bf16[128,2048]{1,0:T(8,128)(2,1)S(1)} %copy-done.2, bf16[96,512]{1,0:T(8,128)(2,1)S(1)} %reshape.106, bf16[1,512,128]{2,1,0:T(8,128)(2,1)} %param.20), kind=kOutput, calls=%fused_computation.15 | convolution fusion | flops 62926848 | bytes 1540096 | tf_op jit(solution)/shard_map/dot_general | solution.py:211
  80.3 3.0 %collective-permute-start.7 = (bf16[48,2048]{1,0:T(8,128)(2,1)S(1)}, bf16[48,2048]{1,0:T(8,128)(2,1)S(1)}, u32[]{:S(2)}, u32[]{:S(2)}) collective-permute-start(bf16[48,2048]{1,0:T(8,128)(2,1)S(1)} %select_convert_fusion.1), channel_id=1, source_target_pairs={{0,32},{32,0},{64,96},{96,64},{128,160},{160,128},{192,224},{224,1... | collective-permute-start | bytes 589832 | tf_op jit(solution)/shard_map/ppermute | solution.py:19
  83.3 4.6 %collective-permute-done.7 = bf16[48,2048]{1,0:T(8,128)(2,1)S(1)} collective-permute-done((bf16[48,2048]{1,0:T(8,128)(2,1)S(1)}, bf16[48,2048]{1,0:T(8,128)(2,1)S(1)}, u32[]{:S(2)}, u32[]{:S(2)}) %collective-permute-start.7) | collective-permute-done | bytes 196640 | tf_op jit(solution)/shard_map/ppermute | solution.py:19
  88.0 3.2 %collective-permute-start.8 = (bf16[24,2048]{1,0:T(8,128)(2,1)S(1)}, bf16[24,2048]{1,0:T(8,128)(2,1)S(1)}, u32[]{:S(2)}, u32[]{:S(2)}) collective-permute-start(bf16[24,2048]{1,0:T(8,128)(2,1)S(1)} %select_convert_fusion.2), channel_id=1, source_target_pairs={{0,64},{64,0},{32,96},{96,32},{128,192},{192,128},{160,224},{224,1... | collective-permute-start | bytes 294920 | tf_op jit(solution)/shard_map/ppermute | solution.py:19
  91.3 5.1 %collective-permute-done.8 = bf16[24,2048]{1,0:T(8,128)(2,1)S(1)} collective-permute-done((bf16[24,2048]{1,0:T(8,128)(2,1)S(1)}, bf16[24,2048]{1,0:T(8,128)(2,1)S(1)}, u32[]{:S(2)}, u32[]{:S(2)}) %collective-permute-start.8) | collective-permute-done | bytes 98336 | tf_op jit(solution)/shard_map/ppermute | solution.py:19
  96.5 4.2 %collective-permute-start.9 = (bf16[6,2048]{1,0:T(8,128)(2,1)S(1)}, bf16[6,2048]{1,0:T(8,128)(2,1)S(1)}, u32[]{:S(2)}, u32[]{:S(2)}) collective-permute-start(bf16[6,2048]{1,0:T(8,128)(2,1)S(1)} %get-tuple-element.34), channel_id=1, source_target_pairs={{0,256},{32,288},{64,320},{96,352},{128,384},{160,416},{192,448},{... | collective-permute-start | bytes 73736 | tf_op jit(solution)/shard_map/ppermute | solution.py:25
  100.8 6.9 %collective-permute-start.11 = (bf16[6,2048]{1,0:T(8,128)(2,1)S(1)}, bf16[6,2048]{1,0:T(8,128)(2,1)S(1)}, u32[]{:S(2)}, u32[]{:S(2)}) collective-permute-start(bf16[6,2048]{1,0:T(8,128)(2,1)S(1)} %get-tuple-element.35), channel_id=1, source_target_pairs={{0,384},{32,416},{64,448},{96,480},{128,0},{160,32},{192,64},{224,... | collective-permute-start | bytes 73736 | tf_op jit(solution)/shard_map/ppermute | solution.py:25
  107.7 2.9 %collective-permute-start.10 = (bf16[6,2048]{1,0:T(8,128)(2,1)S(1)}, bf16[6,2048]{1,0:T(8,128)(2,1)S(1)}, u32[]{:S(2)}, u32[]{:S(2)}) collective-permute-start(bf16[6,2048]{1,0:T(8,128)(2,1)S(1)} %get-tuple-element.36), channel_id=1, source_target_pairs={{0,128},{32,160},{64,192},{96,224},{128,256},{160,288},{192,320},{... | collective-permute-start | bytes 73736 | tf_op jit(solution)/shard_map/ppermute | solution.py:25
  110.6 1.5 %collective-permute-done.9 = bf16[6,2048]{1,0:T(8,128)(2,1)S(1)} collective-permute-done((bf16[6,2048]{1,0:T(8,128)(2,1)S(1)}, bf16[6,2048]{1,0:T(8,128)(2,1)S(1)}, u32[]{:S(2)}, u32[]{:S(2)}) %collective-permute-start.9) | collective-permute-done | bytes 24608 | tf_op jit(solution)/shard_map/ppermute | solution.py:25
  112.1 5.3 %collective-permute-done.10 = bf16[6,2048]{1,0:T(8,128)(2,1)S(1)} collective-permute-done((bf16[6,2048]{1,0:T(8,128)(2,1)S(1)}, bf16[6,2048]{1,0:T(8,128)(2,1)S(1)}, u32[]{:S(2)}, u32[]{:S(2)}) %collective-permute-start.10) | collective-permute-done | bytes 24608 | tf_op jit(solution)/shard_map/ppermute | solution.py:25
  (100 shorter events, 16.9 us)
Async XLA Ops:
  0.0 21.7 %copy-start = (bf16[16,512,128]{2,1,0:T(8,128)(2,1)S(1)}, bf16[16,512,128]{2,1,0:T(8,128)(2,1)}, u32[]{:S(2)}) copy-start(bf16[16,512,128]{2,1,0:T(8,128)(2,1)} %param.19) | copy-start | bytes 6291460
  1.6 9.8 %collective-permute-start = (bf16[6,3072]{1,0:T(8,128)(2,1)S(1)}, bf16[6,3072]{1,0:T(8,128)(2,1)S(1)}, u32[]{:S(2)}, u32[]{:S(2)}) collective-permute-start(bf16[6,3072]{1,0:T(8,128)(2,1)S(1)} %constant_dynamic-update-slice_fusion), channel_id=1, source_target_pairs={{0,4},{4,0},{1,5},{5,1},{2,6},{6,2},{3,7},{7,3},{8,12},{12,8},{9,1... | collective-permute-start | bytes 110600 | tf_op jit(solution)/shard_map/ppermute | solution.py:19
  11.5 6.5 %collective-permute-start.1 = (bf16[12,3072]{1,0:T(8,128)(2,1)S(1)}, bf16[12,3072]{1,0:T(8,128)(2,1)S(1)}, u32[]{:S(2)}, u32[]{:S(2)}) collective-permute-start(bf16[12,3072]{1,0:T(8,128)(2,1)S(1)} %pad_maximum_fusion.8), channel_id=1, source_target_pairs={{0,2},{2,0},{1,3},{3,1},{4,6},{6,4},{5,7},{7,5},{8,10},{10,8},{9,1... | collective-permute-start | bytes 221192 | tf_op jit(solution)/shard_map/ppermute | solution.py:19
  18.1 3.3 %collective-permute-start.2 = (bf16[24,3072]{1,0:T(8,128)(2,1)S(1)}, bf16[24,3072]{1,0:T(8,128)(2,1)S(1)}, u32[]{:S(2)}, u32[]{:S(2)}) collective-permute-start(bf16[24,3072]{1,0:T(8,128)(2,1)S(1)} %pad_maximum_fusion.3), channel_id=1, source_target_pairs={{0,1},{1,0},{2,3},{3,2},{4,5},{5,4},{6,7},{7,6},{8,9},{9,8},{10,11... | collective-permute-start | bytes 442376 | tf_op jit(solution)/shard_map/ppermute | solution.py:19
  21.7 1.1 copy-start.4
  21.7 1.1 copy-start.5
  25.7 1.2 copy-start.1
  27.1 3.7 %collective-permute-start.3 = (bf16[408,512]{1,0:T(8,128)(2,1)S(1)}, bf16[408,512]{1,0:T(8,128)(2,1)S(1)}, u32[]{:S(2)}, u32[]{:S(2)}) collective-permute-start(bf16[408,512]{1,0:T(8,128)(2,1)S(1)} %pad_maximum_fusion.2), channel_id=1, source_target_pairs={{0,1},{1,0},{2,3},{3,2},{4,5},{5,4},{6,7},{7,6},{8,9},{9,8},{10,11... | collective-permute-start | bytes 1253384 | tf_op jit(solution)/shard_map/ppermute | solution.py:19
  32.7 9.5 %collective-permute-start.4 = (bf16[102,512]{1,0:T(8,128)(2,1)S(1)}, bf16[102,512]{1,0:T(8,128)(2,1)S(1)}, u32[]{:S(2)}, u32[]{:S(2)}) collective-permute-start(bf16[102,512]{1,0:T(8,128)(2,1)S(1)} %pad_maximum_fusion.4), channel_id=1, source_target_pairs={{0,4},{1,5},{2,6},{3,7},{4,0},{5,1},{6,2},{7,3},{8,12},{9,13},{10,... | collective-permute-start | bytes 313352 | tf_op jit(solution)/shard_map/ppermute | solution.py:25
  35.5 29.4 %copy-start.3 = (s32[16]{0:T(128)S(1)}, s32[16]{0:T(128)}, u32[]{:S(2)}) copy-start(s32[16]{0:T(128)} %constant.246) | copy-start | bytes 196
  35.6 6.7 %collective-permute-start.6 = (bf16[102,512]{1,0:T(8,128)(2,1)S(1)}, bf16[102,512]{1,0:T(8,128)(2,1)S(1)}, u32[]{:S(2)}, u32[]{:S(2)}) collective-permute-start(bf16[102,512]{1,0:T(8,128)(2,1)S(1)} %pad_maximum_fusion.6), channel_id=1, source_target_pairs={{0,6},{1,7},{2,0},{3,1},{4,2},{5,3},{6,4},{7,5},{8,14},{9,15},{10,... | collective-permute-start | bytes 313352 | tf_op jit(solution)/shard_map/ppermute | solution.py:25
  40.1 38.9 %copy-start.2 = (bf16[128,2048]{1,0:T(8,128)(2,1)S(1)}, bf16[128,2048]{1,0:T(8,128)(2,1)}, u32[]{:S(2)}) copy-start(bf16[128,2048]{1,0:T(8,128)(2,1)} %param.21) | copy-start | bytes 1572868
  40.1 7.9 %collective-permute-start.5 = (bf16[102,512]{1,0:T(8,128)(2,1)S(1)}, bf16[102,512]{1,0:T(8,128)(2,1)S(1)}, u32[]{:S(2)}, u32[]{:S(2)}) collective-permute-start(bf16[102,512]{1,0:T(8,128)(2,1)S(1)} %pad_maximum_fusion.5), channel_id=1, source_target_pairs={{0,2},{1,3},{2,4},{3,5},{4,6},{5,7},{6,0},{7,1},{8,10},{9,11},{10,... | collective-permute-start | bytes 313352 | tf_op jit(solution)/shard_map/ppermute | solution.py:25
  49.7 28.6 %all-to-all-start = ((bf16[16,6,512]{2,1,0:T(8,128)(2,1)}), bf16[16,6,512]{2,1,0:T(8,128)(2,1)S(1)}, u32[]{:S(2)}, u32[]{:S(2)}) async-start(bf16[16,6,512]{2,1,0:T(8,128)(2,1)} %fusion.32), calls=%async_computation | async-start | bytes 262144 | tf_op jit(solution)/shard_map/all_to_all | solution.py:202
  80.3 7.6 %collective-permute-start.7 = (bf16[48,2048]{1,0:T(8,128)(2,1)S(1)}, bf16[48,2048]{1,0:T(8,128)(2,1)S(1)}, u32[]{:S(2)}, u32[]{:S(2)}) collective-permute-start(bf16[48,2048]{1,0:T(8,128)(2,1)S(1)} %select_convert_fusion.1), channel_id=1, source_target_pairs={{0,32},{32,0},{64,96},{96,64},{128,160},{160,128},{192,224},{224,1... | collective-permute-start | bytes 589832 | tf_op jit(solution)/shard_map/ppermute | solution.py:19
  88.0 8.5 %collective-permute-start.8 = (bf16[24,2048]{1,0:T(8,128)(2,1)S(1)}, bf16[24,2048]{1,0:T(8,128)(2,1)S(1)}, u32[]{:S(2)}, u32[]{:S(2)}) collective-permute-start(bf16[24,2048]{1,0:T(8,128)(2,1)S(1)} %select_convert_fusion.2), channel_id=1, source_target_pairs={{0,64},{64,0},{32,96},{96,32},{128,192},{192,128},{160,224},{224,1... | collective-permute-start | bytes 294920 | tf_op jit(solution)/shard_map/ppermute | solution.py:19
  96.5 15.6 %collective-permute-start.9 = (bf16[6,2048]{1,0:T(8,128)(2,1)S(1)}, bf16[6,2048]{1,0:T(8,128)(2,1)S(1)}, u32[]{:S(2)}, u32[]{:S(2)}) collective-permute-start(bf16[6,2048]{1,0:T(8,128)(2,1)S(1)} %get-tuple-element.34), channel_id=1, source_target_pairs={{0,256},{32,288},{64,320},{96,352},{128,384},{160,416},{192,448},{... | collective-permute-start | bytes 73736 | tf_op jit(solution)/shard_map/ppermute | solution.py:25
  100.8 11.3 %collective-permute-start.11 = (bf16[6,2048]{1,0:T(8,128)(2,1)S(1)}, bf16[6,2048]{1,0:T(8,128)(2,1)S(1)}, u32[]{:S(2)}, u32[]{:S(2)}) collective-permute-start(bf16[6,2048]{1,0:T(8,128)(2,1)S(1)} %get-tuple-element.35), channel_id=1, source_target_pairs={{0,384},{32,416},{64,448},{96,480},{128,0},{160,32},{192,64},{224,... | collective-permute-start | bytes 73736 | tf_op jit(solution)/shard_map/ppermute | solution.py:25
  107.7 9.7 %collective-permute-start.10 = (bf16[6,2048]{1,0:T(8,128)(2,1)S(1)}, bf16[6,2048]{1,0:T(8,128)(2,1)S(1)}, u32[]{:S(2)}, u32[]{:S(2)}) collective-permute-start(bf16[6,2048]{1,0:T(8,128)(2,1)S(1)} %get-tuple-element.36), channel_id=1, source_target_pairs={{0,128},{32,160},{64,192},{96,224},{128,256},{160,288},{192,320},{... | collective-permute-start | bytes 73736 | tf_op jit(solution)/shard_map/ppermute | solution.py:25

commit v11 on v9

--- a/solution.py
+++ b/solution.py
@@ -203,7 +203,7 @@
         )
 
     total_rows = block_for(mine)
-    for step in sorted(range(1, ring), key=lambda s: -min(s, ring - s)):
+    for step in sorted(range(1, ring), key=lambda s: (-min(s, ring - s), -s)):
         sent = block_for((mine + step) % ring).astype(jnp.bfloat16)
         total_rows = total_rows + shifted(sent, "grp", grp_size, 4 * step).astype(jnp.float32)
     return total_rows.astype(jnp.bfloat16)

time: 117 us -> 117 us (level)
  no operation moved by 1% of the time
where the time goes in v11:
time: 117 us; the launch traced here: 116 us
  starting transfers between devices  52.3 us (45%)
  waiting for transfers between devices  46.2 us (39%)
  local copies, waits for them, and re-layouts  6.04 us (5%)
  other arithmetic  5.4 us (5%)
  matrix products  5.14 us (4%)
    ppermute x8, waiting for transfers between devices, from_partner(): return lax.ppermute(block, axis, route)  27.2 us
    ppermute x8, starting transfers between devices, from_partner(): return lax.ppermute(block, axis, route)  23.2 us
    all_to_all x1, starting transfers between devices, per_device(): lax.all_to_all(jnp.swapaxes(merged.astype(jnp.bfloat16), 0, 1), 'grp', sp...  15.2 us
    ppermute x3, starting transfers between devices, shifted(): return lax.ppermute(block, axis, route)  14 us
    all_to_all x1, waiting for transfers between devices, per_device(): lax.all_to_all(jnp.swapaxes(merged.astype(jnp.bfloat16), 0, 1), 'grp', sp...  13.4 us
    ppermute x3, waiting for transfers between devices, shifted(): return lax.ppermute(block, axis, route)  5.62 us
  transfers between devices with their start and end apart: 12, of which 10 were waited for; matrix products, arithmetic and copies ran while one was open for 5% of the time, Pallas kernels for 0%

profile of v11, /device:TPU:6, one launch (start us, length us, event | category | flops | bytes accessed | tf_op | source)
XLA Modules:
  0.0 115.9 jit_solution(3686252337792931426)
XLA Ops:
  1.6 5.1 %collective-permute-start = (bf16[6,3072]{1,0:T(8,128)(2,1)S(1)}, bf16[6,3072]{1,0:T(8,128)(2,1)S(1)}, u32[]{:S(2)}, u32[]{:S(2)}) collective-permute-start(bf16[6,3072]{1,0:T(8,128)(2,1)S(1)} %constant_dynamic-update-slice_fusion), channel_id=1, source_target_pairs={{0,4},{4,0},{1,5},{5,1},{2,6},{6,2},{3,7},{7,3},{8,12},{12,8},{9,1... | collective-permute-start | bytes 110600 | tf_op jit(solution)/shard_map/ppermute | solution.py:19
  6.8 1.2 %dynamic_slice.24 = s32[1]{0:T(128)} dynamic-slice(s32[4]{0:T(128)} %param.17, s32[]{:T(128)S(6)} %select_n.241), dynamic_slice_sizes={1} | dynamic-slice | bytes 12 | tf_op jit(solution)/shard_map/jit(dynamic_index_in_dim)/dynamic_slice | solution.py:135
  11.5 2.6 %collective-permute-start.1 = (bf16[12,3072]{1,0:T(8,128)(2,1)S(1)}, bf16[12,3072]{1,0:T(8,128)(2,1)S(1)}, u32[]{:S(2)}, u32[]{:S(2)}) collective-permute-start(bf16[12,3072]{1,0:T(8,128)(2,1)S(1)} %pad_maximum_fusion.7), channel_id=1, source_target_pairs={{0,2},{2,0},{1,3},{3,1},{4,6},{6,4},{5,7},{7,5},{8,10},{10,8},{9,1... | collective-permute-start | bytes 221192 | tf_op jit(solution)/shard_map/ppermute | solution.py:19
  15.4 2.7 %collective-permute-done.1 = bf16[12,3072]{1,0:T(8,128)(2,1)S(1)} collective-permute-done((bf16[12,3072]{1,0:T(8,128)(2,1)S(1)}, bf16[12,3072]{1,0:T(8,128)(2,1)S(1)}, u32[]{:S(2)}, u32[]{:S(2)}) %collective-permute-start.1) | collective-permute-done | bytes 73760 | tf_op jit(solution)/shard_map/ppermute | solution.py:19
  18.1 1.9 %collective-permute-start.2 = (bf16[24,3072]{1,0:T(8,128)(2,1)S(1)}, bf16[24,3072]{1,0:T(8,128)(2,1)S(1)}, u32[]{:S(2)}, u32[]{:S(2)}) collective-permute-start(bf16[24,3072]{1,0:T(8,128)(2,1)S(1)} %pad_maximum_fusion.4), channel_id=1, source_target_pairs={{0,1},{1,0},{2,3},{3,2},{4,5},{5,4},{6,7},{7,6},{8,9},{9,8},{10,11... | collective-permute-start | bytes 442376 | tf_op jit(solution)/shard_map/ppermute | solution.py:19
  20.1 1.3 %collective-permute-done.2 = bf16[24,3072]{1,0:T(8,128)(2,1)S(1)} collective-permute-done((bf16[24,3072]{1,0:T(8,128)(2,1)S(1)}, bf16[24,3072]{1,0:T(8,128)(2,1)S(1)}, u32[]{:S(2)}, u32[]{:S(2)}) %collective-permute-start.2) | collective-permute-done | bytes 147488 | tf_op jit(solution)/shard_map/ppermute | solution.py:19
  22.8 1.1 fusion
  25.9 2.0 %collective-permute-start.3 = (bf16[408,512]{1,0:T(8,128)(2,1)S(1)}, bf16[408,512]{1,0:T(8,128)(2,1)S(1)}, u32[]{:S(2)}, u32[]{:S(2)}) collective-permute-start(bf16[408,512]{1,0:T(8,128)(2,1)S(1)} %pad_maximum_fusion.2), channel_id=1, source_target_pairs={{0,1},{1,0},{2,3},{3,2},{4,5},{5,4},{6,7},{7,6},{8,9},{9,8},{10,11... | collective-permute-start | bytes 1253384 | tf_op jit(solution)/shard_map/ppermute | solution.py:19
  28.0 1.6 %collective-permute-done.3 = bf16[408,512]{1,0:T(8,128)(2,1)S(1)} collective-permute-done((bf16[408,512]{1,0:T(8,128)(2,1)S(1)}, bf16[408,512]{1,0:T(8,128)(2,1)S(1)}, u32[]{:S(2)}, u32[]{:S(2)}) %collective-permute-start.3) | collective-permute-done | bytes 417824 | tf_op jit(solution)/shard_map/ppermute | solution.py:19
  30.2 2.6 %collective-permute-start.4 = (bf16[204,512]{1,0:T(8,128)(2,1)S(1)}, bf16[204,512]{1,0:T(8,128)(2,1)S(1)}, u32[]{:S(2)}, u32[]{:S(2)}) collective-permute-start(bf16[204,512]{1,0:T(8,128)(2,1)S(1)} %pad_maximum_fusion.3), channel_id=1, source_target_pairs={{0,2},{2,0},{1,3},{3,1},{4,6},{6,4},{5,7},{7,5},{8,10},{10,8},{9,1... | collective-permute-start | bytes 626696 | tf_op jit(solution)/shard_map/ppermute | solution.py:19
  32.7 6.6 %collective-permute-done.4 = bf16[204,512]{1,0:T(8,128)(2,1)S(1)} collective-permute-done((bf16[204,512]{1,0:T(8,128)(2,1)S(1)}, bf16[204,512]{1,0:T(8,128)(2,1)S(1)}, u32[]{:S(2)}, u32[]{:S(2)}) %collective-permute-start.4) | collective-permute-done | bytes 208928 | tf_op jit(solution)/shard_map/ppermute | solution.py:19
  39.8 2.8 %collective-permute-start.5 = (bf16[102,512]{1,0:T(8,128)(2,1)S(1)}, bf16[102,512]{1,0:T(8,128)(2,1)S(1)}, u32[]{:S(2)}, u32[]{:S(2)}) collective-permute-start(bf16[102,512]{1,0:T(8,128)(2,1)S(1)} %pad_maximum_fusion.5), channel_id=1, source_target_pairs={{0,4},{4,0},{1,5},{5,1},{2,6},{6,2},{3,7},{7,3},{8,12},{12,8},{9,1... | collective-permute-start | bytes 313352 | tf_op jit(solution)/shard_map/ppermute | solution.py:19
  42.5 5.3 %collective-permute-done.5 = bf16[102,512]{1,0:T(8,128)(2,1)S(1)} collective-permute-done((bf16[102,512]{1,0:T(8,128)(2,1)S(1)}, bf16[102,512]{1,0:T(8,128)(2,1)S(1)}, u32[]{:S(2)}, u32[]{:S(2)}) %collective-permute-start.5) | collective-permute-done | bytes 104480 | tf_op jit(solution)/shard_map/ppermute | solution.py:19
  48.8 15.2 %all-to-all-start = ((bf16[16,6,512]{2,1,0:T(8,128)(2,1)}), bf16[16,6,512]{2,1,0:T(8,128)(2,1)S(1)}, u32[]{:S(2)}, u32[]{:S(2)}) async-start(bf16[16,6,512]{2,1,0:T(8,128)(2,1)} %copy.49), calls=%async_computation | async-start | bytes 262144 | tf_op jit(solution)/shard_map/all_to_all | solution.py:176
  64.0 13.4 %all-to-all-done = bf16[16,6,512]{2,1,0:T(8,128)(2,1)S(1)} async-done(((bf16[16,6,512]{2,1,0:T(8,128)(2,1)}), bf16[16,6,512]{2,1,0:T(8,128)(2,1)S(1)}, u32[]{:S(2)}, u32[]{:S(2)}) %all-to-all-start) | async-done | bytes 98336 | tf_op jit(solution)/shard_map/all_to_all | solution.py:176
  78.1 1.3 %fusion.4 = f32[96,2048]{1,0:T(8,128)S(1)} fusion(bf16[128,2048]{1,0:T(8,128)(2,1)S(1)} %copy-done.1, bf16[96,512]{1,0:T(8,128)(2,1)S(1)} %reshape.87, bf16[1,512,128]{2,1,0:T(8,128)(2,1)} %param.20), kind=kOutput, calls=%fused_computation.15 | convolution fusion | flops 62926848 | bytes 1540096 | tf_op jit(solution)/shard_map/dot_general | solution.py:185
  79.4 2.9 %collective-permute-start.6 = (bf16[48,2048]{1,0:T(8,128)(2,1)S(1)}, bf16[48,2048]{1,0:T(8,128)(2,1)S(1)}, u32[]{:S(2)}, u32[]{:S(2)}) collective-permute-start(bf16[48,2048]{1,0:T(8,128)(2,1)S(1)} %select_convert_fusion.1), channel_id=1, source_target_pairs={{0,32},{32,0},{64,96},{96,64},{128,160},{160,128},{192,224},{224,1... | collective-permute-start | bytes 589832 | tf_op jit(solution)/shard_map/ppermute | solution.py:19
  82.3 4.6 %collective-permute-done.6 = bf16[48,2048]{1,0:T(8,128)(2,1)S(1)} collective-permute-done((bf16[48,2048]{1,0:T(8,128)(2,1)S(1)}, bf16[48,2048]{1,0:T(8,128)(2,1)S(1)}, u32[]{:S(2)}, u32[]{:S(2)}) %collective-permute-start.6) | collective-permute-done | bytes 196640 | tf_op jit(solution)/shard_map/ppermute | solution.py:19
  87.0 3.2 %collective-permute-start.7 = (bf16[24,2048]{1,0:T(8,128)(2,1)S(1)}, bf16[24,2048]{1,0:T(8,128)(2,1)S(1)}, u32[]{:S(2)}, u32[]{:S(2)}) collective-permute-start(bf16[24,2048]{1,0:T(8,128)(2,1)S(1)} %select_convert_fusion.3), channel_id=1, source_target_pairs={{0,64},{64,0},{32,96},{96,32},{128,192},{192,128},{160,224},{224,1... | collective-permute-start | bytes 294920 | tf_op jit(solution)/shard_map/ppermute | solution.py:19
  90.4 5.1 %collective-permute-done.7 = bf16[24,2048]{1,0:T(8,128)(2,1)S(1)} collective-permute-done((bf16[24,2048]{1,0:T(8,128)(2,1)S(1)}, bf16[24,2048]{1,0:T(8,128)(2,1)S(1)}, u32[]{:S(2)}, u32[]{:S(2)}) %collective-permute-start.7) | collective-permute-done | bytes 98336 | tf_op jit(solution)/shard_map/ppermute | solution.py:19
  95.6 4.2 %collective-permute-start.8 = (bf16[6,2048]{1,0:T(8,128)(2,1)S(1)}, bf16[6,2048]{1,0:T(8,128)(2,1)S(1)}, u32[]{:S(2)}, u32[]{:S(2)}) collective-permute-start(bf16[6,2048]{1,0:T(8,128)(2,1)S(1)} %get-tuple-element.24), channel_id=1, source_target_pairs={{0,256},{32,288},{64,320},{96,352},{128,384},{160,416},{192,448},{... | collective-permute-start | bytes 73736 | tf_op jit(solution)/shard_map/ppermute | solution.py:25
  99.8 5.7 %collective-permute-start.10 = (bf16[6,2048]{1,0:T(8,128)(2,1)S(1)}, bf16[6,2048]{1,0:T(8,128)(2,1)S(1)}, u32[]{:S(2)}, u32[]{:S(2)}) collective-permute-start(bf16[6,2048]{1,0:T(8,128)(2,1)S(1)} %get-tuple-element.25), channel_id=1, source_target_pairs={{0,128},{32,160},{64,192},{96,224},{128,256},{160,288},{192,320},{... | collective-permute-start | bytes 73736 | tf_op jit(solution)/shard_map/ppermute | solution.py:25
  105.5 4.1 %collective-permute-start.9 = (bf16[6,2048]{1,0:T(8,128)(2,1)S(1)}, bf16[6,2048]{1,0:T(8,128)(2,1)S(1)}, u32[]{:S(2)}, u32[]{:S(2)}) collective-permute-start(bf16[6,2048]{1,0:T(8,128)(2,1)S(1)} %get-tuple-element.26), channel_id=1, source_target_pairs={{0,384},{32,416},{64,448},{96,480},{128,0},{160,32},{192,64},{224,... | collective-permute-start | bytes 73736 | tf_op jit(solution)/shard_map/ppermute | solution.py:25
  110.5 4.7 %collective-permute-done.9 = bf16[6,2048]{1,0:T(8,128)(2,1)S(1)} collective-permute-done((bf16[6,2048]{1,0:T(8,128)(2,1)S(1)}, bf16[6,2048]{1,0:T(8,128)(2,1)S(1)}, u32[]{:S(2)}, u32[]{:S(2)}) %collective-permute-start.9) | collective-permute-done | bytes 24608 | tf_op jit(solution)/shard_map/ppermute | solution.py:25
  (84 shorter events, 13.8 us)
Async XLA Ops:
  0.0 21.7 %copy-start = (bf16[16,512,128]{2,1,0:T(8,128)(2,1)S(1)}, bf16[16,512,128]{2,1,0:T(8,128)(2,1)}, u32[]{:S(2)}) copy-start(bf16[16,512,128]{2,1,0:T(8,128)(2,1)} %param.19) | copy-start | bytes 6291460
  1.6 9.8 %collective-permute-start = (bf16[6,3072]{1,0:T(8,128)(2,1)S(1)}, bf16[6,3072]{1,0:T(8,128)(2,1)S(1)}, u32[]{:S(2)}, u32[]{:S(2)}) collective-permute-start(bf16[6,3072]{1,0:T(8,128)(2,1)S(1)} %constant_dynamic-update-slice_fusion), channel_id=1, source_target_pairs={{0,4},{4,0},{1,5},{5,1},{2,6},{6,2},{3,7},{7,3},{8,12},{12,8},{9,1... | collective-permute-start | bytes 110600 | tf_op jit(solution)/shard_map/ppermute | solution.py:19
  11.5 6.5 %collective-permute-start.1 = (bf16[12,3072]{1,0:T(8,128)(2,1)S(1)}, bf16[12,3072]{1,0:T(8,128)(2,1)S(1)}, u32[]{:S(2)}, u32[]{:S(2)}) collective-permute-start(bf16[12,3072]{1,0:T(8,128)(2,1)S(1)} %pad_maximum_fusion.7), channel_id=1, source_target_pairs={{0,2},{2,0},{1,3},{3,1},{4,6},{6,4},{5,7},{7,5},{8,10},{10,8},{9,1... | collective-permute-start | bytes 221192 | tf_op jit(solution)/shard_map/ppermute | solution.py:19
  18.1 3.3 %collective-permute-start.2 = (bf16[24,3072]{1,0:T(8,128)(2,1)S(1)}, bf16[24,3072]{1,0:T(8,128)(2,1)S(1)}, u32[]{:S(2)}, u32[]{:S(2)}) collective-permute-start(bf16[24,3072]{1,0:T(8,128)(2,1)S(1)} %pad_maximum_fusion.4), channel_id=1, source_target_pairs={{0,1},{1,0},{2,3},{3,2},{4,5},{5,4},{6,7},{7,6},{8,9},{9,8},{10,11... | collective-permute-start | bytes 442376 | tf_op jit(solution)/shard_map/ppermute | solution.py:19
  21.7 1.1 copy-start.3
  21.7 1.1 copy-start.4
  25.9 3.7 %collective-permute-start.3 = (bf16[408,512]{1,0:T(8,128)(2,1)S(1)}, bf16[408,512]{1,0:T(8,128)(2,1)S(1)}, u32[]{:S(2)}, u32[]{:S(2)}) collective-permute-start(bf16[408,512]{1,0:T(8,128)(2,1)S(1)} %pad_maximum_fusion.2), channel_id=1, source_target_pairs={{0,1},{1,0},{2,3},{3,2},{4,5},{5,4},{6,7},{7,6},{8,9},{9,8},{10,11... | collective-permute-start | bytes 1253384 | tf_op jit(solution)/shard_map/ppermute | solution.py:19
  30.1 33.9 %copy-start.2 = (s32[16]{0:T(128)S(1)}, s32[16]{0:T(128)}, u32[]{:S(2)}) copy-start(s32[16]{0:T(128)} %constant.169) | copy-start | bytes 196
  30.2 9.2 %collective-permute-start.4 = (bf16[204,512]{1,0:T(8,128)(2,1)S(1)}, bf16[204,512]{1,0:T(8,128)(2,1)S(1)}, u32[]{:S(2)}, u32[]{:S(2)}) collective-permute-start(bf16[204,512]{1,0:T(8,128)(2,1)S(1)} %pad_maximum_fusion.3), channel_id=1, source_target_pairs={{0,2},{2,0},{1,3},{3,1},{4,6},{6,4},{5,7},{7,5},{8,10},{10,8},{9,1... | collective-permute-start | bytes 626696 | tf_op jit(solution)/shard_map/ppermute | solution.py:19
  39.5 38.6 %copy-start.1 = (bf16[128,2048]{1,0:T(8,128)(2,1)S(1)}, bf16[128,2048]{1,0:T(8,128)(2,1)}, u32[]{:S(2)}) copy-start(bf16[128,2048]{1,0:T(8,128)(2,1)} %param.21) | copy-start | bytes 1572868
  39.8 8.1 %collective-permute-start.5 = (bf16[102,512]{1,0:T(8,128)(2,1)S(1)}, bf16[102,512]{1,0:T(8,128)(2,1)S(1)}, u32[]{:S(2)}, u32[]{:S(2)}) collective-permute-start(bf16[102,512]{1,0:T(8,128)(2,1)S(1)} %pad_maximum_fusion.5), channel_id=1, source_target_pairs={{0,4},{4,0},{1,5},{5,1},{2,6},{6,2},{3,7},{7,3},{8,12},{12,8},{9,1... | collective-permute-start | bytes 313352 | tf_op jit(solution)/shard_map/ppermute | solution.py:19
  48.8 28.6 %all-to-all-start = ((bf16[16,6,512]{2,1,0:T(8,128)(2,1)}), bf16[16,6,512]{2,1,0:T(8,128)(2,1)S(1)}, u32[]{:S(2)}, u32[]{:S(2)}) async-start(bf16[16,6,512]{2,1,0:T(8,128)(2,1)} %copy.49), calls=%async_computation | async-start | bytes 262144 | tf_op jit(solution)/shard_map/all_to_all | solution.py:176
  79.4 7.6 %collective-permute-start.6 = (bf16[48,2048]{1,0:T(8,128)(2,1)S(1)}, bf16[48,2048]{1,0:T(8,128)(2,1)S(1)}, u32[]{:S(2)}, u32[]{:S(2)}) collective-permute-start(bf16[48,2048]{1,0:T(8,128)(2,1)S(1)} %select_convert_fusion.1), channel_id=1, source_target_pairs={{0,32},{32,0},{64,96},{96,64},{128,160},{160,128},{192,224},{224,1... | collective-permute-start | bytes 589832 | tf_op jit(solution)/shard_map/ppermute | solution.py:19
  87.0 8.5 %collective-permute-start.7 = (bf16[24,2048]{1,0:T(8,128)(2,1)S(1)}, bf16[24,2048]{1,0:T(8,128)(2,1)S(1)}, u32[]{:S(2)}, u32[]{:S(2)}) collective-permute-start(bf16[24,2048]{1,0:T(8,128)(2,1)S(1)} %select_convert_fusion.3), channel_id=1, source_target_pairs={{0,64},{64,0},{32,96},{96,32},{128,192},{192,128},{160,224},{224,1... | collective-permute-start | bytes 294920 | tf_op jit(solution)/shard_map/ppermute | solution.py:19
  95.6 14.9 %collective-permute-start.8 = (bf16[6,2048]{1,0:T(8,128)(2,1)S(1)}, bf16[6,2048]{1,0:T(8,128)(2,1)S(1)}, u32[]{:S(2)}, u32[]{:S(2)}) collective-permute-start(bf16[6,2048]{1,0:T(8,128)(2,1)S(1)} %get-tuple-element.24), channel_id=1, source_target_pairs={{0,256},{32,288},{64,320},{96,352},{128,384},{160,416},{192,448},{... | collective-permute-start | bytes 73736 | tf_op jit(solution)/shard_map/ppermute | solution.py:25
  99.8 10.7 %collective-permute-start.10 = (bf16[6,2048]{1,0:T(8,128)(2,1)S(1)}, bf16[6,2048]{1,0:T(8,128)(2,1)S(1)}, u32[]{:S(2)}, u32[]{:S(2)}) collective-permute-start(bf16[6,2048]{1,0:T(8,128)(2,1)S(1)} %get-tuple-element.25), channel_id=1, source_target_pairs={{0,128},{32,160},{64,192},{96,224},{128,256},{160,288},{192,320},{... | collective-permute-start | bytes 73736 | tf_op jit(solution)/shard_map/ppermute | solution.py:25
  105.5 9.7 %collective-permute-start.9 = (bf16[6,2048]{1,0:T(8,128)(2,1)S(1)}, bf16[6,2048]{1,0:T(8,128)(2,1)S(1)}, u32[]{:S(2)}, u32[]{:S(2)}) collective-permute-start(bf16[6,2048]{1,0:T(8,128)(2,1)S(1)} %get-tuple-element.26), channel_id=1, source_target_pairs={{0,384},{32,416},{64,448},{96,480},{128,0},{160,32},{192,64},{224,... | collective-permute-start | bytes 73736 | tf_op jit(solution)/shard_map/ppermute | solution.py:25

commit v12 on v11

--- a/solution.py
+++ b/solution.py
@@ -112,7 +112,8 @@
     local_rank = position % per_request
     local_request = position // per_request
     score_scale = 1.0 / math.sqrt(nope_width + rope_width)
-    raw_rows = jnp.concatenate([q_nope, q_rope], axis=1)
+    nope_cols, rope_cols = q_nope.shape[1], q_rope.shape[1]
+    raw_rows = jnp.pad(q_nope, ((0, 0), (0, rope_cols))) + jnp.pad(q_rope, ((0, 0), (nope_cols, 0)))
     for bit_level in reversed(range(doublings)):
         partner = from_partner(raw_rows, "ep", bit_level)
         raw_rows = append_partner(raw_rows, partner, position, bit_level)

time: 117 us -> 117 us (level)
  other arithmetic: 5.4 us -> 7.12 us
  local copies, waits for them, and re-layouts: 6.04 us -> 4.41 us
where the time goes in v12:
time: 117 us; the launch traced here: 116 us
  starting transfers between devices  52.4 us (45%)
  waiting for transfers between devices  46.2 us (39%)
  other arithmetic  7.12 us (6%)
  matrix products  5.14 us (4%)
  local copies, waits for them, and re-layouts  4.41 us (4%)
    ppermute x8, waiting for transfers between devices, from_partner(): return lax.ppermute(block, axis, route)  27.2 us
    ppermute x8, starting transfers between devices, from_partner(): return lax.ppermute(block, axis, route)  23.2 us
    all_to_all x1, starting transfers between devices, per_device(): lax.all_to_all(jnp.swapaxes(merged.astype(jnp.bfloat16), 0, 1), 'grp', sp...  15.2 us
    ppermute x3, starting transfers between devices, shifted(): return lax.ppermute(block, axis, route)  14 us
    all_to_all x1, waiting for transfers between devices, per_device(): lax.all_to_all(jnp.swapaxes(merged.astype(jnp.bfloat16), 0, 1), 'grp', sp...  13.4 us
    ppermute x3, waiting for transfers between devices, shifted(): return lax.ppermute(block, axis, route)  5.62 us
  transfers between devices with their start and end apart: 12, of which 10 were waited for; matrix products, arithmetic and copies ran while one was open for 5% of the time, Pallas kernels for 0%

profile of v12, /device:TPU:6, one launch (start us, length us, event | category | flops | bytes accessed | tf_op | source)
XLA Modules:
  0.0 116.0 jit_solution(11052672918722906002)
XLA Ops:
  0.9 5.1 %collective-permute-start = (bf16[6,3072]{1,0:T(8,128)(2,1)S(1)}, bf16[6,3072]{1,0:T(8,128)(2,1)S(1)}, u32[]{:S(2)}, u32[]{:S(2)}) collective-permute-start(bf16[6,3072]{1,0:T(8,128)(2,1)S(1)} %pad_add_fusion.1), channel_id=1, source_target_pairs={{0,4},{4,0},{1,5},{5,1},{2,6},{6,2},{3,7},{7,3},{8,12},{12,8},{9,1... | collective-permute-start | bytes 110600 | tf_op jit(solution)/shard_map/ppermute | solution.py:19
  6.1 1.2 %dynamic_slice.24 = s32[1]{0:T(128)} dynamic-slice(s32[4]{0:T(128)} %param.17, s32[]{:T(128)S(6)} %select_n.241), dynamic_slice_sizes={1} | dynamic-slice | bytes 12 | tf_op jit(solution)/shard_map/jit(dynamic_index_in_dim)/dynamic_slice | solution.py:136
  11.6 2.6 %collective-permute-start.1 = (bf16[12,3072]{1,0:T(8,128)(2,1)S(1)}, bf16[12,3072]{1,0:T(8,128)(2,1)S(1)}, u32[]{:S(2)}, u32[]{:S(2)}) collective-permute-start(bf16[12,3072]{1,0:T(8,128)(2,1)S(1)} %pad_maximum_fusion.7), channel_id=1, source_target_pairs={{0,2},{2,0},{1,3},{3,1},{4,6},{6,4},{5,7},{7,5},{8,10},{10,8},{9,1... | collective-permute-start | bytes 221192 | tf_op jit(solution)/shard_map/ppermute | solution.py:19
  15.5 2.7 %collective-permute-done.1 = bf16[12,3072]{1,0:T(8,128)(2,1)S(1)} collective-permute-done((bf16[12,3072]{1,0:T(8,128)(2,1)S(1)}, bf16[12,3072]{1,0:T(8,128)(2,1)S(1)}, u32[]{:S(2)}, u32[]{:S(2)}) %collective-permute-start.1) | collective-permute-done | bytes 73760 | tf_op jit(solution)/shard_map/ppermute | solution.py:19
  18.2 1.9 %collective-permute-start.2 = (bf16[24,3072]{1,0:T(8,128)(2,1)S(1)}, bf16[24,3072]{1,0:T(8,128)(2,1)S(1)}, u32[]{:S(2)}, u32[]{:S(2)}) collective-permute-start(bf16[24,3072]{1,0:T(8,128)(2,1)S(1)} %pad_maximum_fusion.4), channel_id=1, source_target_pairs={{0,1},{1,0},{2,3},{3,2},{4,5},{5,4},{6,7},{7,6},{8,9},{9,8},{10,11... | collective-permute-start | bytes 442376 | tf_op jit(solution)/shard_map/ppermute | solution.py:19
  20.2 1.3 %collective-permute-done.2 = bf16[24,3072]{1,0:T(8,128)(2,1)S(1)} collective-permute-done((bf16[24,3072]{1,0:T(8,128)(2,1)S(1)}, bf16[24,3072]{1,0:T(8,128)(2,1)S(1)}, u32[]{:S(2)}, u32[]{:S(2)}) %collective-permute-start.2) | collective-permute-done | bytes 147488 | tf_op jit(solution)/shard_map/ppermute | solution.py:19
  22.9 1.1 fusion
  26.0 2.1 %collective-permute-start.3 = (bf16[408,512]{1,0:T(8,128)(2,1)S(1)}, bf16[408,512]{1,0:T(8,128)(2,1)S(1)}, u32[]{:S(2)}, u32[]{:S(2)}) collective-permute-start(bf16[408,512]{1,0:T(8,128)(2,1)S(1)} %pad_maximum_fusion.2), channel_id=1, source_target_pairs={{0,1},{1,0},{2,3},{3,2},{4,5},{5,4},{6,7},{7,6},{8,9},{9,8},{10,11... | collective-permute-start | bytes 1253384 | tf_op jit(solution)/shard_map/ppermute | solution.py:19
  28.1 1.6 %collective-permute-done.3 = bf16[408,512]{1,0:T(8,128)(2,1)S(1)} collective-permute-done((bf16[408,512]{1,0:T(8,128)(2,1)S(1)}, bf16[408,512]{1,0:T(8,128)(2,1)S(1)}, u32[]{:S(2)}, u32[]{:S(2)}) %collective-permute-start.3) | collective-permute-done | bytes 417824 | tf_op jit(solution)/shard_map/ppermute | solution.py:19
  30.2 2.6 %collective-permute-start.4 = (bf16[204,512]{1,0:T(8,128)(2,1)S(1)}, bf16[204,512]{1,0:T(8,128)(2,1)S(1)}, u32[]{:S(2)}, u32[]{:S(2)}) collective-permute-start(bf16[204,512]{1,0:T(8,128)(2,1)S(1)} %pad_maximum_fusion.3), channel_id=1, source_target_pairs={{0,2},{2,0},{1,3},{3,1},{4,6},{6,4},{5,7},{7,5},{8,10},{10,8},{9,1... | collective-permute-start | bytes 626696 | tf_op jit(solution)/shard_map/ppermute | solution.py:19
  32.8 6.6 %collective-permute-done.4 = bf16[204,512]{1,0:T(8,128)(2,1)S(1)} collective-permute-done((bf16[204,512]{1,0:T(8,128)(2,1)S(1)}, bf16[204,512]{1,0:T(8,128)(2,1)S(1)}, u32[]{:S(2)}, u32[]{:S(2)}) %collective-permute-start.4) | collective-permute-done | bytes 208928 | tf_op jit(solution)/shard_map/ppermute | solution.py:19
  39.9 2.8 %collective-permute-start.5 = (bf16[102,512]{1,0:T(8,128)(2,1)S(1)}, bf16[102,512]{1,0:T(8,128)(2,1)S(1)}, u32[]{:S(2)}, u32[]{:S(2)}) collective-permute-start(bf16[102,512]{1,0:T(8,128)(2,1)S(1)} %pad_maximum_fusion.5), channel_id=1, source_target_pairs={{0,4},{4,0},{1,5},{5,1},{2,6},{6,2},{3,7},{7,3},{8,12},{12,8},{9,1... | collective-permute-start | bytes 313352 | tf_op jit(solution)/shard_map/ppermute | solution.py:19
  42.7 5.3 %collective-permute-done.5 = bf16[102,512]{1,0:T(8,128)(2,1)S(1)} collective-permute-done((bf16[102,512]{1,0:T(8,128)(2,1)S(1)}, bf16[102,512]{1,0:T(8,128)(2,1)S(1)}, u32[]{:S(2)}, u32[]{:S(2)}) %collective-permute-start.5) | collective-permute-done | bytes 104480 | tf_op jit(solution)/shard_map/ppermute | solution.py:19
  48.9 15.2 %all-to-all-start = ((bf16[16,6,512]{2,1,0:T(8,128)(2,1)}), bf16[16,6,512]{2,1,0:T(8,128)(2,1)S(1)}, u32[]{:S(2)}, u32[]{:S(2)}) async-start(bf16[16,6,512]{2,1,0:T(8,128)(2,1)} %copy.49), calls=%async_computation | async-start | bytes 262144 | tf_op jit(solution)/shard_map/all_to_all | solution.py:177
  64.1 13.4 %all-to-all-done = bf16[16,6,512]{2,1,0:T(8,128)(2,1)S(1)} async-done(((bf16[16,6,512]{2,1,0:T(8,128)(2,1)}), bf16[16,6,512]{2,1,0:T(8,128)(2,1)S(1)}, u32[]{:S(2)}, u32[]{:S(2)}) %all-to-all-start) | async-done | bytes 98336 | tf_op jit(solution)/shard_map/all_to_all | solution.py:177
  78.2 1.3 %fusion.4 = f32[96,2048]{1,0:T(8,128)S(1)} fusion(bf16[128,2048]{1,0:T(8,128)(2,1)S(1)} %copy-done.1, bf16[96,512]{1,0:T(8,128)(2,1)S(1)} %reshape.87, bf16[1,512,128]{2,1,0:T(8,128)(2,1)} %param.20), kind=kOutput, calls=%fused_computation.15 | convolution fusion | flops 62926848 | bytes 1540096 | tf_op jit(solution)/shard_map/dot_general | solution.py:186
  79.5 2.9 %collective-permute-start.6 = (bf16[48,2048]{1,0:T(8,128)(2,1)S(1)}, bf16[48,2048]{1,0:T(8,128)(2,1)S(1)}, u32[]{:S(2)}, u32[]{:S(2)}) collective-permute-start(bf16[48,2048]{1,0:T(8,128)(2,1)S(1)} %select_convert_fusion.1), channel_id=1, source_target_pairs={{0,32},{32,0},{64,96},{96,64},{128,160},{160,128},{192,224},{224,1... | collective-permute-start | bytes 589832 | tf_op jit(solution)/shard_map/ppermute | solution.py:19
  82.4 4.6 %collective-permute-done.6 = bf16[48,2048]{1,0:T(8,128)(2,1)S(1)} collective-permute-done((bf16[48,2048]{1,0:T(8,128)(2,1)S(1)}, bf16[48,2048]{1,0:T(8,128)(2,1)S(1)}, u32[]{:S(2)}, u32[]{:S(2)}) %collective-permute-start.6) | collective-permute-done | bytes 196640 | tf_op jit(solution)/shard_map/ppermute | solution.py:19
  87.2 3.2 %collective-permute-start.7 = (bf16[24,2048]{1,0:T(8,128)(2,1)S(1)}, bf16[24,2048]{1,0:T(8,128)(2,1)S(1)}, u32[]{:S(2)}, u32[]{:S(2)}) collective-permute-start(bf16[24,2048]{1,0:T(8,128)(2,1)S(1)} %select_convert_fusion.3), channel_id=1, source_target_pairs={{0,64},{64,0},{32,96},{96,32},{128,192},{192,128},{160,224},{224,1... | collective-permute-start | bytes 294920 | tf_op jit(solution)/shard_map/ppermute | solution.py:19
  90.5 5.1 %collective-permute-done.7 = bf16[24,2048]{1,0:T(8,128)(2,1)S(1)} collective-permute-done((bf16[24,2048]{1,0:T(8,128)(2,1)S(1)}, bf16[24,2048]{1,0:T(8,128)(2,1)S(1)}, u32[]{:S(2)}, u32[]{:S(2)}) %collective-permute-start.7) | collective-permute-done | bytes 98336 | tf_op jit(solution)/shard_map/ppermute | solution.py:19
  95.7 4.2 %collective-permute-start.8 = (bf16[6,2048]{1,0:T(8,128)(2,1)S(1)}, bf16[6,2048]{1,0:T(8,128)(2,1)S(1)}, u32[]{:S(2)}, u32[]{:S(2)}) collective-permute-start(bf16[6,2048]{1,0:T(8,128)(2,1)S(1)} %get-tuple-element.24), channel_id=1, source_target_pairs={{0,256},{32,288},{64,320},{96,352},{128,384},{160,416},{192,448},{... | collective-permute-start | bytes 73736 | tf_op jit(solution)/shard_map/ppermute | solution.py:25
  100.0 5.7 %collective-permute-start.10 = (bf16[6,2048]{1,0:T(8,128)(2,1)S(1)}, bf16[6,2048]{1,0:T(8,128)(2,1)S(1)}, u32[]{:S(2)}, u32[]{:S(2)}) collective-permute-start(bf16[6,2048]{1,0:T(8,128)(2,1)S(1)} %get-tuple-element.25), channel_id=1, source_target_pairs={{0,128},{32,160},{64,192},{96,224},{128,256},{160,288},{192,320},{... | collective-permute-start | bytes 73736 | tf_op jit(solution)/shard_map/ppermute | solution.py:25
  105.7 4.1 %collective-permute-start.9 = (bf16[6,2048]{1,0:T(8,128)(2,1)S(1)}, bf16[6,2048]{1,0:T(8,128)(2,1)S(1)}, u32[]{:S(2)}, u32[]{:S(2)}) collective-permute-start(bf16[6,2048]{1,0:T(8,128)(2,1)S(1)} %get-tuple-element.26), channel_id=1, source_target_pairs={{0,384},{32,416},{64,448},{96,480},{128,0},{160,32},{192,64},{224,... | collective-permute-start | bytes 73736 | tf_op jit(solution)/shard_map/ppermute | solution.py:25
  110.7 4.7 %collective-permute-done.9 = bf16[6,2048]{1,0:T(8,128)(2,1)S(1)} collective-permute-done((bf16[6,2048]{1,0:T(8,128)(2,1)S(1)}, bf16[6,2048]{1,0:T(8,128)(2,1)S(1)}, u32[]{:S(2)}, u32[]{:S(2)}) %collective-permute-start.9) | collective-permute-done | bytes 24608 | tf_op jit(solution)/shard_map/ppermute | solution.py:25
  (83 shorter events, 13.9 us)
Async XLA Ops:
  0.0 21.8 %copy-start = (bf16[16,512,128]{2,1,0:T(8,128)(2,1)S(1)}, bf16[16,512,128]{2,1,0:T(8,128)(2,1)}, u32[]{:S(2)}) copy-start(bf16[16,512,128]{2,1,0:T(8,128)(2,1)} %param.19) | copy-start | bytes 6291460
  0.9 9.8 %collective-permute-start = (bf16[6,3072]{1,0:T(8,128)(2,1)S(1)}, bf16[6,3072]{1,0:T(8,128)(2,1)S(1)}, u32[]{:S(2)}, u32[]{:S(2)}) collective-permute-start(bf16[6,3072]{1,0:T(8,128)(2,1)S(1)} %pad_add_fusion.1), channel_id=1, source_target_pairs={{0,4},{4,0},{1,5},{5,1},{2,6},{6,2},{3,7},{7,3},{8,12},{12,8},{9,1... | collective-permute-start | bytes 110600 | tf_op jit(solution)/shard_map/ppermute | solution.py:19
  11.6 6.5 %collective-permute-start.1 = (bf16[12,3072]{1,0:T(8,128)(2,1)S(1)}, bf16[12,3072]{1,0:T(8,128)(2,1)S(1)}, u32[]{:S(2)}, u32[]{:S(2)}) collective-permute-start(bf16[12,3072]{1,0:T(8,128)(2,1)S(1)} %pad_maximum_fusion.7), channel_id=1, source_target_pairs={{0,2},{2,0},{1,3},{3,1},{4,6},{6,4},{5,7},{7,5},{8,10},{10,8},{9,1... | collective-permute-start | bytes 221192 | tf_op jit(solution)/shard_map/ppermute | solution.py:19
  18.2 3.3 %collective-permute-start.2 = (bf16[24,3072]{1,0:T(8,128)(2,1)S(1)}, bf16[24,3072]{1,0:T(8,128)(2,1)S(1)}, u32[]{:S(2)}, u32[]{:S(2)}) collective-permute-start(bf16[24,3072]{1,0:T(8,128)(2,1)S(1)} %pad_maximum_fusion.4), channel_id=1, source_target_pairs={{0,1},{1,0},{2,3},{3,2},{4,5},{5,4},{6,7},{7,6},{8,9},{9,8},{10,11... | collective-permute-start | bytes 442376 | tf_op jit(solution)/shard_map/ppermute | solution.py:19
  21.8 1.1 copy-start.3
  21.9 1.1 copy-start.4
  26.0 3.7 %collective-permute-start.3 = (bf16[408,512]{1,0:T(8,128)(2,1)S(1)}, bf16[408,512]{1,0:T(8,128)(2,1)S(1)}, u32[]{:S(2)}, u32[]{:S(2)}) collective-permute-start(bf16[408,512]{1,0:T(8,128)(2,1)S(1)} %pad_maximum_fusion.2), channel_id=1, source_target_pairs={{0,1},{1,0},{2,3},{3,2},{4,5},{5,4},{6,7},{7,6},{8,9},{9,8},{10,11... | collective-permute-start | bytes 1253384 | tf_op jit(solution)/shard_map/ppermute | solution.py:19
  30.2 33.9 %copy-start.2 = (s32[16]{0:T(128)S(1)}, s32[16]{0:T(128)}, u32[]{:S(2)}) copy-start(s32[16]{0:T(128)} %constant.173) | copy-start | bytes 196
  30.2 9.2 %collective-permute-start.4 = (bf16[204,512]{1,0:T(8,128)(2,1)S(1)}, bf16[204,512]{1,0:T(8,128)(2,1)S(1)}, u32[]{:S(2)}, u32[]{:S(2)}) collective-permute-start(bf16[204,512]{1,0:T(8,128)(2,1)S(1)} %pad_maximum_fusion.3), channel_id=1, source_target_pairs={{0,2},{2,0},{1,3},{3,1},{4,6},{6,4},{5,7},{7,5},{8,10},{10,8},{9,1... | collective-permute-start | bytes 626696 | tf_op jit(solution)/shard_map/ppermute | solution.py:19
  39.6 38.6 %copy-start.1 = (bf16[128,2048]{1,0:T(8,128)(2,1)S(1)}, bf16[128,2048]{1,0:T(8,128)(2,1)}, u32[]{:S(2)}) copy-start(bf16[128,2048]{1,0:T(8,128)(2,1)} %param.21) | copy-start | bytes 1572868
  39.9 8.1 %collective-permute-start.5 = (bf16[102,512]{1,0:T(8,128)(2,1)S(1)}, bf16[102,512]{1,0:T(8,128)(2,1)S(1)}, u32[]{:S(2)}, u32[]{:S(2)}) collective-permute-start(bf16[102,512]{1,0:T(8,128)(2,1)S(1)} %pad_maximum_fusion.5), channel_id=1, source_target_pairs={{0,4},{4,0},{1,5},{5,1},{2,6},{6,2},{3,7},{7,3},{8,12},{12,8},{9,1... | collective-permute-start | bytes 313352 | tf_op jit(solution)/shard_map/ppermute | solution.py:19
  48.9 28.6 %all-to-all-start = ((bf16[16,6,512]{2,1,0:T(8,128)(2,1)}), bf16[16,6,512]{2,1,0:T(8,128)(2,1)S(1)}, u32[]{:S(2)}, u32[]{:S(2)}) async-start(bf16[16,6,512]{2,1,0:T(8,128)(2,1)} %copy.49), calls=%async_computation | async-start | bytes 262144 | tf_op jit(solution)/shard_map/all_to_all | solution.py:177
  79.5 7.6 %collective-permute-start.6 = (bf16[48,2048]{1,0:T(8,128)(2,1)S(1)}, bf16[48,2048]{1,0:T(8,128)(2,1)S(1)}, u32[]{:S(2)}, u32[]{:S(2)}) collective-permute-start(bf16[48,2048]{1,0:T(8,128)(2,1)S(1)} %select_convert_fusion.1), channel_id=1, source_target_pairs={{0,32},{32,0},{64,96},{96,64},{128,160},{160,128},{192,224},{224,1... | collective-permute-start | bytes 589832 | tf_op jit(solution)/shard_map/ppermute | solution.py:19
  87.2 8.5 %collective-permute-start.7 = (bf16[24,2048]{1,0:T(8,128)(2,1)S(1)}, bf16[24,2048]{1,0:T(8,128)(2,1)S(1)}, u32[]{:S(2)}, u32[]{:S(2)}) collective-permute-start(bf16[24,2048]{1,0:T(8,128)(2,1)S(1)} %select_convert_fusion.3), channel_id=1, source_target_pairs={{0,64},{64,0},{32,96},{96,32},{128,192},{192,128},{160,224},{224,1... | collective-permute-start | bytes 294920 | tf_op jit(solution)/shard_map/ppermute | solution.py:19
  95.7 14.9 %collective-permute-start.8 = (bf16[6,2048]{1,0:T(8,128)(2,1)S(1)}, bf16[6,2048]{1,0:T(8,128)(2,1)S(1)}, u32[]{:S(2)}, u32[]{:S(2)}) collective-permute-start(bf16[6,2048]{1,0:T(8,128)(2,1)S(1)} %get-tuple-element.24), channel_id=1, source_target_pairs={{0,256},{32,288},{64,320},{96,352},{128,384},{160,416},{192,448},{... | collective-permute-start | bytes 73736 | tf_op jit(solution)/shard_map/ppermute | solution.py:25
  100.0 10.7 %collective-permute-start.10 = (bf16[6,2048]{1,0:T(8,128)(2,1)S(1)}, bf16[6,2048]{1,0:T(8,128)(2,1)S(1)}, u32[]{:S(2)}, u32[]{:S(2)}) collective-permute-start(bf16[6,2048]{1,0:T(8,128)(2,1)S(1)} %get-tuple-element.25), channel_id=1, source_target_pairs={{0,128},{32,160},{64,192},{96,224},{128,256},{160,288},{192,320},{... | collective-permute-start | bytes 73736 | tf_op jit(solution)/shard_map/ppermute | solution.py:25
  105.7 9.7 %collective-permute-start.9 = (bf16[6,2048]{1,0:T(8,128)(2,1)S(1)}, bf16[6,2048]{1,0:T(8,128)(2,1)S(1)}, u32[]{:S(2)}, u32[]{:S(2)}) collective-permute-start(bf16[6,2048]{1,0:T(8,128)(2,1)S(1)} %get-tuple-element.26), channel_id=1, source_target_pairs={{0,384},{32,416},{64,448},{96,480},{128,0},{160,32},{192,64},{224,... | collective-permute-start | bytes 73736 | tf_op jit(solution)/shard_map/ppermute | solution.py:25
